TPU v7x, 32 devices: a whole 2x2x4 slice. The times are simulated.
32 devices in a mesh: row: 8 (over y, x, core), col: 4 (over z).
Axes of the slice: x: 2, y: 2, z: 4, core: 2. Of those that a mesh axis runs over, the one named last changes fastest.
Arguments:
- pair: bfloat16 [256, 256, 128], P('row', 'col'), may hold values from -6 to 6
- mask: int32 [256], replicated, may hold values 0 or 1
- w_agate: bfloat16 [128, 128], replicated, may hold values from -0.5 to 0.5
- w_aproj: bfloat16 [128, 128], replicated, may hold values from -0.5 to 0.5
- w_bgate: bfloat16 [128, 128], replicated, may hold values from -0.5 to 0.5
- w_bproj: bfloat16 [128, 128], replicated, may hold values from -0.5 to 0.5
- w_gate: bfloat16 [128, 128], replicated, may hold values from -0.5 to 0.5
- w_out: bfloat16 [128, 128], replicated, may hold values from -0.5 to 0.5
- w_up: bfloat16 [128, 512], replicated, may hold values from -0.5 to 0.5
- w_down: bfloat16 [512, 128], replicated, may hold values from -0.25 to 0.25
Outputs:
- updated: bfloat16 [256, 256, 128], P('row', 'col')
All inputs are finite; a program needn't handle non-finite values.
Results may differ from a plain program's by a relative error of at most 0.0059.
Values may be sent and summed in bfloat16 or wider, within the bound.
No kernel may reach another device: no remote copies, remote signals or barrier semaphores. Data moves between devices by JAX's collectives and lax.ppermute only.
A program may use at most 64 MiB of HBM per device.

v0:
```python
import jax
import jax.numpy as jnp
from jax import lax
from jax.sharding import PartitionSpec as P


def layer_norm(values):
    center = values - jnp.mean(values, axis=-1, keepdims=True)
    spread = jnp.mean(center * center, axis=-1, keepdims=True)
    return center * lax.rsqrt(spread + 1e-05)


def body(pair, mask, w_agate, w_aproj, w_bgate, w_bproj, w_gate, w_out, w_up, w_down):
    rows, cols, width = pair.shape
    present = mask.astype(jnp.float32)
    row_start = lax.axis_index("row") * rows
    col_start = lax.axis_index("col") * cols
    row_mask = lax.dynamic_slice_in_dim(present, row_start, rows, 0)
    col_mask = lax.dynamic_slice_in_dim(present, col_start, cols, 0)
    pair_mask = (row_mask[:, None] * col_mask[None, :]).reshape(rows * cols, 1)
    pair_flat = pair.astype(jnp.float32).reshape(rows * cols, width)
    normed = layer_norm(pair_flat).astype(jnp.bfloat16)
    gate = jax.nn.sigmoid(jnp.dot(normed, w_gate, preferred_element_type=jnp.float32))
    left = (
        jax.nn.sigmoid(jnp.dot(normed, w_agate, preferred_element_type=jnp.float32))
        * jnp.dot(normed, w_aproj, preferred_element_type=jnp.float32)
        * pair_mask
    )
    right = (
        jax.nn.sigmoid(jnp.dot(normed, w_bgate, preferred_element_type=jnp.float32))
        * jnp.dot(normed, w_bproj, preferred_element_type=jnp.float32)
        * pair_mask
    )
    left_major = jnp.transpose(left.astype(jnp.bfloat16).reshape(rows, cols, -1), (2, 0, 1))
    right_major = jnp.transpose(right.astype(jnp.bfloat16).reshape(rows, cols, -1), (2, 0, 1))
    left_spread, right_spread = (
        lax.all_to_all(
            lax.all_to_all(left_major, "row", split_axis=0, concat_axis=1, tiled=True),
            "col",
            split_axis=1,
            concat_axis=2,
            tiled=True,
        ),
        lax.all_to_all(
            lax.all_to_all(right_major, "row", split_axis=0, concat_axis=1, tiled=True),
            "col",
            split_axis=1,
            concat_axis=2,
            tiled=True,
        ),
    )
    mixed = jnp.einsum(
        "cik,cjk->cij",
        lax.all_gather(left_spread, "col", axis=1, tiled=True),
        right_spread,
        preferred_element_type=jnp.float32,
    ).astype(jnp.bfloat16)
    mixed = lax.all_to_all(mixed, "row", split_axis=1, concat_axis=0, tiled=True)
    mixed_rows = jnp.transpose(mixed, (1, 2, 0)).astype(jnp.float32).reshape(rows * cols, -1)
    mixed_normed = layer_norm(mixed_rows).astype(jnp.bfloat16)
    middle = pair_flat + gate * jnp.dot(mixed_normed, w_out, preferred_element_type=jnp.float32)
    trans_in = layer_norm(middle).astype(jnp.bfloat16)
    trans_hidden = jax.nn.relu(jnp.dot(trans_in, w_up, preferred_element_type=jnp.float32)).astype(
        jnp.bfloat16
    )
    result = middle + jnp.dot(trans_hidden, w_down, preferred_element_type=jnp.float32)
    return result.astype(jnp.bfloat16).reshape(rows, cols, width)


def solution(mesh):
    placed = (P("row", "col", None), P(), P(), P(), P(), P(), P(), P(), P(), P())
    return jax.shard_map(
        body, mesh=mesh, in_specs=placed, out_specs=P("row", "col", None), check_vma=False
    )
```

profile of v0, /device:TPU:0, one launch (start us, length us, event | category | flops | bytes accessed | tf_op | source)
XLA Modules:
  0.0 144.5 jit_solution(13755586689063979857)
XLA Ops:
  6.5 1.4 convert_reduce_fusion
  8.0 1.7 %multiply_reduce_fusion.2 = f32[32,64]{1,0:T(8,128)S(1)} fusion(bf16[32,64,128]{2,1,0:T(8,128)(2,1)} %param.10, f32[32,64]{1,0:T(8,128)S(1)} %broadcast_multiply_fusion.2), kind=kLoop, calls=%fused_computation.36 | loop fusion | flops 1046528 | bytes 540672 | tf_op jit(solution)/shard_map/reduce_sum | solution.py:9
  9.7 0.7 convert_element_type.47
  10.8 1.6 %fusion.18 = bf16[2048,128]{1,0:T(8,128)(2,1)S(1)} fusion(bf16[32,64,128]{2,1,0:T(8,128)(2,1)} %param.10, f32[2048]{0:T(1024)S(1)} %rsqrt.31, f32[2048]{0:T(1024)S(1)} %div.32), kind=kLoop, calls=%fused_computation.33 | loop fusion | flops 1048576 | bytes 1064960 | tf_op jit(solution)/shard_map/convert_element_type | solution.py:22
  12.5 0.4 fusion.8
  12.9 0.3 copy-done.3
  13.2 0.4 fusion.12
  13.6 1.6 %copy.22 = bf16[32,64,128]{1,0,2:T(8,128)(2,1)S(1)} copy(bf16[32,64,128]{2,1,0:T(8,128)(2,1)S(1)} %bitcast.89) | data formatting | bytes 1048576 | tf_op jit(solution)/shard_map/reshape | solution.py:34
  15.2 0.7 reshape.119
  15.9 14.7 %all_to_all.81 = bf16[8,2,16384]{2,1,0:T(2,128)(2,1)S(1)} all-to-all(bf16[8,2,16384]{2,1,0:T(2,128)(2,1)S(1)} %reshape.119), channel_id=1, replica_groups=mesh['row'=8,'col'=4] {'row'}, dimensions={0} | all-to-all | bytes 1048576 | tf_op jit(solution)/shard_map/all_to_all | solution.py:38
  30.7 0.7 reshape.120
  31.4 0.7 copy.47
  32.1 0.9 reshape.121
  33.0 18.5 %all_to_all.82 = bf16[4,2,32768]{2,1,0:T(2,128)(2,1)S(1)} all-to-all(bf16[4,2,32768]{2,1,0:T(2,128)(2,1)S(1)} %reshape.121), channel_id=1, replica_groups=mesh['row'=8,'col'=4] {'col'}, dimensions={0} | all-to-all | bytes 1048576 | tf_op jit(solution)/shard_map/all_to_all | solution.py:37
  51.5 0.7 reshape.122
  52.2 0.8 copy.45
  53.0 1.5 %all_to_all.66 = bf16[16,64,256]{2,1,0:T(8,128)(2,1)} reshape(bf16[16,64,4,64]{3,2,1,0:T(4,128)(2,1)S(1)} %bitcast.81) | data formatting | bytes 1048576 | tf_op jit(solution)/shard_map/all_to_all | solution.py:37
  54.6 0.4 fusion.4
  55.0 0.3 copy-done.4
  55.3 0.4 fusion.13
  55.7 1.6 %copy.27 = bf16[32,64,128]{1,0,2:T(8,128)(2,1)S(1)} copy(bf16[32,64,128]{2,1,0:T(8,128)(2,1)S(1)} %bitcast.88) | data formatting | bytes 1048576 | tf_op jit(solution)/shard_map/reshape | solution.py:35
  57.3 0.7 reshape.123
  58.0 12.2 %all_to_all.83 = bf16[8,2,16384]{2,1,0:T(2,128)(2,1)S(1)} all-to-all(bf16[8,2,16384]{2,1,0:T(2,128)(2,1)S(1)} %reshape.123), channel_id=1, replica_groups=mesh['row'=8,'col'=4] {'row'}, dimensions={0} | all-to-all | bytes 1048576 | tf_op jit(solution)/shard_map/all_to_all | solution.py:45
  70.2 0.7 reshape.124
  70.9 0.7 copy.46
  71.6 0.9 reshape.125
  72.5 31.4 %all_to_all.84 = bf16[4,2,32768]{2,1,0:T(2,128)(2,1)S(1)} all-to-all(bf16[4,2,32768]{2,1,0:T(2,128)(2,1)S(1)} %reshape.125), channel_id=1, replica_groups=mesh['row'=8,'col'=4] {'col'}, dimensions={0} | all-to-all | bytes 1048576 | tf_op jit(solution)/shard_map/all_to_all | solution.py:44
  103.9 0.7 reshape.126
  104.6 0.8 copy.44
  105.4 0.7 all_to_all.74
  106.1 3.6 %all-gather.2.cloned.1.call-done = bf16[16,256,256]{2,1,0:T(8,128)(2,1)} async-done(((bf16[16,64,256]{2,1,0:T(8,128)(2,1)}), bf16[16,256,256]{2,1,0:T(8,128)(2,1)}) %all-gather.2.cloned.1.call-update) | async-done | bytes 2097168 | tf_op jit(solution)/shard_map/all_gather | solution.py:54
  109.7 2.3 %convolution_convert_fusion = bf16[16,256,64]{1,2,0:T(8,128)(2,1)S(1)} fusion(bf16[16,256,256]{2,1,0:T(8,128)(2,1)} %all-gather.2.cloned.1.call-done, bf16[16,64,256]{2,1,0:T(8,128)(2,1)S(1)} %all_to_all.74), kind=kOutput, calls=%fused_computation.25 | convolution fusion | flops 134479872 | bytes 3145728 | tf_op jit(solution)/shard_map/cik,cjk->cij/dot_general | solution.py:52
  112.0 1.0 copy.32
  113.0 1.5 %reshape.127 = bf16[8,2,16384]{2,1,0:T(2,128)(2,1)} reshape(bf16[256,16,64]{2,1,0:T(8,128)(2,1)S(1)} %bitcast.76) | data formatting | bytes 1048576
  114.5 3.7 %all-to-all-start.4 = ((bf16[8,2,16384]{2,1,0:T(2,128)(2,1)}), bf16[8,2,16384]{2,1,0:T(2,128)(2,1)S(1)}, u32[]{:S(2)}, u32[]{:S(2)}) async-start(bf16[8,2,16384]{2,1,0:T(2,128)(2,1)} %reshape.127), calls=%async_computation.4 | async-start | bytes 1048576 | tf_op jit(solution)/shard_map/all_to_all | solution.py:58
  118.2 1.4 fusion.11
  119.6 8.3 %all-to-all-done.4 = bf16[8,2,16384]{2,1,0:T(2,128)(2,1)S(1)} async-done(((bf16[8,2,16384]{2,1,0:T(2,128)(2,1)}), bf16[8,2,16384]{2,1,0:T(2,128)(2,1)S(1)}, u32[]{:S(2)}, u32[]{:S(2)}) %all-to-all-start.4) | async-done | bytes 524320 | tf_op jit(solution)/shard_map/all_to_all | solution.py:58
  127.9 0.7 reshape.128
  128.6 0.3 copy.33
  128.8 0.3 convert_bitcast_fusion
  129.1 0.2 copy.34
  129.4 0.2 bitcast_reduce_fusion
  129.6 0.3 multiply_reduce_fusion
  130.1 2.3 %copy.35 = f32[32,64,128]{2,1,0:T(8,128)} copy(f32[32,64,128]{1,0,2:T(8,128)S(1)} %bitcast.71) | data formatting | bytes 2097152 | tf_op jit(solution)/shard_map/convert_element_type | solution.py:59
  132.4 1.9 %fusion.16 = bf16[2048,128]{1,0:T(8,128)(2,1)S(1)} fusion(f32[32,64,128]{2,1,0:T(8,128)} %copy.35, f32[2048]{0:T(1024)S(1)} %rsqrt.33, f32[2048]{0:T(1024)S(1)} %div.38), kind=kLoop, calls=%fused_computation.28 | loop fusion | flops 786432 | bytes 1589248 | tf_op jit(solution)/shard_map/convert_element_type | solution.py:60
  134.4 0.5 fusion.24
  134.9 0.6 multiply_reduce_fusion.1
  135.5 2.1 %fusion.14 = bf16[2048,128]{1,0:T(8,128)(2,1)} fusion(f32[2048,128]{1,0:T(8,128)S(1)} %get-tuple-element.6, bf16[512,128]{1,0:T(8,128)(2,1)S(1)} %copy-done, bf16[128,512]{1,0:T(8,128)(2,1)S(1)} %copy-done.6, f32[2048]{0:T(1024)S(1)} %add_rsqrt_fusion.2, f32[2048]{0:T(1024)S(1)} %broadcast_multiply_fusion.3), kind=kOutput, calls=%fused_computation.22 | convolution fusion | flops 540278784 | bytes 1851392 | tf_op jit(solution)/shard_map/dot_general | solution.py:66
  (36 shorter events, 0.9 us)
Async XLA Ops:
  6.5 129.0 %copy-start = (bf16[512,128]{1,0:T(8,128)(2,1)S(1)}, bf16[512,128]{1,0:T(8,128)(2,1)}, u32[]{:S(2)}) copy-start(bf16[512,128]{1,0:T(8,128)(2,1)} %param.19) | copy-start | bytes 393220
  6.5 5.9 %copy-start.7 = (bf16[128,128]{1,0:T(8,128)(2,1)S(1)}, bf16[128,128]{1,0:T(8,128)(2,1)}, u32[]{:S(2)}) copy-start(bf16[128,128]{1,0:T(8,128)(2,1)} %param.12) | copy-start | bytes 98308
  6.5 103.1 %all-gather.2.cloned.1.call-start = ((), (), s32[]{:S(2)}) async-start(), calls=%async_computation.5 | async-start | bytes 2621440 | tf_op jit(solution)/shard_map/all_gather | solution.py:54
  12.5 0.8 copy-start.3
  52.2 2.3 %copy-start.8 = (bf16[128,128]{1,0:T(8,128)(2,1)S(1)}, bf16[128,128]{1,0:T(8,128)(2,1)}, u32[]{:S(2)}) copy-start(bf16[128,128]{1,0:T(8,128)(2,1)} %param.14) | copy-start | bytes 98308
  54.5 0.8 copy-start.4
  112.0 6.2 %copy-start.9 = (bf16[128,128]{1,0:T(8,128)(2,1)S(1)}, bf16[128,128]{1,0:T(8,128)(2,1)}, u32[]{:S(2)}) copy-start(bf16[128,128]{1,0:T(8,128)(2,1)} %param.16) | copy-start | bytes 98308
  114.5 13.4 %all-to-all-start.4 = ((bf16[8,2,16384]{2,1,0:T(2,128)(2,1)}), bf16[8,2,16384]{2,1,0:T(2,128)(2,1)S(1)}, u32[]{:S(2)}, u32[]{:S(2)}) async-start(bf16[8,2,16384]{2,1,0:T(2,128)(2,1)} %reshape.127), calls=%async_computation.4 | async-start | bytes 1048576 | tf_op jit(solution)/shard_map/all_to_all | solution.py:58
  130.0 4.3 %copy-start.1 = (bf16[32,64,128]{2,1,0:T(8,128)(2,1)S(1)}, bf16[32,64,128]{2,1,0:T(8,128)(2,1)}, u32[]{:S(2)}) copy-start(bf16[32,64,128]{2,1,0:T(8,128)(2,1)} %param.10) | copy-start | bytes 1572868
  130.1 4.3 %copy-start.5 = (bf16[128,128]{1,0:T(8,128)(2,1)S(1)}, bf16[128,128]{1,0:T(8,128)(2,1)}, u32[]{:S(2)}) copy-start(bf16[128,128]{1,0:T(8,128)(2,1)} %param.17) | copy-start | bytes 98308
  132.4 1.9 %copy-start.2 = (f32[2048,128]{1,0:T(8,128)S(1)}, f32[2048,128]{1,0:T(8,128)}, u32[]{:S(2)}) copy-start(f32[2048,128]{1,0:T(8,128)} %fusion.11) | copy-start | bytes 3145732
  134.3 1.2 copy-start.6
Sparse Core Ops, SparseCore 0:
  54.6 54.9 all-gather.1
where the time goes:
time: 145 us
  blocking collectives  76.8 us (53%)
  local copies, waits for them, and re-layouts  21.5 us (15%)
  between operations  13.7 us (9%)
  waiting for transfers between devices  11.9 us (8%)
  other arithmetic  8.91 us (6%)
  matrix products  7.95 us (5%)
  starting transfers between devices  3.69 us (3%)
    all_to_all x1, blocking collectives, body(): lax.all_to_all(lax.all_to_all(right_major, 'row', split_axis=0, concat_ax...  31.4 us
    all_to_all x1, blocking collectives, body(): lax.all_to_all(lax.all_to_all(left_major, 'row', split_axis=0, concat_axi...  18.5 us
    all_to_all x1, blocking collectives, body(): lax.all_to_all(left_major, 'row', split_axis=0, concat_axis=1, tiled=True)  14.7 us
    all_to_all x1, blocking collectives, body(): lax.all_to_all(right_major, 'row', split_axis=0, concat_axis=1, tiled=True)  12.2 us
    unnamed x30, local copies, waits for them, and re-layouts  8.68 us
    all_to_all x1, waiting for transfers between devices, body(): lax.all_to_all(mixed, 'row', split_axis=1, concat_axis=0, tiled=True)  8.32 us
    all_to_all x1, starting transfers between devices, body(): lax.all_to_all(mixed, 'row', split_axis=1, concat_axis=0, tiled=True)  3.69 us
    all_gather x1, waiting for transfers between devices, body(): lax.all_gather(left_spread, 'col', axis=1, tiled=True)  3.59 us
  transfers between devices with their start and end apart: 2, of which 2 were waited for; matrix products, arithmetic and copies ran while one was open for 6% of the time, Pallas kernels for 0%

commit v1 on v0

--- a/solution.py
+++ b/solution.py
@@ -1,3 +1,5 @@
+import functools
+
 import jax
 import jax.numpy as jnp
 from jax import lax
@@ -10,7 +12,7 @@
     return center * lax.rsqrt(spread + 1e-05)
 
 
-def body(pair, mask, w_agate, w_aproj, w_bgate, w_bproj, w_gate, w_out, w_up, w_down):
+def project(pair, mask, w_agate, w_aproj, w_bgate, w_bproj, w_gate):
     rows, cols, width = pair.shape
     present = mask.astype(jnp.float32)
     row_start = lax.axis_index("row") * rows
@@ -31,8 +33,47 @@
         * jnp.dot(normed, w_bproj, preferred_element_type=jnp.float32)
         * pair_mask
     )
-    left_major = jnp.transpose(left.astype(jnp.bfloat16).reshape(rows, cols, -1), (2, 0, 1))
-    right_major = jnp.transpose(right.astype(jnp.bfloat16).reshape(rows, cols, -1), (2, 0, 1))
+    return pair_flat, gate, left.astype(jnp.bfloat16), right.astype(jnp.bfloat16)
+
+
+def transition(pair_flat, gate, mixed_rows, w_out, w_up, w_down):
+    mixed_normed = layer_norm(mixed_rows).astype(jnp.bfloat16)
+    middle = pair_flat + gate * jnp.dot(mixed_normed, w_out, preferred_element_type=jnp.float32)
+    trans_in = layer_norm(middle).astype(jnp.bfloat16)
+    trans_hidden = jax.nn.relu(jnp.dot(trans_in, w_up, preferred_element_type=jnp.float32)).astype(
+        jnp.bfloat16
+    )
+    return middle + jnp.dot(trans_hidden, w_down, preferred_element_type=jnp.float32)
+
+
+def body_split(pair, mask, w_agate, w_aproj, w_bgate, w_bproj, w_gate, w_out, w_up, w_down, *, n_row, n_col):
+    rows, cols, width = pair.shape
+    n_dev = n_row * n_col
+    pair_flat, gate, left, right = project(pair, mask, w_agate, w_aproj, w_bgate, w_bproj, w_gate)
+    hid = left.shape[-1]
+    group = hid // n_dev
+    edges = jnp.stack([left, right], axis=0).reshape(2, rows, cols, n_dev, group)
+    edges = jnp.transpose(edges, (3, 0, 4, 1, 2))
+    edges = lax.all_to_all(edges, ("row", "col"), split_axis=0, concat_axis=0, tiled=True)
+    edges = edges.reshape(n_row, n_col, 2, group, rows, cols)
+    edges = jnp.transpose(edges, (2, 3, 0, 4, 1, 5)).reshape(2, group, n_row * rows, n_col * cols)
+    mixed = jnp.einsum(
+        "cik,cjk->cij", edges[0], edges[1], preferred_element_type=jnp.float32
+    ).astype(jnp.bfloat16)
+    mixed = mixed.reshape(group, n_row, rows, n_col, cols)
+    mixed = jnp.transpose(mixed, (1, 3, 0, 2, 4)).reshape(n_dev, group, rows, cols)
+    mixed = lax.all_to_all(mixed, ("row", "col"), split_axis=0, concat_axis=0, tiled=True)
+    mixed_rows = jnp.transpose(mixed.reshape(hid, rows, cols), (1, 2, 0))
+    mixed_rows = mixed_rows.astype(jnp.float32).reshape(rows * cols, hid)
+    result = transition(pair_flat, gate, mixed_rows, w_out, w_up, w_down)
+    return result.astype(jnp.bfloat16).reshape(rows, cols, width)
+
+
+def body_rows(pair, mask, w_agate, w_aproj, w_bgate, w_bproj, w_gate, w_out, w_up, w_down):
+    rows, cols, width = pair.shape
+    pair_flat, gate, left, right = project(pair, mask, w_agate, w_aproj, w_bgate, w_bproj, w_gate)
+    left_major = jnp.transpose(left.reshape(rows, cols, -1), (2, 0, 1))
+    right_major = jnp.transpose(right.reshape(rows, cols, -1), (2, 0, 1))
     left_spread, right_spread = (
         lax.all_to_all(
             lax.all_to_all(left_major, "row", split_axis=0, concat_axis=1, tiled=True),
@@ -57,18 +98,23 @@
     ).astype(jnp.bfloat16)
     mixed = lax.all_to_all(mixed, "row", split_axis=1, concat_axis=0, tiled=True)
     mixed_rows = jnp.transpose(mixed, (1, 2, 0)).astype(jnp.float32).reshape(rows * cols, -1)
-    mixed_normed = layer_norm(mixed_rows).astype(jnp.bfloat16)
-    middle = pair_flat + gate * jnp.dot(mixed_normed, w_out, preferred_element_type=jnp.float32)
-    trans_in = layer_norm(middle).astype(jnp.bfloat16)
-    trans_hidden = jax.nn.relu(jnp.dot(trans_in, w_up, preferred_element_type=jnp.float32)).astype(
-        jnp.bfloat16
-    )
-    result = middle + jnp.dot(trans_hidden, w_down, preferred_element_type=jnp.float32)
+    result = transition(pair_flat, gate, mixed_rows, w_out, w_up, w_down)
     return result.astype(jnp.bfloat16).reshape(rows, cols, width)
 
 
 def solution(mesh):
     placed = (P("row", "col", None), P(), P(), P(), P(), P(), P(), P(), P(), P())
-    return jax.shard_map(
-        body, mesh=mesh, in_specs=placed, out_specs=P("row", "col", None), check_vma=False
-    )
+    n_row, n_col = mesh.shape["row"], mesh.shape["col"]
+
+    def run(pair, mask, w_agate, *weights):
+        hid = w_agate.shape[1]
+        if hid % (n_row * n_col) == 0:
+            body = functools.partial(body_split, n_row=n_row, n_col=n_col)
+        else:
+            body = body_rows
+        mapped = jax.shard_map(
+            body, mesh=mesh, in_specs=placed, out_specs=P("row", "col", None), check_vma=False
+        )
+        return mapped(pair, mask, w_agate, *weights)
+
+    return run

time: 145 us -> 86 us (0.59)
  blocking collectives: 76.8 us -> 32.5 us
  between operations: 13.7 us -> 0.34 us
  matrix products: 7.95 us -> 5.92 us
  local copies, waits for them, and re-layouts: 21.5 us -> 20 us
    all_to_all x4 -> x1, blocking collectives: 76.8 us -> 32.5 us  [body_split(): lax.all_to_all(edges, ('row', 'col'), split_axis=0, concat_axis=0, tiled=...]
    all_to_all x9 -> x0, local copies, waits for them, and re-layouts: 5.6 us -> none  [the longest x2 2.28 us: body(): lax.all_to_all(lax.all_to_all(left_major, 'row', split_axis=0, concat_axi...]
    all_to_all x1, waiting for transfers between devices: 8.32 us -> 12.7 us  [body_split(): lax.all_to_all(mixed, ('row', 'col'), split_axis=0, concat_axis=0, tiled=...]
    all_gather x1 -> x0, waiting for transfers between devices: 3.59 us -> none  [body(): lax.all_gather(left_spread, 'col', axis=1, tiled=True)]
    another operation x0 -> x2, local copies, waits for them, and re-layouts: none -> 2.15 us  [body_split(): jnp.stack([left, right], axis=0).reshape(2, rows, cols, n_dev, group)]
    dot_general x8, matrix products: 7.95 us -> 5.92 us  [the longest x1 2.1 us: transition(): jnp.dot(trans_hidden, w_down, preferred_element_type=jnp.float32)]
    convert_element_type x3, local copies, waits for them, and re-layouts: 3.5 us -> 1.72 us  [the longest x1 1.29 us: body_split(): mixed_rows = mixed_rows.astype(jnp.float32).reshape(rows * cols, hid)]
    slice x0 -> x1, local copies, waits for them, and re-layouts: none -> 1.55 us  [body_split(): edges[1]]
  transfers between devices with their start and end apart: 2 -> 1, of which waited for: 2 -> 1; matrix products, arithmetic and copies ran while one was open for 6% -> 2% of each run, Pallas kernels for 0% -> 0%
where the time goes in v1:
time: 86 us; the launch traced here: 84.7 us
  blocking collectives  32.5 us (38%)
  local copies, waits for them, and re-layouts  20 us (23%)
  waiting for transfers between devices  12.7 us (15%)
  other arithmetic  8.6 us (10%)
  matrix products  5.92 us (7%)
  starting transfers between devices  4.67 us (5%)
    all_to_all x1, blocking collectives, body_split(): lax.all_to_all(edges, ('row', 'col'), split_axis=0, concat_axis=0, tiled=...  32.5 us
    all_to_all x1, waiting for transfers between devices, body_split(): lax.all_to_all(mixed, ('row', 'col'), split_axis=0, concat_axis=0, tiled=...  12.7 us
    unnamed x24, local copies, waits for them, and re-layouts  8.91 us
    all_to_all x1, starting transfers between devices, body_split(): lax.all_to_all(mixed, ('row', 'col'), split_axis=0, concat_axis=0, tiled=...  4.67 us
    reduce_sum x3, other arithmetic, layer_norm(): spread = jnp.mean(center * center, axis=-1, keepdims=True)  2.96 us
    reshape x1, local copies, waits for them, and re-layouts, body_split(): edges = edges.reshape(n_row, n_col, 2, group, rows, cols)  2.7 us
    another operation x2, local copies, waits for them, and re-layouts, body_split(): jnp.stack([left, right], axis=0).reshape(2, rows, cols, n_dev, group)  2.15 us
    dot_general x1, matrix products, transition(): jnp.dot(trans_hidden, w_down, preferred_element_type=jnp.float32)  2.1 us
  transfers between devices with their start and end apart: 1, of which 1 were waited for; matrix products, arithmetic and copies ran while one was open for 2% of the time, Pallas kernels for 0%

profile of v1, /device:TPU:0, one launch (start us, length us, event | category | flops | bytes accessed | tf_op | source)
XLA Modules:
  0.0 84.7 jit_solution(1117473404277247754)
XLA Ops:
  0.0 1.4 %convert_reduce_fusion = f32[32,64]{1,0:T(8,128)S(1)} fusion(bf16[32,64,128]{2,1,0:T(8,128)(2,1)} %param.10), kind=kLoop, calls=%fused_computation.40 | loop fusion | flops 522240 | bytes 532480 | tf_op jit(solution)/shard_map/reduce_sum | solution.py:10
  1.4 1.7 %multiply_reduce_fusion.1 = f32[32,64]{1,0:T(8,128)S(1)} fusion(bf16[32,64,128]{2,1,0:T(8,128)(2,1)} %param.10, f32[32,64]{1,0:T(8,128)S(1)} %broadcast_multiply_fusion.2), kind=kLoop, calls=%fused_computation.39 | loop fusion | flops 1046528 | bytes 540672 | tf_op jit(solution)/shard_map/reduce_sum | solution.py:11
  3.1 0.1 div.32
  3.2 0.7 convert_element_type.41
  3.9 0.1 dynamic_slice.6
  4.0 0.1 dynamic_slice.7
  4.0 0.1 broadcast_multiply_fusion
  4.1 0.1 mul.93
  4.2 0.1 rsqrt.31
  4.3 1.6 %fusion.20 = bf16[2048,128]{1,0:T(8,128)(2,1)S(1)} fusion(bf16[32,64,128]{2,1,0:T(8,128)(2,1)} %param.10, f32[2048]{0:T(1024)S(1)} %rsqrt.31, f32[2048]{0:T(1024)S(1)} %div.32), kind=kLoop, calls=%fused_computation.36 | loop fusion | flops 1048576 | bytes 1064960 | tf_op jit(solution)/shard_map/convert_element_type | solution.py:24
  5.9 0.0 copy-start.3
  5.9 0.4 fusion.4
  6.4 0.3 copy-done.3
  6.7 0.4 fusion.13
  7.1 0.2 copy.18
  7.3 1.1 %stack.10 = bf16[1,32,64,32,4]{2,1,4,3,0:T(8,128)(2,1)S(1)} reshape(bf16[2048,128]{0,1:T(8,128)(2,1)S(1)} %copy.18) | data formatting | bytes 1048576 | tf_op jit(solution)/shard_map/stack | solution.py:55
  8.4 0.4 fusion.8
  8.8 0.3 copy-done.4
  9.1 0.4 fusion.12
  9.5 0.2 copy.17
  9.7 1.1 %stack.9 = bf16[1,32,64,32,4]{2,1,4,3,0:T(8,128)(2,1)S(1)} reshape(bf16[2048,128]{0,1:T(8,128)(2,1)S(1)} %copy.17) | data formatting | bytes 1048576 | tf_op jit(solution)/shard_map/stack | solution.py:55
  10.8 0.5 maximum_bitcast_fusion
  11.3 0.5 copy.19
  11.8 2.3 %reshape.131 = bf16[32,2,8192]{2,1,0:T(2,128)(2,1)} reshape(bf16[32,2,4,32,64]{4,3,2,1,0:T(8,128)(2,1)S(1)} %copy.19) | data formatting | bytes 2097152
  14.0 32.5 %all_to_all.10 = bf16[32,2,8192]{2,1,0:T(2,128)(2,1)} all-to-all(bf16[32,2,8192]{2,1,0:T(2,128)(2,1)} %reshape.131), channel_id=1, replica_groups=mesh['row'=8,'col'=4] {'row','col'}, dimensions={0} | all-to-all | bytes 2097152 | tf_op jit(solution)/shard_map/all_to_all | solution.py:57
  46.5 3.8 %reshape.132 = bf16[32,2,4,32,64]{4,3,2,1,0:T(8,128)(2,1)S(1)} reshape(bf16[32,2,8192]{2,1,0:T(2,128)(2,1)} %all_to_all.10) | data formatting | bytes 2097152
  50.3 2.7 %copy.24 = bf16[8,4,2,4,32,64]{5,1,4,0,3,2:T(4,128)(2,1)S(1)} copy(bf16[8,4,2,4,32,64]{5,4,3,2,1,0:T(8,128)(2,1)S(1)} %bitcast.56) | data formatting | bytes 2097152 | tf_op jit(solution)/shard_map/reshape | solution.py:58
  53.0 1.6 %fusion.26 = (bf16[1,4,8,32,4,64]{5,4,3,2,1,0:T(4,128)(2,1)S(1)}, bf16[1,4,8,32,4,64]{5,4,3,2,1,0:T(4,128)(2,1)S(1)}) fusion(bf16[2,4,8,32,4,64]{5,4,3,2,1,0:T(4,128)(2,1)S(1)} %bitcast.55), kind=kLoop, calls=%fused_computation.51 | loop fusion | bytes 2097152 | tf_op jit(solution)/shard_map/slice | solution.py:61
  54.6 0.7 squeeze.6
  55.2 0.7 squeeze.7
  55.9 0.3 convolution_convert_fusion
  56.2 0.4 reshape.126
  56.7 0.2 copy.21
  56.9 1.5 %reshape.133 = bf16[32,2,4096]{2,1,0:T(2,128)(2,1)} reshape(bf16[32,4,32,64]{3,2,1,0:T(8,128)(2,1)S(1)} %bitcast.57) | data formatting | bytes 1048576
  58.5 4.7 %all-to-all-start.1 = ((bf16[32,2,4096]{2,1,0:T(2,128)(2,1)}), bf16[32,2,4096]{2,1,0:T(2,128)(2,1)S(1)}, u32[]{:S(2)}, u32[]{:S(2)}) async-start(bf16[32,2,4096]{2,1,0:T(2,128)(2,1)} %reshape.133), calls=%async_computation.1 | async-start | bytes 1048576 | tf_op jit(solution)/shard_map/all_to_all | solution.py:65
  63.1 1.4 %fusion.11 = f32[2048,128]{1,0:T(8,128)} fusion(bf16[2048,128]{1,0:T(8,128)(2,1)S(1)} %fusion.20, bf16[128,128]{1,0:T(8,128)(2,1)S(1)} %copy-done.9), kind=kOutput, calls=%fused_computation.19 | convolution fusion | flops 67895296 | bytes 1605632 | tf_op jit(solution)/shard_map/dot_general | solution.py:25
  64.6 12.7 %all-to-all-done.1 = bf16[32,2,4096]{2,1,0:T(2,128)(2,1)S(1)} async-done(((bf16[32,2,4096]{2,1,0:T(2,128)(2,1)}), bf16[32,2,4096]{2,1,0:T(2,128)(2,1)S(1)}, u32[]{:S(2)}, u32[]{:S(2)}) %all-to-all-start.1) | async-done | bytes 524320 | tf_op jit(solution)/shard_map/all_to_all | solution.py:65
  77.3 0.7 reshape.134
  78.0 0.3 bitcast_convert_fusion
  78.3 1.3 %copy.22 = f32[128,32,64]{0,2,1:T(8,128)S(1)} copy(f32[128,32,64]{2,1,0:T(8,128)S(1)} %bitcast_convert_fusion) | data formatting | bytes 2097152 | tf_op jit(solution)/shard_map/convert_element_type | solution.py:67
  79.6 0.3 bitcast_reduce_fusion
  80.0 0.6 fusion.18
  80.6 0.1 div.38
  80.7 0.1 rsqrt.33
  80.8 0.6 fusion.16
  81.4 0.5 fusion.27
  82.0 0.6 multiply_reduce_fusion
  82.6 2.1 %fusion.14 = bf16[2048,128]{1,0:T(8,128)(2,1)} fusion(f32[2048,128]{1,0:T(8,128)S(1)} %get-tuple-element.8, bf16[512,128]{1,0:T(8,128)(2,1)S(1)} %copy-done, bf16[128,512]{1,0:T(8,128)(2,1)S(1)} %copy-done.6, f32[2048]{0:T(1024)S(1)} %add_rsqrt_fusion.2, f32[2048]{0:T(1024)S(1)} %broadcast_multiply_fusion.3), kind=kOutput, calls=%fused_computation.22 | convolution fusion | flops 540278784 | bytes 1851392 | tf_op jit(solution)/shard_map/dot_general | solution.py:46
  (23 shorter events, 0.1 us)
Async XLA Ops:
  0.0 82.6 %copy-start = (bf16[512,128]{1,0:T(8,128)(2,1)S(1)}, bf16[512,128]{1,0:T(8,128)(2,1)}, u32[]{:S(2)}) copy-start(bf16[512,128]{1,0:T(8,128)(2,1)} %param.19) | copy-start | bytes 393220
  0.0 5.9 %copy-start.7 = (bf16[128,128]{1,0:T(8,128)(2,1)S(1)}, bf16[128,128]{1,0:T(8,128)(2,1)}, u32[]{:S(2)}) copy-start(bf16[128,128]{1,0:T(8,128)(2,1)} %param.14) | copy-start | bytes 98308
  5.9 0.8 copy-start.3
  6.7 1.7 %copy-start.8 = (bf16[128,128]{1,0:T(8,128)(2,1)S(1)}, bf16[128,128]{1,0:T(8,128)(2,1)}, u32[]{:S(2)}) copy-start(bf16[128,128]{1,0:T(8,128)(2,1)} %param.12) | copy-start | bytes 98308
  8.4 0.8 copy-start.4
  56.7 6.5 %copy-start.9 = (bf16[128,128]{1,0:T(8,128)(2,1)S(1)}, bf16[128,128]{1,0:T(8,128)(2,1)}, u32[]{:S(2)}) copy-start(bf16[128,128]{1,0:T(8,128)(2,1)} %param.16) | copy-start | bytes 98308
  58.5 18.8 %all-to-all-start.1 = ((bf16[32,2,4096]{2,1,0:T(2,128)(2,1)}), bf16[32,2,4096]{2,1,0:T(2,128)(2,1)S(1)}, u32[]{:S(2)}, u32[]{:S(2)}) async-start(bf16[32,2,4096]{2,1,0:T(2,128)(2,1)} %reshape.133), calls=%async_computation.1 | async-start | bytes 1048576 | tf_op jit(solution)/shard_map/all_to_all | solution.py:65
  79.6 1.8 %copy-start.1 = (bf16[32,64,128]{2,1,0:T(8,128)(2,1)S(1)}, bf16[32,64,128]{2,1,0:T(8,128)(2,1)}, u32[]{:S(2)}) copy-start(bf16[32,64,128]{2,1,0:T(8,128)(2,1)} %param.10) | copy-start | bytes 1572868
  79.6 1.8 %copy-start.2 = (f32[2048,128]{1,0:T(8,128)S(1)}, f32[2048,128]{1,0:T(8,128)}, u32[]{:S(2)}) copy-start(f32[2048,128]{1,0:T(8,128)} %fusion.11) | copy-start | bytes 3145732
  79.6 1.8 %copy-start.5 = (bf16[128,128]{1,0:T(8,128)(2,1)S(1)}, bf16[128,128]{1,0:T(8,128)(2,1)}, u32[]{:S(2)}) copy-start(bf16[128,128]{1,0:T(8,128)(2,1)} %param.17) | copy-start | bytes 98308
  81.4 1.2 %copy-start.6 = (bf16[128,512]{1,0:T(8,128)(2,1)S(1)}, bf16[128,512]{1,0:T(8,128)(2,1)}, u32[]{:S(2)}) copy-start(bf16[128,512]{1,0:T(8,128)(2,1)} %param.18) | copy-start | bytes 393220

commit v2 on v1

--- a/solution.py
+++ b/solution.py
@@ -3,6 +3,7 @@
 import jax
 import jax.numpy as jnp
 from jax import lax
+from jax.experimental import pallas as pl
 from jax.sharding import PartitionSpec as P
 
 
@@ -69,6 +70,60 @@
     return result.astype(jnp.bfloat16).reshape(rows, cols, width)
 
 
+def mix_kernel(edges_ref, out_ref, *, n_col):
+    n_dev, _, pairs, rows, lanes = edges_ref.shape
+    n_row = n_dev // n_col
+    cols = lanes // 2
+    parity = (lax.broadcasted_iota(jnp.int32, (1, n_col * lanes), 1) // cols) % 2
+    for hp in range(pairs):
+
+        def whole(side):
+            return jnp.concatenate(
+                [
+                    jnp.concatenate([edges_ref[r * n_col + c, side, hp] for c in range(n_col)], axis=1)
+                    for r in range(n_row)
+                ],
+                axis=0,
+            )
+
+        left = whole(0)
+        right = whole(1)
+        right_even = jnp.where(parity == 0, right, jnp.zeros_like(right))
+        right_odd = jnp.where(parity == 1, right, jnp.zeros_like(right))
+        for c in range(n_col):
+            block = slice(c * cols, (c + 1) * cols)
+            rhs = jnp.concatenate([right_even[block], right_odd[block]], axis=0)
+            mixed = lax.dot_general(
+                left, rhs, (((1,), (1,)), ((), ())), preferred_element_type=jnp.float32
+            ).astype(out_ref.dtype)
+            for r in range(n_row):
+                out_ref[r * n_col + c, hp] = mixed[r * rows : (r + 1) * rows]
+
+
+def body_kernel(pair, mask, w_agate, w_aproj, w_bgate, w_bproj, w_gate, w_out, w_up, w_down, *, n_row, n_col):
+    rows, cols, width = pair.shape
+    n_dev = n_row * n_col
+    pair_flat, gate, left, right = project(pair, mask, w_agate, w_aproj, w_bgate, w_bproj, w_gate)
+    hid = left.shape[-1]
+    pairs = hid // n_dev // 2
+
+    def chunks(edges):
+        edges = jnp.transpose(edges.reshape(rows, cols, n_dev, pairs, 2), (2, 3, 0, 4, 1))
+        return edges.reshape(n_dev, pairs, rows, 2 * cols)
+
+    edges = jnp.stack([chunks(left), chunks(right)], axis=1)
+    edges = lax.all_to_all(edges, ("row", "col"), split_axis=0, concat_axis=0, tiled=True)
+    mixed = pl.pallas_call(
+        functools.partial(mix_kernel, n_col=n_col),
+        out_shape=jax.ShapeDtypeStruct((n_dev, pairs, rows, 2 * cols), jnp.bfloat16),
+    )(edges)
+    mixed = lax.all_to_all(mixed, ("row", "col"), split_axis=0, concat_axis=0, tiled=True)
+    mixed = jnp.transpose(mixed.reshape(n_dev, pairs, rows, 2, cols), (2, 4, 0, 1, 3))
+    mixed_rows = mixed.astype(jnp.float32).reshape(rows * cols, hid)
+    result = transition(pair_flat, gate, mixed_rows, w_out, w_up, w_down)
+    return result.astype(jnp.bfloat16).reshape(rows, cols, width)
+
+
 def body_rows(pair, mask, w_agate, w_aproj, w_bgate, w_bproj, w_gate, w_out, w_up, w_down):
     rows, cols, width = pair.shape
     pair_flat, gate, left, right = project(pair, mask, w_agate, w_aproj, w_bgate, w_bproj, w_gate)
@@ -108,7 +163,10 @@
 
     def run(pair, mask, w_agate, *weights):
         hid = w_agate.shape[1]
-        if hid % (n_row * n_col) == 0:
+        rows, cols = pair.shape[0] // n_row, pair.shape[1] // n_col
+        if hid % (2 * n_row * n_col) == 0 and 2 * cols == 128 and rows % 16 == 0 and n_row * rows == n_col * cols:
+            body = functools.partial(body_kernel, n_row=n_row, n_col=n_col)
+        elif hid % (n_row * n_col) == 0:
             body = functools.partial(body_split, n_row=n_row, n_col=n_col)
         else:
             body = body_rows

time: 86 us -> 79.6 us (0.926)
  local copies, waits for them, and re-layouts: 20 us -> 11.8 us
  Pallas kernels: 0 us -> 2.74 us
  other arithmetic: 8.6 us -> 6.84 us
  matrix products: 5.92 us -> 6.93 us
    unnamed x24 -> x18, local copies, waits for them, and re-layouts: 8.91 us -> 0.68 us
    pallas_call x0 -> x1, Pallas kernels: none -> 2.74 us  [body_kernel(): pl.pallas_call(functools.partial(mix_kernel, n_col=n_col), out_shape=jax....]
    transpose x1 -> x2, local copies, waits for them, and re-layouts: 0.49 us -> 2.18 us  [chunks(): jnp.transpose(edges.reshape(rows, cols, n_dev, pairs, 2), (2, 3, 0, 4, 1))]
    slice x1 -> x0, local copies, waits for them, and re-layouts: 1.55 us -> none  [body_split(): edges[1]]
    convert_element_type x1 -> x2, local copies, waits for them, and re-layouts: 1.29 us -> 2.75 us  [body_kernel(): mixed_rows = mixed.astype(jnp.float32).reshape(rows * cols, hid)]
    squeeze x2 -> x0, local copies, waits for them, and re-layouts: 1.33 us -> none  [the longest x1 0.67 us: body_split(): edges[0]]
    dot_general x1, matrix products: 0.51 us -> 1.83 us  [transition(): jnp.dot(mixed_normed, w_out, preferred_element_type=jnp.float32)]
    another operation x2, local copies, waits for them, and re-layouts: 2.15 us -> 0.97 us  [body_kernel(): edges = jnp.stack([chunks(left), chunks(right)], axis=1)]
where the time goes in v2:
time: 79.6 us; the launch traced here: 78.2 us
  blocking collectives  32.3 us (41%)
  waiting for transfers between devices  12.8 us (16%)
  local copies, waits for them, and re-layouts  11.8 us (15%)
  matrix products  6.93 us (9%)
  other arithmetic  6.84 us (9%)
  starting transfers between devices  4.63 us (6%)
  Pallas kernels  2.74 us (3%)
    all_to_all x1, blocking collectives, body_kernel(): lax.all_to_all(edges, ('row', 'col'), split_axis=0, concat_axis=0, tiled=...  32.3 us
    all_to_all x1, waiting for transfers between devices, body_kernel(): lax.all_to_all(mixed, ('row', 'col'), split_axis=0, concat_axis=0, tiled=...  12.8 us
    all_to_all x1, starting transfers between devices, body_kernel(): lax.all_to_all(mixed, ('row', 'col'), split_axis=0, concat_axis=0, tiled=...  4.63 us
    convert_element_type x2, local copies, waits for them, and re-layouts, body_kernel(): mixed_rows = mixed.astype(jnp.float32).reshape(rows * cols, hid)  2.75 us
    pallas_call x1, Pallas kernels, body_kernel(): pl.pallas_call(functools.partial(mix_kernel, n_col=n_col), out_shape=jax....  2.74 us
    reduce_sum x3, other arithmetic, layer_norm(): spread = jnp.mean(center * center, axis=-1, keepdims=True)  2.65 us
    transpose x2, local copies, waits for them, and re-layouts, chunks(): jnp.transpose(edges.reshape(rows, cols, n_dev, pairs, 2), (2, 3, 0, 4, 1))  2.18 us
    reshape x2, local copies, waits for them, and re-layouts, chunks(): edges.reshape(rows, cols, n_dev, pairs, 2)  2.15 us
  transfers between devices with their start and end apart: 1, of which 1 were waited for; matrix products, arithmetic and copies ran while one was open for 2% of the time, Pallas kernels for 0%

profile of v2, /device:TPU:0, one launch (start us, length us, event | category | flops | bytes accessed | tf_op | source)
XLA Modules:
  0.0 78.2 jit_solution(9887206048797390879)
XLA Ops:
  0.0 0.0 copy-start
  0.0 1.4 %convert_reduce_fusion = f32[32,64]{1,0:T(8,128)S(1)} fusion(bf16[32,64,128]{2,1,0:T(8,128)(2,1)} %param.10), kind=kLoop, calls=%fused_computation.33 | loop fusion | flops 522240 | bytes 532480 | tf_op jit(solution)/shard_map/reduce_sum | solution.py:11
  1.4 1.7 %multiply_reduce_fusion.2 = f32[32,64]{1,0:T(8,128)S(1)} fusion(bf16[32,64,128]{2,1,0:T(8,128)(2,1)} %param.10, f32[32,64]{1,0:T(8,128)S(1)} %broadcast_multiply_fusion.2), kind=kLoop, calls=%fused_computation.32 | loop fusion | flops 1046528 | bytes 540672 | tf_op jit(solution)/shard_map/reduce_sum | solution.py:12
  3.1 0.1 div.32
  3.2 0.7 convert_element_type.38
  3.9 0.1 dynamic_slice.6
  4.0 0.1 dynamic_slice.7
  4.0 0.1 broadcast_multiply_fusion
  4.1 0.1 mul.93
  4.2 0.1 rsqrt.31
  4.3 1.6 %fusion.16 = bf16[2048,128]{1,0:T(8,128)(2,1)S(1)} fusion(bf16[32,64,128]{2,1,0:T(8,128)(2,1)} %param.10, f32[2048]{0:T(1024)S(1)} %rsqrt.31, f32[2048]{0:T(1024)S(1)} %div.32), kind=kLoop, calls=%fused_computation.28 | loop fusion | flops 1048576 | bytes 1064960 | tf_op jit(solution)/shard_map/convert_element_type | solution.py:25
  5.9 0.0 copy-done.6
  5.9 0.0 copy-start.2
  5.9 0.4 fusion.8
  6.4 0.3 copy-done.2
  6.7 0.4 fusion.12
  7.1 0.2 copy.13
  7.3 1.1 %reshape.112 = bf16[32,64,32,2,2]{1,0,4,3,2:T(8,128)(2,1)S(1)} reshape(bf16[2048,128]{0,1:T(8,128)(2,1)S(1)} %copy.13) | data formatting | bytes 1048576 | tf_op jit(solution)/shard_map/reshape | solution.py:111
  8.4 0.0 copy-start.7
  8.4 1.1 %copy.14 = bf16[32,2,32,2,64]{4,3,2,1,0:T(2,128)(2,1)S(1)} copy(bf16[32,2,32,2,64]{4,2,3,1,0:T(8,128)(2,1)S(1)} %bitcast.42) | data formatting | bytes 1048576 | tf_op jit(solution)/shard_map/transpose | solution.py:111
  9.5 0.5 stack_reshape.6
  10.0 0.0 copy-done.7
  10.0 0.0 copy-start.3
  10.0 0.4 fusion.4
  10.4 0.3 copy-done.3
  10.7 0.4 fusion.13
  11.1 0.2 copy.15
  11.3 1.1 %reshape.113 = bf16[32,64,32,2,2]{1,0,4,3,2:T(8,128)(2,1)S(1)} reshape(bf16[2048,128]{0,1:T(8,128)(2,1)S(1)} %copy.15) | data formatting | bytes 1048576 | tf_op jit(solution)/shard_map/reshape | solution.py:111
  12.4 1.1 %copy.16 = bf16[32,2,32,2,64]{4,3,2,1,0:T(2,128)(2,1)S(1)} copy(bf16[32,2,32,2,64]{4,2,3,1,0:T(8,128)(2,1)S(1)} %bitcast.43) | data formatting | bytes 1048576 | tf_op jit(solution)/shard_map/transpose | solution.py:111
  13.5 0.5 stack_reshape.7
  14.0 0.1 pad_maximum_fusion
  14.1 0.0 copy-start.8
  14.1 32.3 %all_to_all.10.edges_ref = bf16[32,2,2,32,128]{4,3,2,1,0:T(8,128)(2,1)} all-to-all(bf16[32,2,2,32,128]{4,3,2,1,0:T(8,128)(2,1)S(1)} %pad_maximum_fusion), channel_id=1, replica_groups=mesh['row'=8,'col'=4] {'row','col'}, dimensions={0} | all-to-all | bytes 2097152 | tf_op jit(solution)/shard_map/all_to_all | solution.py:115
  46.4 2.7 %shard_map.100 = bf16[32,2,32,128]{3,2,1,0:T(8,128)(2,1)} custom-call(bf16[32,2,2,32,128]{4,3,2,1,0:T(8,128)(2,1)} %all_to_all.10.edges_ref), custom_call_target="tpu_custom_call" | custom-call | tf_op jit(solution)/shard_map/pallas_call | solution.py:116
  49.1 4.6 %all-to-all-start.1 = ((bf16[32,2,32,128]{3,2,1,0:T(8,128)(2,1)}), bf16[32,2,32,128]{3,2,1,0:T(8,128)(2,1)S(1)}, u32[]{:S(2)}, u32[]{:S(2)}) async-start(bf16[32,2,32,128]{3,2,1,0:T(8,128)(2,1)} %shard_map.100), calls=%async_computation.1 | async-start | bytes 1048576 | tf_op jit(solution)/shard_map/all_to_all | solution.py:120
  53.8 1.4 %fusion.11 = f32[2048,128]{1,0:T(8,128)} fusion(bf16[2048,128]{1,0:T(8,128)(2,1)S(1)} %fusion.16, bf16[128,128]{1,0:T(8,128)(2,1)S(1)} %copy-done.8), kind=kOutput, calls=%fused_computation.19 | convolution fusion | flops 67895296 | bytes 1605632 | tf_op jit(solution)/shard_map/dot_general | solution.py:26
  55.2 12.8 %all-to-all-done.1 = bf16[32,2,32,128]{3,2,1,0:T(8,128)(2,1)S(1)} async-done(((bf16[32,2,32,128]{3,2,1,0:T(8,128)(2,1)}), bf16[32,2,32,128]{3,2,1,0:T(8,128)(2,1)S(1)}, u32[]{:S(2)}, u32[]{:S(2)}) %all-to-all-start.1) | async-done | bytes 524320 | tf_op jit(solution)/shard_map/all_to_all | solution.py:120
  67.9 1.1 %reshape.116 = f32[32,2,32,2,64]{4,3,2,1,0:T(2,128)S(1)} reshape(bf16[32,2,32,128]{3,2,1,0:T(8,128)(2,1)S(1)} %all-to-all-done.1) | data formatting | bytes 1572864 | tf_op jit(solution)/shard_map/convert_element_type | solution.py:122
  69.1 0.2 fusion.24
  69.3 0.3 multiply_reduce_fusion
  69.6 0.1 div.38
  69.7 1.6 %copy.23 = f32[32,2,32,2,64]{4,2,3,1,0:T(8,128)} copy(f32[32,2,32,2,64]{4,3,2,1,0:T(2,128)S(1)} %reshape.116) | data formatting | bytes 2097152 | tf_op jit(solution)/shard_map/convert_element_type | solution.py:122
  71.4 0.1 rsqrt.33
  71.4 2.1 %reshape.114 = f32[2048,128]{0,1:T(8,128)S(1)} reshape(f32[32,64,32,2,2]{1,0,4,3,2:T(8,128)} %bitcast.41) | data formatting | bytes 2097152 | tf_op jit(solution)/shard_map/reshape | solution.py:122
  73.6 0.0 copy-start.5
  73.6 1.8 %fusion.25 = (f32[2048]{0:T(1024)S(1)}, f32[2048,128]{1,0:T(8,128)S(1)}) fusion(f32[2048,128]{1,0:T(8,128)} %fusion.11, bf16[128,128]{1,0:T(8,128)(2,1)S(1)} %copy-done.4, f32[2048,128]{0,1:T(8,128)S(1)} %reshape.114, f32[2048]{0:T(1024)S(1)} %rsqrt.33, f32[2048]{0:T(1024)S(1)} %div.38, bf16[2048,128]{1,0:T(8,128)(2,1)S(1)} %bitcast.40), kind=kOutput, calls=%fused_computation.47 | convolution fusion | flops 68941824 | bytes 3727360 | tf_op jit(solution)/shard_map/dot_general | solution.py:42
  75.4 0.6 multiply_reduce_fusion.1
  76.1 2.1 %fusion.14 = bf16[2048,128]{1,0:T(8,128)(2,1)} fusion(f32[2048,128]{1,0:T(8,128)S(1)} %get-tuple-element.6, bf16[512,128]{1,0:T(8,128)(2,1)S(1)} %copy-done, bf16[128,512]{1,0:T(8,128)(2,1)S(1)} %copy-done.5, f32[2048]{0:T(1024)S(1)} %add_rsqrt_fusion.2, f32[2048]{0:T(1024)S(1)} %broadcast_multiply_fusion.3), kind=kOutput, calls=%fused_computation.22 | convolution fusion | flops 540278784 | bytes 1851392 | tf_op jit(solution)/shard_map/dot_general | solution.py:47
  (14 shorter events, 0.1 us)
Async XLA Ops:
  0.0 76.1 %copy-start = (bf16[512,128]{1,0:T(8,128)(2,1)S(1)}, bf16[512,128]{1,0:T(8,128)(2,1)}, u32[]{:S(2)}) copy-start(bf16[512,128]{1,0:T(8,128)(2,1)} %param.19) | copy-start | bytes 393220
  0.0 5.9 %copy-start.6 = (bf16[128,128]{1,0:T(8,128)(2,1)S(1)}, bf16[128,128]{1,0:T(8,128)(2,1)}, u32[]{:S(2)}) copy-start(bf16[128,128]{1,0:T(8,128)(2,1)} %param.12) | copy-start | bytes 98308
  5.9 0.8 copy-start.2
  8.4 1.6 %copy-start.7 = (bf16[128,128]{1,0:T(8,128)(2,1)S(1)}, bf16[128,128]{1,0:T(8,128)(2,1)}, u32[]{:S(2)}) copy-start(bf16[128,128]{1,0:T(8,128)(2,1)} %param.14) | copy-start | bytes 98308
  10.0 0.8 copy-start.3
  14.1 39.6 %copy-start.8 = (bf16[128,128]{1,0:T(8,128)(2,1)S(1)}, bf16[128,128]{1,0:T(8,128)(2,1)}, u32[]{:S(2)}) copy-start(bf16[128,128]{1,0:T(8,128)(2,1)} %param.16) | copy-start | bytes 98308
  49.1 18.8 %all-to-all-start.1 = ((bf16[32,2,32,128]{3,2,1,0:T(8,128)(2,1)}), bf16[32,2,32,128]{3,2,1,0:T(8,128)(2,1)S(1)}, u32[]{:S(2)}, u32[]{:S(2)}) async-start(bf16[32,2,32,128]{3,2,1,0:T(8,128)(2,1)} %shard_map.100), calls=%async_computation.1 | async-start | bytes 1048576 | tf_op jit(solution)/shard_map/all_to_all | solution.py:120
  71.3 2.2 %copy-start.1 = (bf16[32,64,128]{2,1,0:T(8,128)(2,1)S(1)}, bf16[32,64,128]{2,1,0:T(8,128)(2,1)}, u32[]{:S(2)}) copy-start(bf16[32,64,128]{2,1,0:T(8,128)(2,1)} %param.10) | copy-start | bytes 1572868
  71.3 2.2 %copy-start.4 = (bf16[128,128]{1,0:T(8,128)(2,1)S(1)}, bf16[128,128]{1,0:T(8,128)(2,1)}, u32[]{:S(2)}) copy-start(bf16[128,128]{1,0:T(8,128)(2,1)} %param.17) | copy-start | bytes 98308
  73.6 2.5 %copy-start.5 = (bf16[128,512]{1,0:T(8,128)(2,1)S(1)}, bf16[128,512]{1,0:T(8,128)(2,1)}, u32[]{:S(2)}) copy-start(bf16[128,512]{1,0:T(8,128)(2,1)} %param.18) | copy-start | bytes 393220

commit v3 on v2

--- a/solution.py
+++ b/solution.py
@@ -124,6 +124,67 @@
     return result.astype(jnp.bfloat16).reshape(rows, cols, width)
 
 
+def project_kernel(pair_ref, mask_ref, w2_ref, wg_ref, z_ref, gate_ref):
+    rows, cols, width = pair_ref.shape
+    quarter = w2_ref.shape[0] // 4
+
+    def row(i, carry):
+        values = pair_ref[i].astype(jnp.float32)
+        center = values - jnp.mean(values, axis=-1, keepdims=True)
+        spread = jnp.mean(center * center, axis=-1, keepdims=True)
+        normed = (center * lax.rsqrt(spread + 1e-05)).astype(jnp.bfloat16)
+        gate_ref[i] = jax.nn.sigmoid(jnp.dot(normed, wg_ref[...], preferred_element_type=jnp.float32))
+        zeros = jnp.zeros_like(normed)
+        doubled = jnp.concatenate(
+            [jnp.concatenate([normed, zeros], axis=1), jnp.concatenate([zeros, normed], axis=1)], axis=0
+        )
+        proj = lax.dot_general(
+            w2_ref[...], doubled, (((1,), (1,)), ((), ())), preferred_element_type=jnp.float32
+        )
+        present = mask_ref[pl.ds(i, 1), :]
+        left = jax.nn.sigmoid(proj[0:quarter]) * proj[quarter : 2 * quarter] * present
+        right = jax.nn.sigmoid(proj[2 * quarter : 3 * quarter]) * proj[3 * quarter :] * present
+        z_ref[i] = jnp.concatenate([left, right], axis=0).astype(z_ref.dtype)
+        return carry
+
+    lax.fori_loop(0, rows, row, 0)
+
+
+def body_fused(pair, mask, w_agate, w_aproj, w_bgate, w_bproj, w_gate, w_out, w_up, w_down, *, n_row, n_col):
+    rows, cols, width = pair.shape
+    n_dev = n_row * n_col
+    hid = w_agate.shape[1]
+    pairs = hid // n_dev // 2
+    present = mask.astype(jnp.float32)
+    row_mask = lax.dynamic_slice_in_dim(present, lax.axis_index("row") * rows, rows, 0)
+    col_mask = lax.dynamic_slice_in_dim(present, lax.axis_index("col") * cols, cols, 0)
+    lane_mask = row_mask[:, None] * jnp.concatenate([col_mask, col_mask])[None, :]
+
+    def paired(w):
+        return jnp.transpose(w.reshape(width, hid // 2, 2), (1, 2, 0)).reshape(hid // 2, 2 * width)
+
+    w2 = jnp.concatenate([paired(w) for w in (w_agate, w_aproj, w_bgate, w_bproj)], axis=0)
+    z, gate = pl.pallas_call(
+        project_kernel,
+        out_shape=(
+            jax.ShapeDtypeStruct((rows, hid, 2 * cols), jnp.bfloat16),
+            jax.ShapeDtypeStruct((rows, cols, width), jnp.float32),
+        ),
+    )(pair, lane_mask, w2, w_gate)
+    edges = jnp.transpose(z.reshape(rows, 2, n_dev, pairs, 2 * cols), (2, 1, 3, 0, 4))
+    edges = lax.all_to_all(edges, ("row", "col"), split_axis=0, concat_axis=0, tiled=True)
+    mixed = pl.pallas_call(
+        functools.partial(mix_kernel, n_col=n_col),
+        out_shape=jax.ShapeDtypeStruct((n_dev, pairs, rows, 2 * cols), jnp.bfloat16),
+    )(edges)
+    mixed = lax.all_to_all(mixed, ("row", "col"), split_axis=0, concat_axis=0, tiled=True)
+    mixed = jnp.transpose(mixed.reshape(n_dev, pairs, rows, 2, cols), (2, 4, 0, 1, 3))
+    mixed_rows = mixed.astype(jnp.float32).reshape(rows * cols, hid)
+    pair_flat = pair.astype(jnp.float32).reshape(rows * cols, width)
+    result = transition(pair_flat, gate.reshape(rows * cols, width), mixed_rows, w_out, w_up, w_down)
+    return result.astype(jnp.bfloat16).reshape(rows, cols, width)
+
+
 def body_rows(pair, mask, w_agate, w_aproj, w_bgate, w_bproj, w_gate, w_out, w_up, w_down):
     rows, cols, width = pair.shape
     pair_flat, gate, left, right = project(pair, mask, w_agate, w_aproj, w_bgate, w_bproj, w_gate)
@@ -165,7 +226,7 @@
         hid = w_agate.shape[1]
         rows, cols = pair.shape[0] // n_row, pair.shape[1] // n_col
         if hid % (2 * n_row * n_col) == 0 and 2 * cols == 128 and rows % 16 == 0 and n_row * rows == n_col * cols:
-            body = functools.partial(body_kernel, n_row=n_row, n_col=n_col)
+            body = functools.partial(body_fused, n_row=n_row, n_col=n_col)
         elif hid % (n_row * n_col) == 0:
             body = functools.partial(body_split, n_row=n_row, n_col=n_col)
         else:

time: 79.6 us -> 87.8 us (1.10)
  blocking collectives: 32.3 us -> 51.1 us
  Pallas kernels: 2.74 us -> 16.8 us
  waiting for transfers between devices: 12.8 us -> 0 us
  starting transfers between devices: 4.63 us -> 0 us
  other arithmetic: 6.84 us -> 3.36 us
  matrix products: 6.93 us -> 3.95 us
    all_to_all x1 -> x2, blocking collectives: 32.3 us -> 51.1 us  [the longest x1 32.3 us: body_fused(): lax.all_to_all(edges, ('row', 'col'), split_axis=0, concat_axis=0, tiled=...]
    pallas_call x1 -> x2, Pallas kernels: 2.74 us -> 16.8 us  [the longest x1 14.1 us: body_fused(): pl.pallas_call(project_kernel, out_shape=(jax.ShapeDtypeStruct((rows, hid...]
    all_to_all x1 -> x0, waiting for transfers between devices: 12.8 us -> none  [body_kernel(): lax.all_to_all(mixed, ('row', 'col'), split_axis=0, concat_axis=0, tiled=...]
    all_to_all x1 -> x0, starting transfers between devices: 4.63 us -> none  [body_kernel(): lax.all_to_all(mixed, ('row', 'col'), split_axis=0, concat_axis=0, tiled=...]
    dot_general x5 -> x0, matrix products: 2.98 us -> none  [the longest x1 1.4 us: project(): jnp.dot(normed, w_gate, preferred_element_type=jnp.float32)]
    unnamed x18 -> x12, local copies, waits for them, and re-layouts: 0.68 us -> 3.49 us
    transpose x2 -> x0, local copies, waits for them, and re-layouts: 2.18 us -> none  [chunks(): jnp.transpose(edges.reshape(rows, cols, n_dev, pairs, 2), (2, 3, 0, 4, 1))]
    reduce_sum x3 -> x2, other arithmetic: 2.65 us -> 0.96 us  [layer_norm(): spread = jnp.mean(center * center, axis=-1, keepdims=True)]
  transfers between devices with their start and end apart: 1 -> 0, of which waited for: 1 -> 0; matrix products, arithmetic and copies ran while one was open for 2% -> 0% of each run, Pallas kernels for 0% -> 0%
where the time goes in v3:
time: 87.8 us; the launch traced here: 86.5 us
  blocking collectives  51.1 us (58%)
  Pallas kernels  16.8 us (19%)
  local copies, waits for them, and re-layouts  11.1 us (13%)
  matrix products  3.95 us (4%)
  other arithmetic  3.36 us (4%)
    all_to_all x1, blocking collectives, body_fused(): lax.all_to_all(edges, ('row', 'col'), split_axis=0, concat_axis=0, tiled=...  32.3 us
    all_to_all x1, blocking collectives, body_fused(): lax.all_to_all(mixed, ('row', 'col'), split_axis=0, concat_axis=0, tiled=...  18.8 us
    pallas_call x1, Pallas kernels, body_fused(): pl.pallas_call(project_kernel, out_shape=(jax.ShapeDtypeStruct((rows, hid...  14.1 us
    unnamed x12, local copies, waits for them, and re-layouts  3.49 us
    convert_element_type x2, local copies, waits for them, and re-layouts, body_fused(): mixed_rows = mixed.astype(jnp.float32).reshape(rows * cols, hid)  2.75 us
    pallas_call x1, Pallas kernels, body_fused(): pl.pallas_call(functools.partial(mix_kernel, n_col=n_col), out_shape=jax....  2.73 us
    reshape x1, local copies, waits for them, and re-layouts, body_fused(): z.reshape(rows, 2, n_dev, pairs, 2 * cols)  2.44 us
    reshape x1, local copies, waits for them, and re-layouts, body_fused(): mixed_rows = mixed.astype(jnp.float32).reshape(rows * cols, hid)  2.13 us

profile of v3, /device:TPU:0, one launch (start us, length us, event | category | flops | bytes accessed | tf_op | source)
XLA Modules:
  0.0 86.5 jit_solution(7401123330619094625)
XLA Ops:
  0.0 0.0 copy-start
  0.0 0.7 convert_element_type.25
  0.7 0.1 dynamic_slice.6
  0.8 0.1 dynamic_slice.7
  0.9 0.1 pad_maximum_fusion.1
  0.9 0.9 copy.17
  1.8 0.9 %copy.18 = bf16[128,128]{0,1:T(8,128)(2,1)S(1)} copy(bf16[128,128]{1,0:T(8,128)(2,1)} %param.15) | data formatting | bytes 65536 | tf_op args[5]
  2.7 0.9 %copy.15 = bf16[128,128]{0,1:T(8,128)(2,1)S(1)} copy(bf16[128,128]{1,0:T(8,128)(2,1)} %param.12) | data formatting | bytes 65536 | tf_op args[2]
  3.6 0.9 %copy.16 = bf16[128,128]{0,1:T(8,128)(2,1)S(1)} copy(bf16[128,128]{1,0:T(8,128)(2,1)} %param.13) | data formatting | bytes 65536 | tf_op args[3]
  4.4 0.7 broadcast_multiply_fusion.1.mask_ref
  5.2 0.7 pad_maximum_fusion.w2_ref
  5.8 14.1 %shard_map.100 = (bf16[32,128,128]{2,1,0:T(8,128)(2,1)}, f32[32,64,128]{2,1,0:T(8,128)}) custom-call(bf16[32,64,128]{2,1,0:T(8,128)(2,1)} %pair_ref.1, f32[32,128]{1,0:T(8,128)} %broadcast_multiply_fusion.1.mask_ref, bf16[256,256]{1,0:T(8,128)(2,1)} %pad_maximum_fusion.w2_ref, bf16[128,128]{1,0:T(8,128)(2,1)} %wg_ref.1), custom_call_target="tpu_custom_call" | custom-call | tf_op jit(solution)/shard_map/pallas_call | solution.py:167
  19.9 2.4 %copy.39 = bf16[32,2,32,2,128]{4,0,3,1,2:T(8,128)(2,1)S(1)} copy(bf16[32,2,32,2,128]{4,3,2,1,0:T(2,128)(2,1)} %bitcast.52) | data formatting | bytes 2097152 | tf_op jit(solution)/shard_map/reshape | solution.py:174
  22.4 32.3 %all_to_all.10.edges_ref = bf16[32,2,2,32,128]{4,3,2,1,0:T(8,128)(2,1)} all-to-all(bf16[32,2,2,32,128]{4,3,2,1,0:T(8,128)(2,1)S(1)} %bitcast.49), channel_id=1, replica_groups=mesh['row'=8,'col'=4] {'row','col'}, dimensions={0} | all-to-all | bytes 2097152 | tf_op jit(solution)/shard_map/all_to_all | solution.py:175
  54.6 2.7 %shard_map.101 = bf16[32,2,32,128]{3,2,1,0:T(8,128)(2,1)} custom-call(bf16[32,2,2,32,128]{4,3,2,1,0:T(8,128)(2,1)} %all_to_all.10.edges_ref), custom_call_target="tpu_custom_call" | custom-call | tf_op jit(solution)/shard_map/pallas_call | solution.py:176
  57.4 18.8 %all_to_all.11 = bf16[32,2,32,128]{3,2,1,0:T(8,128)(2,1)S(1)} all-to-all(bf16[32,2,32,128]{3,2,1,0:T(8,128)(2,1)} %shard_map.101), channel_id=1, replica_groups=mesh['row'=8,'col'=4] {'row','col'}, dimensions={0} | all-to-all | bytes 1048576 | tf_op jit(solution)/shard_map/all_to_all | solution.py:180
  76.2 1.1 %reshape.107 = f32[32,2,32,2,64]{4,3,2,1,0:T(2,128)S(1)} reshape(bf16[32,2,32,128]{3,2,1,0:T(8,128)(2,1)S(1)} %all_to_all.11) | data formatting | bytes 1572864 | tf_op jit(solution)/shard_map/convert_element_type | solution.py:182
  77.3 0.2 fusion.9
  77.6 0.3 multiply_reduce_fusion
  77.9 0.1 div.15
  78.0 1.6 %copy.38 = f32[32,2,32,2,64]{4,2,3,1,0:T(8,128)} copy(f32[32,2,32,2,64]{4,3,2,1,0:T(2,128)S(1)} %reshape.107) | data formatting | bytes 2097152 | tf_op jit(solution)/shard_map/convert_element_type | solution.py:182
  79.6 0.0 copy-start.1
  79.6 0.0 copy-start.2
  79.6 0.1 rsqrt.20
  79.7 2.1 %reshape.103 = f32[2048,128]{0,1:T(8,128)S(1)} reshape(f32[32,64,32,2,2]{1,0,4,3,2:T(8,128)} %bitcast.48) | data formatting | bytes 2097152 | tf_op jit(solution)/shard_map/reshape | solution.py:182
  81.8 0.0 copy-done.1
  81.8 0.0 copy-done.2
  81.8 0.0 copy-start.3
  81.9 1.8 %fusion.10 = (f32[2048]{0:T(1024)S(1)}, f32[2048,128]{1,0:T(8,128)S(1)}) fusion(f32[2048,128]{1,0:T(8,128)} %bitcast.51, bf16[128,128]{1,0:T(8,128)(2,1)S(1)} %copy-done.2, f32[2048,128]{0,1:T(8,128)S(1)} %reshape.103, f32[2048]{0:T(1024)S(1)} %rsqrt.20, f32[2048]{0:T(1024)S(1)} %div.15, bf16[2048,128]{1,0:T(8,128)(2,1)S(1)} %bitcast.50), kind=kOutput, calls=%fused_computation.28 | convolution fusion | flops 68941824 | bytes 3727360 | tf_op jit(solution)/shard_map/dot_general | solution.py:42
  83.7 0.6 multiply_reduce_fusion.1
  84.4 0.0 copy-done
  84.4 0.0 copy-done.3
  84.4 2.1 %fusion.1 = bf16[2048,128]{1,0:T(8,128)(2,1)} fusion(f32[2048,128]{1,0:T(8,128)S(1)} %get-tuple-element.10, bf16[512,128]{1,0:T(8,128)(2,1)S(1)} %copy-done, bf16[128,512]{1,0:T(8,128)(2,1)S(1)} %copy-done.3, f32[2048]{0:T(1024)S(1)} %add_rsqrt_fusion.1, f32[2048]{0:T(1024)S(1)} %broadcast_multiply_fusion.2), kind=kOutput, calls=%fused_computation.4 | convolution fusion | flops 540278784 | bytes 1851392 | tf_op jit(solution)/shard_map/dot_general | solution.py:47
  (6 shorter events, 0.0 us)
Async XLA Ops:
  0.0 84.4 %copy-start = (bf16[512,128]{1,0:T(8,128)(2,1)S(1)}, bf16[512,128]{1,0:T(8,128)(2,1)}, u32[]{:S(2)}) copy-start(bf16[512,128]{1,0:T(8,128)(2,1)} %param.19) | copy-start | bytes 393220
  79.6 2.2 %copy-start.1 = (bf16[32,64,128]{2,1,0:T(8,128)(2,1)S(1)}, bf16[32,64,128]{2,1,0:T(8,128)(2,1)}, u32[]{:S(2)}) copy-start(bf16[32,64,128]{2,1,0:T(8,128)(2,1)} %pair_ref.1) | copy-start | bytes 1572868
  79.6 2.2 %copy-start.2 = (bf16[128,128]{1,0:T(8,128)(2,1)S(1)}, bf16[128,128]{1,0:T(8,128)(2,1)}, u32[]{:S(2)}) copy-start(bf16[128,128]{1,0:T(8,128)(2,1)} %param.17) | copy-start | bytes 98308
  81.8 2.5 %copy-start.3 = (bf16[128,512]{1,0:T(8,128)(2,1)S(1)}, bf16[128,512]{1,0:T(8,128)(2,1)}, u32[]{:S(2)}) copy-start(bf16[128,512]{1,0:T(8,128)(2,1)} %param.18) | copy-start | bytes 393220

commit v4 on v3

--- a/solution.py
+++ b/solution.py
@@ -124,30 +124,34 @@
     return result.astype(jnp.bfloat16).reshape(rows, cols, width)
 
 
-def project_kernel(pair_ref, mask_ref, w2_ref, wg_ref, z_ref, gate_ref):
+def project_kernel(pair_ref, mask_ref, w2_ref, wg_ref, z_ref, gate_ref, *, block):
     rows, cols, width = pair_ref.shape
     quarter = w2_ref.shape[0] // 4
 
-    def row(i, carry):
-        values = pair_ref[i].astype(jnp.float32)
+    def rows_of(step, carry):
+        first = pl.multiple_of(step * block, block)
+        values = pair_ref[pl.ds(first, block)].astype(jnp.float32).reshape(block * cols, width)
         center = values - jnp.mean(values, axis=-1, keepdims=True)
         spread = jnp.mean(center * center, axis=-1, keepdims=True)
         normed = (center * lax.rsqrt(spread + 1e-05)).astype(jnp.bfloat16)
-        gate_ref[i] = jax.nn.sigmoid(jnp.dot(normed, wg_ref[...], preferred_element_type=jnp.float32))
+        gate = jax.nn.sigmoid(jnp.dot(normed, wg_ref[...], preferred_element_type=jnp.float32))
+        gate_ref[pl.ds(first, block)] = gate.reshape(block, cols, width)
         zeros = jnp.zeros_like(normed)
-        doubled = jnp.concatenate(
-            [jnp.concatenate([normed, zeros], axis=1), jnp.concatenate([zeros, normed], axis=1)], axis=0
-        )
+        top = jnp.concatenate([normed, zeros], axis=1).reshape(block, cols, 2 * width)
+        bottom = jnp.concatenate([zeros, normed], axis=1).reshape(block, cols, 2 * width)
+        doubled = jnp.concatenate([top, bottom], axis=1).reshape(block * 2 * cols, 2 * width)
         proj = lax.dot_general(
             w2_ref[...], doubled, (((1,), (1,)), ((), ())), preferred_element_type=jnp.float32
         )
-        present = mask_ref[pl.ds(i, 1), :]
-        left = jax.nn.sigmoid(proj[0:quarter]) * proj[quarter : 2 * quarter] * present
-        right = jax.nn.sigmoid(proj[2 * quarter : 3 * quarter]) * proj[3 * quarter :] * present
-        z_ref[i] = jnp.concatenate([left, right], axis=0).astype(z_ref.dtype)
+        for i in range(block):
+            part = proj[:, i * 2 * cols : (i + 1) * 2 * cols]
+            present = mask_ref[pl.ds(first + i, 1), :]
+            left = jax.nn.sigmoid(part[0:quarter]) * part[quarter : 2 * quarter] * present
+            right = jax.nn.sigmoid(part[2 * quarter : 3 * quarter]) * part[3 * quarter :] * present
+            z_ref[first + i] = jnp.concatenate([left, right], axis=0).astype(z_ref.dtype)
         return carry
 
-    lax.fori_loop(0, rows, row, 0)
+    lax.fori_loop(0, rows // block, rows_of, 0)
 
 
 def body_fused(pair, mask, w_agate, w_aproj, w_bgate, w_bproj, w_gate, w_out, w_up, w_down, *, n_row, n_col):
@@ -160,12 +164,10 @@
     col_mask = lax.dynamic_slice_in_dim(present, lax.axis_index("col") * cols, cols, 0)
     lane_mask = row_mask[:, None] * jnp.concatenate([col_mask, col_mask])[None, :]
 
-    def paired(w):
-        return jnp.transpose(w.reshape(width, hid // 2, 2), (1, 2, 0)).reshape(hid // 2, 2 * width)
-
-    w2 = jnp.concatenate([paired(w) for w in (w_agate, w_aproj, w_bgate, w_bproj)], axis=0)
+    w2 = jnp.stack([w_agate, w_aproj, w_bgate, w_bproj]).reshape(4, width, hid // 2, 2)
+    w2 = jnp.transpose(w2, (0, 2, 3, 1)).reshape(2 * hid, 2 * width)
     z, gate = pl.pallas_call(
-        project_kernel,
+        functools.partial(project_kernel, block=8),
         out_shape=(
             jax.ShapeDtypeStruct((rows, hid, 2 * cols), jnp.bfloat16),
             jax.ShapeDtypeStruct((rows, cols, width), jnp.float32),

time: 87.8 us -> 78.4 us (0.89)
  Pallas kernels: 16.8 us -> 7.15 us
    pallas_call x1, Pallas kernels: 14.1 us -> 4.42 us  [body_fused(): pl.pallas_call(functools.partial(project_kernel, block=8), out_shape=(jax...]
    unnamed x12 -> x13, local copies, waits for them, and re-layouts: 3.49 us -> 4.17 us
where the time goes in v4:
time: 78.4 us; the launch traced here: 77 us
  blocking collectives  51.1 us (65%)
  local copies, waits for them, and re-layouts  11.8 us (15%)
  Pallas kernels  7.15 us (9%)
  matrix products  3.94 us (5%)
  other arithmetic  2.92 us (4%)
    all_to_all x1, blocking collectives, body_fused(): lax.all_to_all(edges, ('row', 'col'), split_axis=0, concat_axis=0, tiled=...  32.3 us
    all_to_all x1, blocking collectives, body_fused(): lax.all_to_all(mixed, ('row', 'col'), split_axis=0, concat_axis=0, tiled=...  18.8 us
    pallas_call x1, Pallas kernels, body_fused(): pl.pallas_call(functools.partial(project_kernel, block=8), out_shape=(jax...  4.42 us
    unnamed x13, local copies, waits for them, and re-layouts  4.17 us
    convert_element_type x2, local copies, waits for them, and re-layouts, body_fused(): mixed_rows = mixed.astype(jnp.float32).reshape(rows * cols, hid)  2.75 us
    pallas_call x1, Pallas kernels, body_fused(): pl.pallas_call(functools.partial(mix_kernel, n_col=n_col), out_shape=jax....  2.74 us
    reshape x1, local copies, waits for them, and re-layouts, body_fused(): z.reshape(rows, 2, n_dev, pairs, 2 * cols)  2.44 us
    reshape x1, local copies, waits for them, and re-layouts, body_fused(): mixed_rows = mixed.astype(jnp.float32).reshape(rows * cols, hid)  2.13 us

profile of v4, /device:TPU:0, one launch (start us, length us, event | category | flops | bytes accessed | tf_op | source)
XLA Modules:
  0.0 77.0 jit_solution(9354874300062389445)
XLA Ops:
  0.0 0.0 copy-start
  0.0 0.7 convert_element_type.25
  0.7 0.1 dynamic_slice.6
  0.8 0.1 dynamic_slice.7
  0.9 0.1 pad_maximum_fusion.1
  0.9 0.9 %copy.15 = bf16[128,128]{0,1:T(8,128)(2,1)S(1)} copy(bf16[128,128]{1,0:T(8,128)(2,1)} %param.12) | data formatting | bytes 65536 | tf_op args[2]
  1.8 0.9 %copy.16 = bf16[128,128]{0,1:T(8,128)(2,1)S(1)} copy(bf16[128,128]{1,0:T(8,128)(2,1)} %param.13) | data formatting | bytes 65536 | tf_op args[3]
  2.7 0.9 %copy.17 = bf16[128,128]{0,1:T(8,128)(2,1)S(1)} copy(bf16[128,128]{1,0:T(8,128)(2,1)} %param.14) | data formatting | bytes 65536 | tf_op args[4]
  3.6 0.9 %copy.18 = bf16[128,128]{0,1:T(8,128)(2,1)S(1)} copy(bf16[128,128]{1,0:T(8,128)(2,1)} %param.15) | data formatting | bytes 65536 | tf_op args[5]
  4.4 0.2 pad_maximum_fusion
  4.7 0.7 copy.34
  5.4 0.7 broadcast_multiply_fusion.1.mask_ref
  6.0 4.4 %shard_map.100 = (bf16[32,128,128]{2,1,0:T(8,128)(2,1)}, f32[32,64,128]{2,1,0:T(8,128)}) custom-call(bf16[32,64,128]{2,1,0:T(8,128)(2,1)} %pair_ref.1, f32[32,128]{1,0:T(8,128)} %broadcast_multiply_fusion.1.mask_ref, bf16[256,256]{1,0:T(8,128)(2,1)} %bitcast.40, bf16[128,128]{1,0:T(8,128)(2,1)} %wg_ref.1), custom_call_target="tpu_custom_call" | custom-call | tf_op jit(solution)/shard_map/pallas_call | solution.py:169
  10.5 2.4 %copy.33 = bf16[32,2,32,2,128]{4,0,3,1,2:T(8,128)(2,1)S(1)} copy(bf16[32,2,32,2,128]{4,3,2,1,0:T(2,128)(2,1)} %bitcast.38) | data formatting | bytes 2097152 | tf_op jit(solution)/shard_map/reshape | solution.py:176
  12.9 32.3 %all_to_all.10.edges_ref = bf16[32,2,2,32,128]{4,3,2,1,0:T(8,128)(2,1)} all-to-all(bf16[32,2,2,32,128]{4,3,2,1,0:T(8,128)(2,1)S(1)} %bitcast.35), channel_id=1, replica_groups=mesh['row'=8,'col'=4] {'row','col'}, dimensions={0} | all-to-all | bytes 2097152 | tf_op jit(solution)/shard_map/all_to_all | solution.py:177
  45.2 2.7 %shard_map.101 = bf16[32,2,32,128]{3,2,1,0:T(8,128)(2,1)} custom-call(bf16[32,2,2,32,128]{4,3,2,1,0:T(8,128)(2,1)} %all_to_all.10.edges_ref), custom_call_target="tpu_custom_call" | custom-call | tf_op jit(solution)/shard_map/pallas_call | solution.py:178
  47.9 18.8 %all_to_all.11 = bf16[32,2,32,128]{3,2,1,0:T(8,128)(2,1)S(1)} all-to-all(bf16[32,2,32,128]{3,2,1,0:T(8,128)(2,1)} %shard_map.101), channel_id=1, replica_groups=mesh['row'=8,'col'=4] {'row','col'}, dimensions={0} | all-to-all | bytes 1048576 | tf_op jit(solution)/shard_map/all_to_all | solution.py:182
  66.7 1.1 %reshape.88 = f32[32,2,32,2,64]{4,3,2,1,0:T(2,128)S(1)} reshape(bf16[32,2,32,128]{3,2,1,0:T(8,128)(2,1)S(1)} %all_to_all.11) | data formatting | bytes 1572864 | tf_op jit(solution)/shard_map/convert_element_type | solution.py:184
  67.9 0.2 fusion.9
  68.1 0.3 multiply_reduce_fusion
  68.5 0.1 div.15
  68.5 1.6 %copy.32 = f32[32,2,32,2,64]{4,2,3,1,0:T(8,128)} copy(f32[32,2,32,2,64]{4,3,2,1,0:T(2,128)S(1)} %reshape.88) | data formatting | bytes 2097152 | tf_op jit(solution)/shard_map/convert_element_type | solution.py:184
  70.1 0.0 copy-start.1
  70.1 0.0 copy-start.2
  70.2 0.1 rsqrt.20
  70.2 2.1 %reshape.84 = f32[2048,128]{0,1:T(8,128)S(1)} reshape(f32[32,64,32,2,2]{1,0,4,3,2:T(8,128)} %bitcast.34) | data formatting | bytes 2097152 | tf_op jit(solution)/shard_map/reshape | solution.py:184
  72.4 0.0 copy-done.1
  72.4 0.0 copy-done.2
  72.4 0.0 copy-start.3
  72.4 1.8 %fusion.10 = (f32[2048]{0:T(1024)S(1)}, f32[2048,128]{1,0:T(8,128)S(1)}) fusion(f32[2048,128]{1,0:T(8,128)} %bitcast.37, bf16[128,128]{1,0:T(8,128)(2,1)S(1)} %copy-done.2, f32[2048,128]{0,1:T(8,128)S(1)} %reshape.84, f32[2048]{0:T(1024)S(1)} %rsqrt.20, f32[2048]{0:T(1024)S(1)} %div.15, bf16[2048,128]{1,0:T(8,128)(2,1)S(1)} %bitcast.36), kind=kOutput, calls=%fused_computation.25 | convolution fusion | flops 68941824 | bytes 3727360 | tf_op jit(solution)/shard_map/dot_general | solution.py:42
  74.2 0.6 multiply_reduce_fusion.1
  74.9 0.0 copy-done
  74.9 0.0 copy-done.3
  74.9 2.1 %fusion.1 = bf16[2048,128]{1,0:T(8,128)(2,1)} fusion(f32[2048,128]{1,0:T(8,128)S(1)} %get-tuple-element.10, bf16[512,128]{1,0:T(8,128)(2,1)S(1)} %copy-done, bf16[128,512]{1,0:T(8,128)(2,1)S(1)} %copy-done.3, f32[2048]{0:T(1024)S(1)} %add_rsqrt_fusion.1, f32[2048]{0:T(1024)S(1)} %broadcast_multiply_fusion.2), kind=kOutput, calls=%fused_computation.4 | convolution fusion | flops 540278784 | bytes 1851392 | tf_op jit(solution)/shard_map/dot_general | solution.py:47
  (4 shorter events, 0.0 us)
Async XLA Ops:
  0.0 74.9 %copy-start = (bf16[512,128]{1,0:T(8,128)(2,1)S(1)}, bf16[512,128]{1,0:T(8,128)(2,1)}, u32[]{:S(2)}) copy-start(bf16[512,128]{1,0:T(8,128)(2,1)} %param.19) | copy-start | bytes 393220
  70.1 2.2 %copy-start.1 = (bf16[32,64,128]{2,1,0:T(8,128)(2,1)S(1)}, bf16[32,64,128]{2,1,0:T(8,128)(2,1)}, u32[]{:S(2)}) copy-start(bf16[32,64,128]{2,1,0:T(8,128)(2,1)} %pair_ref.1) | copy-start | bytes 1572868
  70.1 2.2 %copy-start.2 = (bf16[128,128]{1,0:T(8,128)(2,1)S(1)}, bf16[128,128]{1,0:T(8,128)(2,1)}, u32[]{:S(2)}) copy-start(bf16[128,128]{1,0:T(8,128)(2,1)} %param.17) | copy-start | bytes 98308
  72.4 2.5 %copy-start.3 = (bf16[128,512]{1,0:T(8,128)(2,1)S(1)}, bf16[128,512]{1,0:T(8,128)(2,1)}, u32[]{:S(2)}) copy-start(bf16[128,512]{1,0:T(8,128)(2,1)} %param.18) | copy-start | bytes 393220

commit v5 on v4

--- a/solution.py
+++ b/solution.py
@@ -124,9 +124,15 @@
     return result.astype(jnp.bfloat16).reshape(rows, cols, width)
 
 
-def project_kernel(pair_ref, mask_ref, w2_ref, wg_ref, z_ref, gate_ref, *, block):
+def project_kernel(pair_ref, mask_ref, wag_ref, wap_ref, wbg_ref, wbp_ref, wg_ref, z_ref, gate_ref, *, block):
     rows, cols, width = pair_ref.shape
-    quarter = w2_ref.shape[0] // 4
+    quarter = wag_ref.shape[1] // 2
+
+    def paired(w_ref):
+        turned = w_ref[...].astype(jnp.float32).T.astype(jnp.bfloat16)
+        return jnp.concatenate([turned[:quarter], turned[quarter:]], axis=1)
+
+    w2 = jnp.concatenate([paired(w) for w in (wag_ref, wap_ref, wbg_ref, wbp_ref)], axis=0)
 
     def rows_of(step, carry):
         first = pl.multiple_of(step * block, block)
@@ -141,7 +147,7 @@
         bottom = jnp.concatenate([zeros, normed], axis=1).reshape(block, cols, 2 * width)
         doubled = jnp.concatenate([top, bottom], axis=1).reshape(block * 2 * cols, 2 * width)
         proj = lax.dot_general(
-            w2_ref[...], doubled, (((1,), (1,)), ((), ())), preferred_element_type=jnp.float32
+            w2, doubled, (((1,), (1,)), ((), ())), preferred_element_type=jnp.float32
         )
         for i in range(block):
             part = proj[:, i * 2 * cols : (i + 1) * 2 * cols]
@@ -164,15 +170,13 @@
     col_mask = lax.dynamic_slice_in_dim(present, lax.axis_index("col") * cols, cols, 0)
     lane_mask = row_mask[:, None] * jnp.concatenate([col_mask, col_mask])[None, :]
 
-    w2 = jnp.stack([w_agate, w_aproj, w_bgate, w_bproj]).reshape(4, width, hid // 2, 2)
-    w2 = jnp.transpose(w2, (0, 2, 3, 1)).reshape(2 * hid, 2 * width)
     z, gate = pl.pallas_call(
         functools.partial(project_kernel, block=8),
         out_shape=(
             jax.ShapeDtypeStruct((rows, hid, 2 * cols), jnp.bfloat16),
             jax.ShapeDtypeStruct((rows, cols, width), jnp.float32),
         ),
-    )(pair, lane_mask, w2, w_gate)
+    )(pair, lane_mask, w_agate, w_aproj, w_bgate, w_bproj, w_gate)
     edges = jnp.transpose(z.reshape(rows, 2, n_dev, pairs, 2 * cols), (2, 1, 3, 0, 4))
     edges = lax.all_to_all(edges, ("row", "col"), split_axis=0, concat_axis=0, tiled=True)
     mixed = pl.pallas_call(
@@ -180,7 +184,7 @@
         out_shape=jax.ShapeDtypeStruct((n_dev, pairs, rows, 2 * cols), jnp.bfloat16),
     )(edges)
     mixed = lax.all_to_all(mixed, ("row", "col"), split_axis=0, concat_axis=0, tiled=True)
-    mixed = jnp.transpose(mixed.reshape(n_dev, pairs, rows, 2, cols), (2, 4, 0, 1, 3))
+    mixed = jnp.transpose(mixed.reshape(n_dev, pairs, rows, 2, cols), (2, 4, 3, 0, 1))
     mixed_rows = mixed.astype(jnp.float32).reshape(rows * cols, hid)
     pair_flat = pair.astype(jnp.float32).reshape(rows * cols, width)
     result = transition(pair_flat, gate.reshape(rows * cols, width), mixed_rows, w_out, w_up, w_down)

time: 78.4 us -> 73.9 us (0.943)
  local copies, waits for them, and re-layouts: 11.8 us -> 7.67 us
    unnamed x13 -> x8, local copies, waits for them, and re-layouts: 4.17 us -> 0.02 us
where the time goes in v5:
time: 73.9 us; the launch traced here: 72.8 us
  blocking collectives  51.1 us (69%)
  local copies, waits for them, and re-layouts  7.67 us (10%)
  Pallas kernels  7.29 us (10%)
  matrix products  3.94 us (5%)
  other arithmetic  2.69 us (4%)
    all_to_all x1, blocking collectives, body_fused(): lax.all_to_all(edges, ('row', 'col'), split_axis=0, concat_axis=0, tiled=...  32.3 us
    all_to_all x1, blocking collectives, body_fused(): lax.all_to_all(mixed, ('row', 'col'), split_axis=0, concat_axis=0, tiled=...  18.8 us
    pallas_call x1, Pallas kernels, body_fused(): pl.pallas_call(functools.partial(project_kernel, block=8), out_shape=(jax...  4.55 us
    convert_element_type x2, local copies, waits for them, and re-layouts, body_fused(): mixed_rows = mixed.astype(jnp.float32).reshape(rows * cols, hid)  2.78 us
    pallas_call x1, Pallas kernels, body_fused(): pl.pallas_call(functools.partial(mix_kernel, n_col=n_col), out_shape=jax....  2.74 us
    reshape x1, local copies, waits for them, and re-layouts, body_fused(): z.reshape(rows, 2, n_dev, pairs, 2 * cols)  2.44 us
    reshape x1, local copies, waits for them, and re-layouts, body_fused(): mixed_rows = mixed.astype(jnp.float32).reshape(rows * cols, hid)  2.13 us
    dot_general x1, matrix products, transition(): jnp.dot(trans_hidden, w_down, preferred_element_type=jnp.float32)  2.1 us

profile of v5, /device:TPU:0, one launch (start us, length us, event | category | flops | bytes accessed | tf_op | source)
XLA Modules:
  0.0 72.8 jit_solution(3190106489795247262)
XLA Ops:
  0.0 0.0 copy-start
  0.0 0.7 convert_element_type.25
  0.7 0.1 dynamic_slice.6
  0.8 0.1 dynamic_slice.7
  0.9 0.1 pad_maximum_fusion
  0.9 0.7 broadcast_multiply_fusion.1.mask_ref
  1.6 4.5 %shard_map.100 = (bf16[32,128,128]{2,1,0:T(8,128)(2,1)}, f32[32,64,128]{2,1,0:T(8,128)}) custom-call(bf16[32,64,128]{2,1,0:T(8,128)(2,1)} %pair_ref.1, f32[32,128]{1,0:T(8,128)} %broadcast_multiply_fusion.1.mask_ref, bf16[128,128]{1,0:T(8,128)(2,1)} %wag_ref.1, bf16[128,128]{1,0:T(8,128)(2,1)} %wap_ref.1, bf16[128,128]{1,0:T(8,128)(2,1)} %wbg_ref.1, ...), custom_call_target="tpu_custom_call" | custom-call | tf_op jit(solution)/shard_map/pallas_call | solution.py:173
  6.2 2.4 %copy.23 = bf16[32,2,32,2,128]{4,0,3,1,2:T(8,128)(2,1)S(1)} copy(bf16[32,2,32,2,128]{4,3,2,1,0:T(2,128)(2,1)} %bitcast.28) | data formatting | bytes 2097152 | tf_op jit(solution)/shard_map/reshape | solution.py:180
  8.6 32.3 %all_to_all.10.edges_ref = bf16[32,2,2,32,128]{4,3,2,1,0:T(8,128)(2,1)} all-to-all(bf16[32,2,2,32,128]{4,3,2,1,0:T(8,128)(2,1)S(1)} %bitcast.25), channel_id=1, replica_groups=mesh['row'=8,'col'=4] {'row','col'}, dimensions={0} | all-to-all | bytes 2097152 | tf_op jit(solution)/shard_map/all_to_all | solution.py:181
  40.9 2.7 %shard_map.101 = bf16[32,2,32,128]{3,2,1,0:T(8,128)(2,1)} custom-call(bf16[32,2,2,32,128]{4,3,2,1,0:T(8,128)(2,1)} %all_to_all.10.edges_ref), custom_call_target="tpu_custom_call" | custom-call | tf_op jit(solution)/shard_map/pallas_call | solution.py:182
  43.6 18.8 %all_to_all.11 = bf16[32,2,32,128]{3,2,1,0:T(8,128)(2,1)S(1)} all-to-all(bf16[32,2,32,128]{3,2,1,0:T(8,128)(2,1)} %shard_map.101), channel_id=1, replica_groups=mesh['row'=8,'col'=4] {'row','col'}, dimensions={0} | all-to-all | bytes 1048576 | tf_op jit(solution)/shard_map/all_to_all | solution.py:186
  62.5 1.1 %reshape.75 = f32[32,2,32,2,64]{4,3,2,1,0:T(2,128)S(1)} reshape(bf16[32,2,32,128]{3,2,1,0:T(8,128)(2,1)S(1)} %all_to_all.11) | data formatting | bytes 1572864 | tf_op jit(solution)/shard_map/convert_element_type | solution.py:188
  63.6 0.2 fusion.9
  63.8 0.3 multiply_reduce_fusion
  64.2 0.1 div.15
  64.2 1.6 %copy.22 = f32[32,2,32,2,64]{4,2,1,0,3:T(8,128)} copy(f32[32,2,32,2,64]{4,3,2,1,0:T(2,128)S(1)} %reshape.75) | data formatting | bytes 2097152 | tf_op jit(solution)/shard_map/convert_element_type | solution.py:188
  65.9 0.0 copy-start.1
  65.9 0.0 copy-start.2
  65.9 0.1 rsqrt.20
  66.0 2.1 %reshape.71 = f32[2048,128]{0,1:T(8,128)S(1)} reshape(f32[32,64,2,32,2]{1,0,4,3,2:T(8,128)} %bitcast.24) | data formatting | bytes 2097152 | tf_op jit(solution)/shard_map/reshape | solution.py:188
  68.1 0.0 copy-done.1
  68.1 0.0 copy-done.2
  68.1 0.0 copy-start.3
  68.1 1.8 %fusion.10 = (f32[2048]{0:T(1024)S(1)}, f32[2048,128]{1,0:T(8,128)S(1)}) fusion(f32[2048,128]{1,0:T(8,128)} %bitcast.27, bf16[128,128]{1,0:T(8,128)(2,1)S(1)} %copy-done.2, f32[2048,128]{0,1:T(8,128)S(1)} %reshape.71, f32[2048]{0:T(1024)S(1)} %rsqrt.20, f32[2048]{0:T(1024)S(1)} %div.15, bf16[2048,128]{1,0:T(8,128)(2,1)S(1)} %bitcast.26), kind=kOutput, calls=%fused_computation.23 | convolution fusion | flops 68941824 | bytes 3727360 | tf_op jit(solution)/shard_map/dot_general | solution.py:42
  70.0 0.6 multiply_reduce_fusion.1
  70.6 0.0 copy-done
  70.7 0.0 copy-done.3
  70.7 2.1 %fusion.1 = bf16[2048,128]{1,0:T(8,128)(2,1)} fusion(f32[2048,128]{1,0:T(8,128)S(1)} %get-tuple-element.10, bf16[512,128]{1,0:T(8,128)(2,1)S(1)} %copy-done, bf16[128,512]{1,0:T(8,128)(2,1)S(1)} %copy-done.3, f32[2048]{0:T(1024)S(1)} %add_rsqrt_fusion.1, f32[2048]{0:T(1024)S(1)} %broadcast_multiply_fusion.2), kind=kOutput, calls=%fused_computation.4 | convolution fusion | flops 540278784 | bytes 1851392 | tf_op jit(solution)/shard_map/dot_general | solution.py:47
  (4 shorter events, 0.0 us)
Async XLA Ops:
  0.0 70.6 %copy-start = (bf16[512,128]{1,0:T(8,128)(2,1)S(1)}, bf16[512,128]{1,0:T(8,128)(2,1)}, u32[]{:S(2)}) copy-start(bf16[512,128]{1,0:T(8,128)(2,1)} %param.19) | copy-start | bytes 393220
  65.9 2.2 %copy-start.1 = (bf16[32,64,128]{2,1,0:T(8,128)(2,1)S(1)}, bf16[32,64,128]{2,1,0:T(8,128)(2,1)}, u32[]{:S(2)}) copy-start(bf16[32,64,128]{2,1,0:T(8,128)(2,1)} %pair_ref.1) | copy-start | bytes 1572868
  65.9 2.2 %copy-start.2 = (bf16[128,128]{1,0:T(8,128)(2,1)S(1)}, bf16[128,128]{1,0:T(8,128)(2,1)}, u32[]{:S(2)}) copy-start(bf16[128,128]{1,0:T(8,128)(2,1)} %param.17) | copy-start | bytes 98308
  68.1 2.5 %copy-start.3 = (bf16[128,512]{1,0:T(8,128)(2,1)S(1)}, bf16[128,512]{1,0:T(8,128)(2,1)}, u32[]{:S(2)}) copy-start(bf16[128,512]{1,0:T(8,128)(2,1)} %param.18) | copy-start | bytes 393220

commit v6 on v5

--- a/solution.py
+++ b/solution.py
@@ -160,6 +160,30 @@
     lax.fori_loop(0, rows // block, rows_of, 0)
 
 
+def transition_kernel(mixed_ref, pair_ref, gate_ref, wo_ref, wu_ref, wd_ref, out_ref, *, block):
+    rows, cols, width = pair_ref.shape
+
+    def norm(values):
+        center = values - jnp.mean(values, axis=-1, keepdims=True)
+        spread = jnp.mean(center * center, axis=-1, keepdims=True)
+        return center * lax.rsqrt(spread + 1e-05)
+
+    def rows_of(step, carry):
+        first = pl.multiple_of(step * block, block)
+        mixed = mixed_ref[pl.ds(first, block)].astype(jnp.float32).reshape(block * cols, -1)
+        pair = pair_ref[pl.ds(first, block)].astype(jnp.float32).reshape(block * cols, width)
+        gate = gate_ref[pl.ds(first, block)].reshape(block * cols, width)
+        mixed_normed = norm(mixed).astype(jnp.bfloat16)
+        middle = pair + gate * jnp.dot(mixed_normed, wo_ref[...], preferred_element_type=jnp.float32)
+        trans_in = norm(middle).astype(jnp.bfloat16)
+        hidden = jnp.maximum(jnp.dot(trans_in, wu_ref[...], preferred_element_type=jnp.float32), 0.0)
+        result = middle + jnp.dot(hidden.astype(jnp.bfloat16), wd_ref[...], preferred_element_type=jnp.float32)
+        out_ref[pl.ds(first, block)] = result.astype(out_ref.dtype).reshape(block, cols, width)
+        return carry
+
+    lax.fori_loop(0, rows // block, rows_of, 0)
+
+
 def body_fused(pair, mask, w_agate, w_aproj, w_bgate, w_bproj, w_gate, w_out, w_up, w_down, *, n_row, n_col):
     rows, cols, width = pair.shape
     n_dev = n_row * n_col
@@ -184,11 +208,11 @@
         out_shape=jax.ShapeDtypeStruct((n_dev, pairs, rows, 2 * cols), jnp.bfloat16),
     )(edges)
     mixed = lax.all_to_all(mixed, ("row", "col"), split_axis=0, concat_axis=0, tiled=True)
-    mixed = jnp.transpose(mixed.reshape(n_dev, pairs, rows, 2, cols), (2, 4, 3, 0, 1))
-    mixed_rows = mixed.astype(jnp.float32).reshape(rows * cols, hid)
-    pair_flat = pair.astype(jnp.float32).reshape(rows * cols, width)
-    result = transition(pair_flat, gate.reshape(rows * cols, width), mixed_rows, w_out, w_up, w_down)
-    return result.astype(jnp.bfloat16).reshape(rows, cols, width)
+    mixed = jnp.transpose(mixed.reshape(n_dev, pairs, rows, 2, cols), (2, 4, 3, 0, 1)).reshape(rows, cols, hid)
+    return pl.pallas_call(
+        functools.partial(transition_kernel, block=8),
+        out_shape=jax.ShapeDtypeStruct((rows, cols, width), jnp.bfloat16),
+    )(mixed, pair, gate, w_out, w_up, w_down)
 
 
 def body_rows(pair, mask, w_agate, w_aproj, w_bgate, w_bproj, w_gate, w_out, w_up, w_down):

time: 73.9 us -> 72.7 us (0.984)
  Pallas kernels: 7.29 us -> 13.9 us
  matrix products: 3.94 us -> 0 us
  other arithmetic: 2.69 us -> 0.76 us
  local copies, waits for them, and re-layouts: 7.67 us -> 5.83 us
    pallas_call x0 -> x1, Pallas kernels: none -> 6.64 us  [body_fused(): pl.pallas_call(functools.partial(transition_kernel, block=8), out_shape=j...]
    dot_general x2 -> x0, matrix products: 3.94 us -> none  [the longest x1 2.1 us: transition(): jnp.dot(trans_hidden, w_down, preferred_element_type=jnp.float32)]
    convert_element_type x2 -> x0, local copies, waits for them, and re-layouts: 2.78 us -> none  [body_fused(): mixed_rows = mixed.astype(jnp.float32).reshape(rows * cols, hid)]
    reduce_sum x3 -> x0, other arithmetic: 1.19 us -> none  [the longest x2 0.96 us: layer_norm(): spread = jnp.mean(center * center, axis=-1, keepdims=True)]
    reshape x1 -> x3, local copies, waits for them, and re-layouts: 2.13 us -> 2.55 us  [the longest x1 1.9 us: body_fused(): jnp.transpose(mixed.reshape(n_dev, pairs, rows, 2, cols), (2, 4, 3, 0, 1))]
where the time goes in v6:
time: 72.7 us; the launch traced here: 71.6 us
  blocking collectives  51.1 us (70%)
  Pallas kernels  13.9 us (19%)
  local copies, waits for them, and re-layouts  5.83 us (8%)
  other arithmetic  0.76 us (1%)
    all_to_all x1, blocking collectives, body_fused(): lax.all_to_all(edges, ('row', 'col'), split_axis=0, concat_axis=0, tiled=...  32.3 us
    all_to_all x1, blocking collectives, body_fused(): lax.all_to_all(mixed, ('row', 'col'), split_axis=0, concat_axis=0, tiled=...  18.8 us
    pallas_call x1, Pallas kernels, body_fused(): pl.pallas_call(functools.partial(transition_kernel, block=8), out_shape=j...  6.64 us
    pallas_call x1, Pallas kernels, body_fused(): pl.pallas_call(functools.partial(project_kernel, block=8), out_shape=(jax...  4.56 us
    pallas_call x1, Pallas kernels, body_fused(): pl.pallas_call(functools.partial(mix_kernel, n_col=n_col), out_shape=jax....  2.73 us
    reshape x1, local copies, waits for them, and re-layouts, body_fused(): z.reshape(rows, 2, n_dev, pairs, 2 * cols)  2.44 us
    reshape x1, local copies, waits for them, and re-layouts, body_fused(): jnp.transpose(mixed.reshape(n_dev, pairs, rows, 2, cols), (2, 4, 3, 0, 1))  1.9 us

profile of v6, /device:TPU:0, one launch (start us, length us, event | category | flops | bytes accessed | tf_op | source)
XLA Modules:
  0.0 71.6 jit_solution(8108119117534748813)
XLA Ops:
  0.0 0.0 copy-start
  0.0 0.7 copy-done
  0.7 0.1 dynamic_slice.7
  0.8 0.1 dynamic_slice.6
  0.8 0.1 pad_maximum_fusion
  0.9 0.7 broadcast_multiply_fusion.mask_ref
  1.6 4.6 %shard_map.100 = (bf16[32,128,128]{2,1,0:T(8,128)(2,1)}, f32[32,64,128]{2,1,0:T(8,128)}) custom-call(bf16[32,64,128]{2,1,0:T(8,128)(2,1)} %pair_ref.3, f32[32,128]{1,0:T(8,128)} %broadcast_multiply_fusion.mask_ref, bf16[128,128]{1,0:T(8,128)(2,1)} %wag_ref.1, bf16[128,128]{1,0:T(8,128)(2,1)} %wap_ref.1, bf16[128,128]{1,0:T(8,128)(2,1)} %wbg_ref.1, ...), custom_call_target="tpu_custom_call" | custom-call | tf_op jit(solution)/shard_map/pallas_call | solution.py:197
  6.1 2.4 %copy.19 = bf16[32,2,32,2,128]{4,0,3,1,2:T(8,128)(2,1)S(1)} copy(bf16[32,2,32,2,128]{4,3,2,1,0:T(2,128)(2,1)} %bitcast.11) | data formatting | bytes 2097152 | tf_op jit(solution)/shard_map/reshape | solution.py:204
  8.6 32.3 %all_to_all.10.edges_ref = bf16[32,2,2,32,128]{4,3,2,1,0:T(8,128)(2,1)} all-to-all(bf16[32,2,2,32,128]{4,3,2,1,0:T(8,128)(2,1)S(1)} %bitcast.9), channel_id=1, replica_groups=mesh['row'=8,'col'=4] {'row','col'}, dimensions={0} | all-to-all | bytes 2097152 | tf_op jit(solution)/shard_map/all_to_all | solution.py:205
  40.9 2.7 %shard_map.101 = bf16[32,2,32,128]{3,2,1,0:T(8,128)(2,1)} custom-call(bf16[32,2,2,32,128]{4,3,2,1,0:T(8,128)(2,1)} %all_to_all.10.edges_ref), custom_call_target="tpu_custom_call" | custom-call | tf_op jit(solution)/shard_map/pallas_call | solution.py:206
  43.6 18.8 %all_to_all.11 = bf16[32,2,32,128]{3,2,1,0:T(8,128)(2,1)S(1)} all-to-all(bf16[32,2,32,128]{3,2,1,0:T(8,128)(2,1)} %shard_map.101), channel_id=1, replica_groups=mesh['row'=8,'col'=4] {'row','col'}, dimensions={0} | all-to-all | bytes 1048576 | tf_op jit(solution)/shard_map/all_to_all | solution.py:210
  62.4 0.4 reshape.12
  62.8 0.3 copy.14
  63.1 1.9 %copy.15.mixed_ref = bf16[32,64,128]{2,1,0:T(8,128)(2,1)} copy(bf16[32,64,128]{1,0,2:T(8,128)(2,1)S(1)} %bitcast.10) | data formatting | bytes 1048576 | tf_op jit(solution)/shard_map/reshape | solution.py:211
  65.0 6.6 %shard_map.102 = bf16[32,64,128]{2,1,0:T(8,128)(2,1)} custom-call(bf16[32,64,128]{2,1,0:T(8,128)(2,1)} %copy.15.mixed_ref, bf16[32,64,128]{2,1,0:T(8,128)(2,1)} %pair_ref.3, f32[32,64,128]{2,1,0:T(8,128)} %get-tuple-element.8.gate_ref, bf16[128,128]{1,0:T(8,128)(2,1)} %wo_ref.1, bf16[128,512]{1,0:T(8,128)(2,1)} %wu_ref.1, bf16[512,128]{1,0:T(8,128)(2,1)} %wd_ref.1), custom_call_target="tpu_custom_call" | custom-call | tf_op jit(solution)/shard_map/pallas_call | solution.py:212
  (1 shorter events, 0.0 us)
Async XLA Ops:
  0.0 0.7 copy-start

commit v7 on v6

--- a/solution.py
+++ b/solution.py
@@ -195,7 +195,7 @@
     lane_mask = row_mask[:, None] * jnp.concatenate([col_mask, col_mask])[None, :]
 
     z, gate = pl.pallas_call(
-        functools.partial(project_kernel, block=8),
+        functools.partial(project_kernel, block=rows),
         out_shape=(
             jax.ShapeDtypeStruct((rows, hid, 2 * cols), jnp.bfloat16),
             jax.ShapeDtypeStruct((rows, cols, width), jnp.float32),
@@ -210,7 +210,7 @@
     mixed = lax.all_to_all(mixed, ("row", "col"), split_axis=0, concat_axis=0, tiled=True)
     mixed = jnp.transpose(mixed.reshape(n_dev, pairs, rows, 2, cols), (2, 4, 3, 0, 1)).reshape(rows, cols, hid)
     return pl.pallas_call(
-        functools.partial(transition_kernel, block=8),
+        functools.partial(transition_kernel, block=rows),
         out_shape=jax.ShapeDtypeStruct((rows, cols, width), jnp.bfloat16),
     )(mixed, pair, gate, w_out, w_up, w_down)
 

time: 72.7 us -> 69.9 us (0.961)
  Pallas kernels: 13.9 us -> 11.1 us
    pallas_call x2, Pallas kernels: 11.2 us -> 8.36 us  [the longest x1 4.83 us: body_fused(): pl.pallas_call(functools.partial(transition_kernel, block=rows), out_shap...]
where the time goes in v7:
time: 69.9 us; the launch traced here: 68.8 us
  blocking collectives  51.1 us (73%)
  Pallas kernels  11.1 us (16%)
  local copies, waits for them, and re-layouts  5.83 us (8%)
  other arithmetic  0.76 us (1%)
    all_to_all x1, blocking collectives, body_fused(): lax.all_to_all(edges, ('row', 'col'), split_axis=0, concat_axis=0, tiled=...  32.3 us
    all_to_all x1, blocking collectives, body_fused(): lax.all_to_all(mixed, ('row', 'col'), split_axis=0, concat_axis=0, tiled=...  18.8 us
    pallas_call x1, Pallas kernels, body_fused(): pl.pallas_call(functools.partial(transition_kernel, block=rows), out_shap...  4.83 us
    pallas_call x1, Pallas kernels, body_fused(): pl.pallas_call(functools.partial(project_kernel, block=rows), out_shape=(...  3.53 us
    pallas_call x1, Pallas kernels, body_fused(): pl.pallas_call(functools.partial(mix_kernel, n_col=n_col), out_shape=jax....  2.73 us
    reshape x1, local copies, waits for them, and re-layouts, body_fused(): z.reshape(rows, 2, n_dev, pairs, 2 * cols)  2.44 us
    reshape x1, local copies, waits for them, and re-layouts, body_fused(): jnp.transpose(mixed.reshape(n_dev, pairs, rows, 2, cols), (2, 4, 3, 0, 1))  1.9 us

profile of v7, /device:TPU:0, one launch (start us, length us, event | category | flops | bytes accessed | tf_op | source)
XLA Modules:
  0.0 68.8 jit_solution(9442281444082940383)
XLA Ops:
  0.0 0.0 copy-start
  0.0 0.7 copy-done
  0.7 0.1 dynamic_slice.7
  0.8 0.1 dynamic_slice.6
  0.8 0.1 pad_maximum_fusion
  0.9 0.7 broadcast_multiply_fusion.mask_ref
  1.6 3.5 %shard_map.100 = (bf16[32,128,128]{2,1,0:T(8,128)(2,1)}, f32[32,64,128]{2,1,0:T(8,128)}) custom-call(bf16[32,64,128]{2,1,0:T(8,128)(2,1)} %pair_ref.3, f32[32,128]{1,0:T(8,128)} %broadcast_multiply_fusion.mask_ref, bf16[128,128]{1,0:T(8,128)(2,1)} %wag_ref.1, bf16[128,128]{1,0:T(8,128)(2,1)} %wap_ref.1, bf16[128,128]{1,0:T(8,128)(2,1)} %wbg_ref.1, ...), custom_call_target="tpu_custom_call" | custom-call | tf_op jit(solution)/shard_map/pallas_call | solution.py:197
  5.1 2.4 %copy.19 = bf16[32,2,32,2,128]{4,0,3,1,2:T(8,128)(2,1)S(1)} copy(bf16[32,2,32,2,128]{4,3,2,1,0:T(2,128)(2,1)} %bitcast.11) | data formatting | bytes 2097152 | tf_op jit(solution)/shard_map/reshape | solution.py:204
  7.6 32.3 %all_to_all.10.edges_ref = bf16[32,2,2,32,128]{4,3,2,1,0:T(8,128)(2,1)} all-to-all(bf16[32,2,2,32,128]{4,3,2,1,0:T(8,128)(2,1)S(1)} %bitcast.9), channel_id=1, replica_groups=mesh['row'=8,'col'=4] {'row','col'}, dimensions={0} | all-to-all | bytes 2097152 | tf_op jit(solution)/shard_map/all_to_all | solution.py:205
  39.8 2.7 %shard_map.101 = bf16[32,2,32,128]{3,2,1,0:T(8,128)(2,1)} custom-call(bf16[32,2,2,32,128]{4,3,2,1,0:T(8,128)(2,1)} %all_to_all.10.edges_ref), custom_call_target="tpu_custom_call" | custom-call | tf_op jit(solution)/shard_map/pallas_call | solution.py:206
  42.6 18.8 %all_to_all.11 = bf16[32,2,32,128]{3,2,1,0:T(8,128)(2,1)S(1)} all-to-all(bf16[32,2,32,128]{3,2,1,0:T(8,128)(2,1)} %shard_map.101), channel_id=1, replica_groups=mesh['row'=8,'col'=4] {'row','col'}, dimensions={0} | all-to-all | bytes 1048576 | tf_op jit(solution)/shard_map/all_to_all | solution.py:210
  61.4 0.4 reshape.12
  61.8 0.3 copy.14
  62.1 1.9 %copy.15.mixed_ref = bf16[32,64,128]{2,1,0:T(8,128)(2,1)} copy(bf16[32,64,128]{1,0,2:T(8,128)(2,1)S(1)} %bitcast.10) | data formatting | bytes 1048576 | tf_op jit(solution)/shard_map/reshape | solution.py:211
  64.0 4.8 %shard_map.102 = bf16[32,64,128]{2,1,0:T(8,128)(2,1)} custom-call(bf16[32,64,128]{2,1,0:T(8,128)(2,1)} %copy.15.mixed_ref, bf16[32,64,128]{2,1,0:T(8,128)(2,1)} %pair_ref.3, f32[32,64,128]{2,1,0:T(8,128)} %get-tuple-element.8.gate_ref, bf16[128,128]{1,0:T(8,128)(2,1)} %wo_ref.1, bf16[128,512]{1,0:T(8,128)(2,1)} %wu_ref.1, bf16[512,128]{1,0:T(8,128)(2,1)} %wd_ref.1), custom_call_target="tpu_custom_call" | custom-call | tf_op jit(solution)/shard_map/pallas_call | solution.py:212
  (1 shorter events, 0.0 us)
Async XLA Ops:
  0.0 0.7 copy-start

commit v8 on v7

--- a/solution.py
+++ b/solution.py
@@ -4,6 +4,7 @@
 import jax.numpy as jnp
 from jax import lax
 from jax.experimental import pallas as pl
+from jax.experimental.pallas import tpu as pltpu
 from jax.sharding import PartitionSpec as P
 
 
@@ -124,7 +125,7 @@
     return result.astype(jnp.bfloat16).reshape(rows, cols, width)
 
 
-def project_kernel(pair_ref, mask_ref, wag_ref, wap_ref, wbg_ref, wbp_ref, wg_ref, z_ref, gate_ref, *, block):
+def project_kernel(mask_ref, pair_ref, wag_ref, wap_ref, wbg_ref, wbp_ref, wg_ref, z_ref, gate_ref, *, block):
     rows, cols, width = pair_ref.shape
     quarter = wag_ref.shape[1] // 2
 
@@ -133,6 +134,12 @@
         return jnp.concatenate([turned[:quarter], turned[quarter:]], axis=1)
 
     w2 = jnp.concatenate([paired(w) for w in (wag_ref, wap_ref, wbg_ref, wbp_ref)], axis=0)
+    row_start = lax.axis_index("row") * rows
+    col_start = lax.axis_index("col") * cols
+    lane = lax.broadcasted_iota(jnp.int32, (1, 2 * cols), 1) % cols
+    col_mask = jnp.zeros((1, 2 * cols), jnp.float32)
+    for k in range(cols):
+        col_mask = jnp.where(lane == k, mask_ref[col_start + k].astype(jnp.float32), col_mask)
 
     def rows_of(step, carry):
         first = pl.multiple_of(step * block, block)
@@ -151,7 +158,7 @@
         )
         for i in range(block):
             part = proj[:, i * 2 * cols : (i + 1) * 2 * cols]
-            present = mask_ref[pl.ds(first + i, 1), :]
+            present = col_mask * mask_ref[row_start + first + i].astype(jnp.float32)
             left = jax.nn.sigmoid(part[0:quarter]) * part[quarter : 2 * quarter] * present
             right = jax.nn.sigmoid(part[2 * quarter : 3 * quarter]) * part[3 * quarter :] * present
             z_ref[first + i] = jnp.concatenate([left, right], axis=0).astype(z_ref.dtype)
@@ -189,10 +196,6 @@
     n_dev = n_row * n_col
     hid = w_agate.shape[1]
     pairs = hid // n_dev // 2
-    present = mask.astype(jnp.float32)
-    row_mask = lax.dynamic_slice_in_dim(present, lax.axis_index("row") * rows, rows, 0)
-    col_mask = lax.dynamic_slice_in_dim(present, lax.axis_index("col") * cols, cols, 0)
-    lane_mask = row_mask[:, None] * jnp.concatenate([col_mask, col_mask])[None, :]
 
     z, gate = pl.pallas_call(
         functools.partial(project_kernel, block=rows),
@@ -200,7 +203,8 @@
             jax.ShapeDtypeStruct((rows, hid, 2 * cols), jnp.bfloat16),
             jax.ShapeDtypeStruct((rows, cols, width), jnp.float32),
         ),
-    )(pair, lane_mask, w_agate, w_aproj, w_bgate, w_bproj, w_gate)
+        in_specs=[pl.BlockSpec(memory_space=pltpu.SMEM)] + [pl.BlockSpec(memory_space=pltpu.VMEM)] * 6,
+    )(mask, pair, w_agate, w_aproj, w_bgate, w_bproj, w_gate)
     edges = jnp.transpose(z.reshape(rows, 2, n_dev, pairs, 2 * cols), (2, 1, 3, 0, 4))
     edges = lax.all_to_all(edges, ("row", "col"), split_axis=0, concat_axis=0, tiled=True)
     mixed = pl.pallas_call(

time: 69.9 us -> 68.3 us (0.977)
  local copies, waits for them, and re-layouts: 5.83 us -> 5.01 us
  other arithmetic: 0.76 us -> 0 us
where the time goes in v8:
time: 68.3 us; the launch traced here: 67.2 us
  blocking collectives  51.1 us (75%)
  Pallas kernels  11.1 us (16%)
  local copies, waits for them, and re-layouts  5.01 us (7%)
    all_to_all x1, blocking collectives, body_fused(): lax.all_to_all(edges, ('row', 'col'), split_axis=0, concat_axis=0, tiled=...  32.3 us
    all_to_all x1, blocking collectives, body_fused(): lax.all_to_all(mixed, ('row', 'col'), split_axis=0, concat_axis=0, tiled=...  18.8 us
    pallas_call x1, Pallas kernels, body_fused(): pl.pallas_call(functools.partial(transition_kernel, block=rows), out_shap...  4.83 us
    pallas_call x1, Pallas kernels, body_fused(): pl.pallas_call(functools.partial(project_kernel, block=rows), out_shape=(...  3.53 us
    pallas_call x1, Pallas kernels, body_fused(): pl.pallas_call(functools.partial(mix_kernel, n_col=n_col), out_shape=jax....  2.74 us
    reshape x1, local copies, waits for them, and re-layouts, body_fused(): z.reshape(rows, 2, n_dev, pairs, 2 * cols)  2.44 us
    reshape x1, local copies, waits for them, and re-layouts, body_fused(): jnp.transpose(mixed.reshape(n_dev, pairs, rows, 2, cols), (2, 4, 3, 0, 1))  1.91 us

profile of v8, /device:TPU:0, one launch (start us, length us, event | category | flops | bytes accessed | tf_op | source)
XLA Modules:
  0.0 67.2 jit_solution(17106115333290010983)
XLA Ops:
  0.0 3.5 %shard_map.100 = (bf16[32,128,128]{2,1,0:T(8,128)(2,1)}, f32[32,64,128]{2,1,0:T(8,128)}) custom-call(s32[256]{0:T(256)} %mask_ref.1, bf16[32,64,128]{2,1,0:T(8,128)(2,1)} %pair_ref.3, bf16[128,128]{1,0:T(8,128)(2,1)} %wag_ref.1, bf16[128,128]{1,0:T(8,128)(2,1)} %wap_ref.1, bf16[128,128]{1,0:T(8,128)(2,1)} %wbg_ref.1, bf16[128,128]{1,0:T(8,128)(2,1)} %wbp_ref.1, ...), custom_call_target="tpu_custom_call" | custom-call | tf_op jit(solution)/shard_map/pallas_call | solution.py:200
  3.5 2.4 %copy.19 = bf16[32,2,32,2,128]{4,0,3,1,2:T(8,128)(2,1)S(1)} copy(bf16[32,2,32,2,128]{4,3,2,1,0:T(2,128)(2,1)} %bitcast.11) | data formatting | bytes 2097152 | tf_op jit(solution)/shard_map/reshape | solution.py:208
  6.0 32.3 %all_to_all.10.edges_ref = bf16[32,2,2,32,128]{4,3,2,1,0:T(8,128)(2,1)} all-to-all(bf16[32,2,2,32,128]{4,3,2,1,0:T(8,128)(2,1)S(1)} %bitcast.9), channel_id=1, replica_groups=mesh['row'=8,'col'=4] {'row','col'}, dimensions={0} | all-to-all | bytes 2097152 | tf_op jit(solution)/shard_map/all_to_all | solution.py:209
  38.2 2.7 %shard_map.101 = bf16[32,2,32,128]{3,2,1,0:T(8,128)(2,1)} custom-call(bf16[32,2,2,32,128]{4,3,2,1,0:T(8,128)(2,1)} %all_to_all.10.edges_ref), custom_call_target="tpu_custom_call" | custom-call | tf_op jit(solution)/shard_map/pallas_call | solution.py:210
  41.0 18.8 %all_to_all.11 = bf16[32,2,32,128]{3,2,1,0:T(8,128)(2,1)S(1)} all-to-all(bf16[32,2,32,128]{3,2,1,0:T(8,128)(2,1)} %shard_map.101), channel_id=1, replica_groups=mesh['row'=8,'col'=4] {'row','col'}, dimensions={0} | all-to-all | bytes 1048576 | tf_op jit(solution)/shard_map/all_to_all | solution.py:214
  59.8 0.4 reshape.10
  60.2 0.3 copy.14
  60.5 1.9 %copy.15.mixed_ref = bf16[32,64,128]{2,1,0:T(8,128)(2,1)} copy(bf16[32,64,128]{1,0,2:T(8,128)(2,1)S(1)} %bitcast.10) | data formatting | bytes 1048576 | tf_op jit(solution)/shard_map/reshape | solution.py:215
  62.4 4.8 %shard_map.102 = bf16[32,64,128]{2,1,0:T(8,128)(2,1)} custom-call(bf16[32,64,128]{2,1,0:T(8,128)(2,1)} %copy.15.mixed_ref, bf16[32,64,128]{2,1,0:T(8,128)(2,1)} %pair_ref.3, f32[32,64,128]{2,1,0:T(8,128)} %get-tuple-element.8.gate_ref, bf16[128,128]{1,0:T(8,128)(2,1)} %wo_ref.1, bf16[128,512]{1,0:T(8,128)(2,1)} %wu_ref.1, bf16[512,128]{1,0:T(8,128)(2,1)} %wd_ref.1), custom_call_target="tpu_custom_call" | custom-call | tf_op jit(solution)/shard_map/pallas_call | solution.py:216

commit v9 on v8

--- a/solution.py
+++ b/solution.py
@@ -125,7 +125,7 @@
     return result.astype(jnp.bfloat16).reshape(rows, cols, width)
 
 
-def project_kernel(mask_ref, pair_ref, wag_ref, wap_ref, wbg_ref, wbp_ref, wg_ref, z_ref, gate_ref, *, block):
+def project_kernel(mask_ref, pair_ref, wag_ref, wap_ref, wbg_ref, wbp_ref, z_ref, *, block):
     rows, cols, width = pair_ref.shape
     quarter = wag_ref.shape[1] // 2
 
@@ -147,8 +147,6 @@
         center = values - jnp.mean(values, axis=-1, keepdims=True)
         spread = jnp.mean(center * center, axis=-1, keepdims=True)
         normed = (center * lax.rsqrt(spread + 1e-05)).astype(jnp.bfloat16)
-        gate = jax.nn.sigmoid(jnp.dot(normed, wg_ref[...], preferred_element_type=jnp.float32))
-        gate_ref[pl.ds(first, block)] = gate.reshape(block, cols, width)
         zeros = jnp.zeros_like(normed)
         top = jnp.concatenate([normed, zeros], axis=1).reshape(block, cols, 2 * width)
         bottom = jnp.concatenate([zeros, normed], axis=1).reshape(block, cols, 2 * width)
@@ -167,6 +165,16 @@
     lax.fori_loop(0, rows // block, rows_of, 0)
 
 
+def gate_kernel(pair_ref, wg_ref, gate_ref):
+    rows, cols, width = pair_ref.shape
+    values = pair_ref[...].astype(jnp.float32).reshape(rows * cols, width)
+    center = values - jnp.mean(values, axis=-1, keepdims=True)
+    spread = jnp.mean(center * center, axis=-1, keepdims=True)
+    normed = (center * lax.rsqrt(spread + 1e-05)).astype(jnp.bfloat16)
+    gate = jax.nn.sigmoid(jnp.dot(normed, wg_ref[...], preferred_element_type=jnp.float32))
+    gate_ref[...] = gate.reshape(rows, cols, width)
+
+
 def transition_kernel(mixed_ref, pair_ref, gate_ref, wo_ref, wu_ref, wd_ref, out_ref, *, block):
     rows, cols, width = pair_ref.shape
 
@@ -197,14 +205,14 @@
     hid = w_agate.shape[1]
     pairs = hid // n_dev // 2
 
-    z, gate = pl.pallas_call(
+    z = pl.pallas_call(
         functools.partial(project_kernel, block=rows),
-        out_shape=(
-            jax.ShapeDtypeStruct((rows, hid, 2 * cols), jnp.bfloat16),
-            jax.ShapeDtypeStruct((rows, cols, width), jnp.float32),
-        ),
-        in_specs=[pl.BlockSpec(memory_space=pltpu.SMEM)] + [pl.BlockSpec(memory_space=pltpu.VMEM)] * 6,
-    )(mask, pair, w_agate, w_aproj, w_bgate, w_bproj, w_gate)
+        out_shape=jax.ShapeDtypeStruct((rows, hid, 2 * cols), jnp.bfloat16),
+        in_specs=[pl.BlockSpec(memory_space=pltpu.SMEM)] + [pl.BlockSpec(memory_space=pltpu.VMEM)] * 5,
+    )(mask, pair, w_agate, w_aproj, w_bgate, w_bproj)
+    gate = pl.pallas_call(
+        gate_kernel, out_shape=jax.ShapeDtypeStruct((rows, cols, width), jnp.float32)
+    )(pair, w_gate)
     edges = jnp.transpose(z.reshape(rows, 2, n_dev, pairs, 2 * cols), (2, 1, 3, 0, 4))
     edges = lax.all_to_all(edges, ("row", "col"), split_axis=0, concat_axis=0, tiled=True)
     mixed = pl.pallas_call(

time: 68.3 us -> 68.4 us (level)
  blocking collectives: 51.1 us -> 32.3 us
  waiting for transfers between devices: 0 us -> 11.6 us
  starting transfers between devices: 0 us -> 4.45 us
  Pallas kernels: 11.1 us -> 14 us
    all_to_all x1 -> x0, blocking collectives: 18.8 us -> none  [body_fused(): lax.all_to_all(mixed, ('row', 'col'), split_axis=0, concat_axis=0, tiled=...]
    all_to_all x0 -> x1, waiting for transfers between devices: none -> 11.6 us  [body_fused(): lax.all_to_all(mixed, ('row', 'col'), split_axis=0, concat_axis=0, tiled=...]
    all_to_all x0 -> x1, starting transfers between devices: none -> 4.45 us  [body_fused(): lax.all_to_all(mixed, ('row', 'col'), split_axis=0, concat_axis=0, tiled=...]
    pallas_call x1 -> x2, Pallas kernels: 3.53 us -> 6.38 us  [the longest x1 3.59 us: body_fused(): pl.pallas_call(functools.partial(project_kernel, block=rows), out_shape=j...]
  transfers between devices with their start and end apart: 0 -> 1, of which waited for: 0 -> 1; matrix products, arithmetic and copies ran while one was open for 0% -> 0% of each run, Pallas kernels for 0% -> 4%
where the time goes in v9:
time: 68.4 us; the launch traced here: 67.3 us
  blocking collectives  32.3 us (47%)
  Pallas kernels  14 us (20%)
  waiting for transfers between devices  11.6 us (17%)
  local copies, waits for them, and re-layouts  5 us (7%)
  starting transfers between devices  4.45 us (7%)
    all_to_all x1, blocking collectives, body_fused(): lax.all_to_all(edges, ('row', 'col'), split_axis=0, concat_axis=0, tiled=...  32.3 us
    all_to_all x1, waiting for transfers between devices, body_fused(): lax.all_to_all(mixed, ('row', 'col'), split_axis=0, concat_axis=0, tiled=...  11.6 us
    pallas_call x1, Pallas kernels, body_fused(): pl.pallas_call(functools.partial(transition_kernel, block=rows), out_shap...  4.83 us
    all_to_all x1, starting transfers between devices, body_fused(): lax.all_to_all(mixed, ('row', 'col'), split_axis=0, concat_axis=0, tiled=...  4.45 us
    pallas_call x1, Pallas kernels, body_fused(): pl.pallas_call(functools.partial(project_kernel, block=rows), out_shape=j...  3.59 us
    pallas_call x1, Pallas kernels, body_fused(): pl.pallas_call(gate_kernel, out_shape=jax.ShapeDtypeStruct((rows, cols, w...  2.79 us
    pallas_call x1, Pallas kernels, body_fused(): pl.pallas_call(functools.partial(mix_kernel, n_col=n_col), out_shape=jax....  2.74 us
    reshape x1, local copies, waits for them, and re-layouts, body_fused(): z.reshape(rows, 2, n_dev, pairs, 2 * cols)  2.44 us
  transfers between devices with their start and end apart: 1, of which 1 were waited for; matrix products, arithmetic and copies ran while one was open for 0% of the time, Pallas kernels for 4%

profile of v9, /device:TPU:0, one launch (start us, length us, event | category | flops | bytes accessed | tf_op | source)
XLA Modules:
  0.0 67.3 jit_solution(18073006973279262423)
XLA Ops:
  0.0 3.6 %shard_map.100 = bf16[32,128,128]{2,1,0:T(8,128)(2,1)} custom-call(s32[256]{0:T(256)} %mask_ref.1, bf16[32,64,128]{2,1,0:T(8,128)(2,1)} %pair_ref.5, bf16[128,128]{1,0:T(8,128)(2,1)} %wag_ref.1, bf16[128,128]{1,0:T(8,128)(2,1)} %wap_ref.1, bf16[128,128]{1,0:T(8,128)(2,1)} %wbg_ref.1, bf16[128,128]{1,0:T(8,128)(2,1)} %wbp_ref.1), custom_call_target="tpu_custom_call" | custom-call | tf_op jit(solution)/shard_map/pallas_call | solution.py:208
  3.6 2.4 %copy.19 = bf16[32,2,32,2,128]{4,0,3,1,2:T(8,128)(2,1)S(1)} copy(bf16[32,2,32,2,128]{4,3,2,1,0:T(2,128)(2,1)} %bitcast.11) | data formatting | bytes 2097152 | tf_op jit(solution)/shard_map/reshape | solution.py:216
  6.0 32.3 %all_to_all.10.edges_ref = bf16[32,2,2,32,128]{4,3,2,1,0:T(8,128)(2,1)} all-to-all(bf16[32,2,2,32,128]{4,3,2,1,0:T(8,128)(2,1)S(1)} %bitcast.9), channel_id=1, replica_groups=mesh['row'=8,'col'=4] {'row','col'}, dimensions={0} | all-to-all | bytes 2097152 | tf_op jit(solution)/shard_map/all_to_all | solution.py:217
  38.3 2.7 %shard_map.101 = bf16[32,2,32,128]{3,2,1,0:T(8,128)(2,1)} custom-call(bf16[32,2,2,32,128]{4,3,2,1,0:T(8,128)(2,1)} %all_to_all.10.edges_ref), custom_call_target="tpu_custom_call" | custom-call | tf_op jit(solution)/shard_map/pallas_call | solution.py:218
  41.0 4.5 %all-to-all-start.1 = ((bf16[32,2,32,128]{3,2,1,0:T(8,128)(2,1)}), bf16[32,2,32,128]{3,2,1,0:T(8,128)(2,1)S(1)}, u32[]{:S(2)}, u32[]{:S(2)}) async-start(bf16[32,2,32,128]{3,2,1,0:T(8,128)(2,1)} %shard_map.101), calls=%async_computation.1 | async-start | bytes 1048576 | tf_op jit(solution)/shard_map/all_to_all | solution.py:222
  45.5 2.8 %shard_map.102.gate_ref = f32[32,64,128]{2,1,0:T(8,128)} custom-call(bf16[32,64,128]{2,1,0:T(8,128)(2,1)} %pair_ref.5, bf16[128,128]{1,0:T(8,128)(2,1)} %wg_ref.1), custom_call_target="tpu_custom_call" | custom-call | tf_op jit(solution)/shard_map/pallas_call | solution.py:213
  48.3 11.6 %all-to-all-done.1 = bf16[32,2,32,128]{3,2,1,0:T(8,128)(2,1)S(1)} async-done(((bf16[32,2,32,128]{3,2,1,0:T(8,128)(2,1)}), bf16[32,2,32,128]{3,2,1,0:T(8,128)(2,1)S(1)}, u32[]{:S(2)}, u32[]{:S(2)}) %all-to-all-start.1) | async-done | bytes 524320 | tf_op jit(solution)/shard_map/all_to_all | solution.py:222
  59.9 0.4 reshape.10
  60.3 0.3 copy.14
  60.6 1.9 %copy.15.mixed_ref = bf16[32,64,128]{2,1,0:T(8,128)(2,1)} copy(bf16[32,64,128]{1,0,2:T(8,128)(2,1)S(1)} %bitcast.10) | data formatting | bytes 1048576 | tf_op jit(solution)/shard_map/reshape | solution.py:223
  62.5 4.8 %shard_map.103 = bf16[32,64,128]{2,1,0:T(8,128)(2,1)} custom-call(bf16[32,64,128]{2,1,0:T(8,128)(2,1)} %copy.15.mixed_ref, bf16[32,64,128]{2,1,0:T(8,128)(2,1)} %pair_ref.5, f32[32,64,128]{2,1,0:T(8,128)} %shard_map.102.gate_ref, bf16[128,128]{1,0:T(8,128)(2,1)} %wo_ref.1, bf16[128,512]{1,0:T(8,128)(2,1)} %wu_ref.1, bf16[512,128]{1,0:T(8,128)(2,1)} %wd_ref.1), custom_call_target="tpu_custom_call" | custom-call | tf_op jit(solution)/shard_map/pallas_call | solution.py:224
Async XLA Ops:
  41.0 18.8 %all-to-all-start.1 = ((bf16[32,2,32,128]{3,2,1,0:T(8,128)(2,1)}), bf16[32,2,32,128]{3,2,1,0:T(8,128)(2,1)S(1)}, u32[]{:S(2)}, u32[]{:S(2)}) async-start(bf16[32,2,32,128]{3,2,1,0:T(8,128)(2,1)} %shard_map.101), calls=%async_computation.1 | async-start | bytes 1048576 | tf_op jit(solution)/shard_map/all_to_all | solution.py:222

commit v10 on v9

--- a/solution.py
+++ b/solution.py
@@ -175,28 +175,28 @@
     gate_ref[...] = gate.reshape(rows, cols, width)
 
 
-def transition_kernel(mixed_ref, pair_ref, gate_ref, wo_ref, wu_ref, wd_ref, out_ref, *, block):
+def transition_kernel(mixed_ref, pair_ref, gate_ref, wo_ref, wu_ref, wd_ref, out_ref):
     rows, cols, width = pair_ref.shape
+    pairs = mixed_ref.shape[0] // rows
 
     def norm(values):
         center = values - jnp.mean(values, axis=-1, keepdims=True)
         spread = jnp.mean(center * center, axis=-1, keepdims=True)
         return center * lax.rsqrt(spread + 1e-05)
 
-    def rows_of(step, carry):
-        first = pl.multiple_of(step * block, block)
-        mixed = mixed_ref[pl.ds(first, block)].astype(jnp.float32).reshape(block * cols, -1)
-        pair = pair_ref[pl.ds(first, block)].astype(jnp.float32).reshape(block * cols, width)
-        gate = gate_ref[pl.ds(first, block)].reshape(block * cols, width)
-        mixed_normed = norm(mixed).astype(jnp.bfloat16)
-        middle = pair + gate * jnp.dot(mixed_normed, wo_ref[...], preferred_element_type=jnp.float32)
-        trans_in = norm(middle).astype(jnp.bfloat16)
-        hidden = jnp.maximum(jnp.dot(trans_in, wu_ref[...], preferred_element_type=jnp.float32), 0.0)
-        result = middle + jnp.dot(hidden.astype(jnp.bfloat16), wd_ref[...], preferred_element_type=jnp.float32)
-        out_ref[pl.ds(first, block)] = result.astype(out_ref.dtype).reshape(block, cols, width)
-        return carry
-
-    lax.fori_loop(0, rows // block, rows_of, 0)
+    parts = []
+    for i in range(rows):
+        turned = mixed_ref[pl.ds(i, pairs, stride=rows), :].astype(jnp.float32).T
+        parts.append(jnp.concatenate([turned[:cols], turned[cols:]], axis=1))
+    mixed = jnp.concatenate(parts, axis=0)
+    pair = pair_ref[...].astype(jnp.float32).reshape(rows * cols, width)
+    gate = gate_ref[...].reshape(rows * cols, width)
+    mixed_normed = norm(mixed).astype(jnp.bfloat16)
+    middle = pair + gate * jnp.dot(mixed_normed, wo_ref[...], preferred_element_type=jnp.float32)
+    trans_in = norm(middle).astype(jnp.bfloat16)
+    hidden = jnp.maximum(jnp.dot(trans_in, wu_ref[...], preferred_element_type=jnp.float32), 0.0)
+    result = middle + jnp.dot(hidden.astype(jnp.bfloat16), wd_ref[...], preferred_element_type=jnp.float32)
+    out_ref[...] = result.astype(out_ref.dtype).reshape(rows, cols, width)
 
 
 def body_fused(pair, mask, w_agate, w_aproj, w_bgate, w_bproj, w_gate, w_out, w_up, w_down, *, n_row, n_col):
@@ -220,9 +220,9 @@
         out_shape=jax.ShapeDtypeStruct((n_dev, pairs, rows, 2 * cols), jnp.bfloat16),
     )(edges)
     mixed = lax.all_to_all(mixed, ("row", "col"), split_axis=0, concat_axis=0, tiled=True)
-    mixed = jnp.transpose(mixed.reshape(n_dev, pairs, rows, 2, cols), (2, 4, 3, 0, 1)).reshape(rows, cols, hid)
+    mixed = mixed.reshape(n_dev * pairs * rows, 2 * cols)
     return pl.pallas_call(
-        functools.partial(transition_kernel, block=rows),
+        transition_kernel,
         out_shape=jax.ShapeDtypeStruct((rows, cols, width), jnp.bfloat16),
     )(mixed, pair, gate, w_out, w_up, w_down)
 

time: 68.4 us -> 67.6 us (0.988)
  local copies, waits for them, and re-layouts: 5 us -> 3.24 us
  Pallas kernels: 14 us -> 15 us
    reshape x3 -> x0, local copies, waits for them, and re-layouts: 2.55 us -> none  [the longest x1 1.9 us: body_fused(): jnp.transpose(mixed.reshape(n_dev, pairs, rows, 2, cols), (2, 4, 3, 0, 1))]
    pallas_call x1, Pallas kernels: 4.83 us -> 5.86 us  [body_fused(): pl.pallas_call(transition_kernel, out_shape=jax.ShapeDtypeStruct((rows, c...]
    unnamed x0 -> x2, local copies, waits for them, and re-layouts: none -> 0.8 us
where the time goes in v10:
time: 67.6 us; the launch traced here: 66.5 us
  blocking collectives  32.3 us (48%)
  Pallas kernels  15 us (22%)
  waiting for transfers between devices  11.6 us (17%)
  starting transfers between devices  4.45 us (7%)
  local copies, waits for them, and re-layouts  3.24 us (5%)
    all_to_all x1, blocking collectives, body_fused(): lax.all_to_all(edges, ('row', 'col'), split_axis=0, concat_axis=0, tiled=...  32.3 us
    all_to_all x1, waiting for transfers between devices, body_fused(): lax.all_to_all(mixed, ('row', 'col'), split_axis=0, concat_axis=0, tiled=...  11.6 us
    pallas_call x1, Pallas kernels, body_fused(): pl.pallas_call(transition_kernel, out_shape=jax.ShapeDtypeStruct((rows, c...  5.86 us
    all_to_all x1, starting transfers between devices, body_fused(): lax.all_to_all(mixed, ('row', 'col'), split_axis=0, concat_axis=0, tiled=...  4.45 us
    pallas_call x1, Pallas kernels, body_fused(): pl.pallas_call(functools.partial(project_kernel, block=rows), out_shape=j...  3.59 us
    pallas_call x1, Pallas kernels, body_fused(): pl.pallas_call(gate_kernel, out_shape=jax.ShapeDtypeStruct((rows, cols, w...  2.78 us
    pallas_call x1, Pallas kernels, body_fused(): pl.pallas_call(functools.partial(mix_kernel, n_col=n_col), out_shape=jax....  2.73 us
    reshape x1, local copies, waits for them, and re-layouts, body_fused(): z.reshape(rows, 2, n_dev, pairs, 2 * cols)  2.44 us
  transfers between devices with their start and end apart: 1, of which 1 were waited for; matrix products, arithmetic and copies ran while one was open for 0% of the time, Pallas kernels for 4%

profile of v10, /device:TPU:0, one launch (start us, length us, event | category | flops | bytes accessed | tf_op | source)
XLA Modules:
  0.0 66.5 jit_solution(729030431909997204)
XLA Ops:
  0.0 3.6 %shard_map.100 = bf16[32,128,128]{2,1,0:T(8,128)(2,1)} custom-call(s32[256]{0:T(256)} %mask_ref.1, bf16[32,64,128]{2,1,0:T(8,128)(2,1)} %pair_ref.5, bf16[128,128]{1,0:T(8,128)(2,1)} %wag_ref.1, bf16[128,128]{1,0:T(8,128)(2,1)} %wap_ref.1, bf16[128,128]{1,0:T(8,128)(2,1)} %wbg_ref.1, bf16[128,128]{1,0:T(8,128)(2,1)} %wbp_ref.1), custom_call_target="tpu_custom_call" | custom-call | tf_op jit(solution)/shard_map/pallas_call | solution.py:208
  3.6 2.4 %copy.16 = bf16[32,2,32,2,128]{4,0,3,1,2:T(8,128)(2,1)S(1)} copy(bf16[32,2,32,2,128]{4,3,2,1,0:T(2,128)(2,1)} %bitcast.6) | data formatting | bytes 2097152 | tf_op jit(solution)/shard_map/reshape | solution.py:216
  6.0 32.3 %all_to_all.10.edges_ref = bf16[32,2,2,32,128]{4,3,2,1,0:T(8,128)(2,1)} all-to-all(bf16[32,2,2,32,128]{4,3,2,1,0:T(8,128)(2,1)S(1)} %bitcast.5), channel_id=1, replica_groups=mesh['row'=8,'col'=4] {'row','col'}, dimensions={0} | all-to-all | bytes 2097152 | tf_op jit(solution)/shard_map/all_to_all | solution.py:217
  38.3 2.7 %shard_map.101 = bf16[32,2,32,128]{3,2,1,0:T(8,128)(2,1)} custom-call(bf16[32,2,2,32,128]{4,3,2,1,0:T(8,128)(2,1)} %all_to_all.10.edges_ref), custom_call_target="tpu_custom_call" | custom-call | tf_op jit(solution)/shard_map/pallas_call | solution.py:218
  41.0 4.5 %all-to-all-start.1 = ((bf16[32,2,32,128]{3,2,1,0:T(8,128)(2,1)}), bf16[32,2,32,128]{3,2,1,0:T(8,128)(2,1)S(1)}, u32[]{:S(2)}, u32[]{:S(2)}) async-start(bf16[32,2,32,128]{3,2,1,0:T(8,128)(2,1)} %shard_map.101), calls=%async_computation.1 | async-start | bytes 1048576 | tf_op jit(solution)/shard_map/all_to_all | solution.py:222
  45.5 2.8 %shard_map.102.gate_ref = f32[32,64,128]{2,1,0:T(8,128)} custom-call(bf16[32,64,128]{2,1,0:T(8,128)(2,1)} %pair_ref.5, bf16[128,128]{1,0:T(8,128)(2,1)} %wg_ref.1), custom_call_target="tpu_custom_call" | custom-call | tf_op jit(solution)/shard_map/pallas_call | solution.py:213
  48.3 11.6 %all-to-all-done.1 = bf16[32,2,32,128]{3,2,1,0:T(8,128)(2,1)S(1)} async-done(((bf16[32,2,32,128]{3,2,1,0:T(8,128)(2,1)}), bf16[32,2,32,128]{3,2,1,0:T(8,128)(2,1)S(1)}, u32[]{:S(2)}, u32[]{:S(2)}) %all-to-all-start.1) | async-done | bytes 524320 | tf_op jit(solution)/shard_map/all_to_all | solution.py:222
  59.9 0.0 copy-start
  59.9 0.8 %copy-done = bf16[32,2,32,128]{3,2,1,0:T(8,128)(2,1)} copy-done((bf16[32,2,32,128]{3,2,1,0:T(8,128)(2,1)}, bf16[32,2,32,128]{3,2,1,0:T(8,128)(2,1)S(1)}, u32[]{:S(2)}) %copy-start) | copy-done | bytes 524312
  60.7 5.9 %shard_map.103 = bf16[32,64,128]{2,1,0:T(8,128)(2,1)} custom-call(bf16[2048,128]{1,0:T(8,128)(2,1)} %bitcast.7, bf16[32,64,128]{2,1,0:T(8,128)(2,1)} %pair_ref.5, f32[32,64,128]{2,1,0:T(8,128)} %shard_map.102.gate_ref, bf16[128,128]{1,0:T(8,128)(2,1)} %wo_ref.1, bf16[128,512]{1,0:T(8,128)(2,1)} %wu_ref.1, bf16[512,128]{1,0:T(8,128)(2,1)} %wd_ref.1), custom_call_target="tpu_custom_call" | custom-call | tf_op jit(solution)/shard_map/pallas_call | solution.py:224
Async XLA Ops:
  41.0 18.8 %all-to-all-start.1 = ((bf16[32,2,32,128]{3,2,1,0:T(8,128)(2,1)}), bf16[32,2,32,128]{3,2,1,0:T(8,128)(2,1)S(1)}, u32[]{:S(2)}, u32[]{:S(2)}) async-start(bf16[32,2,32,128]{3,2,1,0:T(8,128)(2,1)} %shard_map.101), calls=%async_computation.1 | async-start | bytes 1048576 | tf_op jit(solution)/shard_map/all_to_all | solution.py:222
  59.9 0.8 %copy-start = (bf16[32,2,32,128]{3,2,1,0:T(8,128)(2,1)}, bf16[32,2,32,128]{3,2,1,0:T(8,128)(2,1)S(1)}, u32[]{:S(2)}) copy-start(bf16[32,2,32,128]{3,2,1,0:T(8,128)(2,1)S(1)} %all-to-all-done.1) | copy-start | bytes 1572868

commit v11 on v10

--- a/solution.py
+++ b/solution.py
@@ -71,17 +71,21 @@
     return result.astype(jnp.bfloat16).reshape(rows, cols, width)
 
 
-def mix_kernel(edges_ref, out_ref, *, n_col):
-    n_dev, _, pairs, rows, lanes = edges_ref.shape
+def mix_kernel(edges_ref, out_ref, *, n_col, side_major=True):
+    n_dev, rows, lanes = edges_ref.shape[0], edges_ref.shape[3], edges_ref.shape[4]
+    pairs = edges_ref.shape[2] if side_major else edges_ref.shape[1]
     n_row = n_dev // n_col
     cols = lanes // 2
     parity = (lax.broadcasted_iota(jnp.int32, (1, n_col * lanes), 1) // cols) % 2
     for hp in range(pairs):
 
+        def chunk(source, side):
+            return edges_ref[source, side, hp] if side_major else edges_ref[source, hp, side]
+
         def whole(side):
             return jnp.concatenate(
                 [
-                    jnp.concatenate([edges_ref[r * n_col + c, side, hp] for c in range(n_col)], axis=1)
+                    jnp.concatenate([chunk(r * n_col + c, side) for c in range(n_col)], axis=1)
                     for r in range(n_row)
                 ],
                 axis=0,
@@ -125,7 +129,7 @@
     return result.astype(jnp.bfloat16).reshape(rows, cols, width)
 
 
-def project_kernel(mask_ref, pair_ref, wag_ref, wap_ref, wbg_ref, wbp_ref, z_ref, *, block):
+def project_kernel(mask_ref, pair_ref, wag_ref, wap_ref, wbg_ref, wbp_ref, z_ref, staged_ref, *, block):
     rows, cols, width = pair_ref.shape
     quarter = wag_ref.shape[1] // 2
 
@@ -159,10 +163,12 @@
             present = col_mask * mask_ref[row_start + first + i].astype(jnp.float32)
             left = jax.nn.sigmoid(part[0:quarter]) * part[quarter : 2 * quarter] * present
             right = jax.nn.sigmoid(part[2 * quarter : 3 * quarter]) * part[3 * quarter :] * present
-            z_ref[first + i] = jnp.concatenate([left, right], axis=0).astype(z_ref.dtype)
+            staged_ref[pl.ds(first + i, quarter, stride=2 * rows), :] = left
+            staged_ref[pl.ds(rows + first + i, quarter, stride=2 * rows), :] = right
         return carry
 
     lax.fori_loop(0, rows // block, rows_of, 0)
+    z_ref[...] = staged_ref[...].astype(z_ref.dtype)
 
 
 def gate_kernel(pair_ref, wg_ref, gate_ref):
@@ -207,16 +213,17 @@
 
     z = pl.pallas_call(
         functools.partial(project_kernel, block=rows),
-        out_shape=jax.ShapeDtypeStruct((rows, hid, 2 * cols), jnp.bfloat16),
+        out_shape=jax.ShapeDtypeStruct((hid * rows, 2 * cols), jnp.bfloat16),
         in_specs=[pl.BlockSpec(memory_space=pltpu.SMEM)] + [pl.BlockSpec(memory_space=pltpu.VMEM)] * 5,
+        scratch_shapes=[pltpu.VMEM((hid * rows, 2 * cols), jnp.float32)],
     )(mask, pair, w_agate, w_aproj, w_bgate, w_bproj)
     gate = pl.pallas_call(
         gate_kernel, out_shape=jax.ShapeDtypeStruct((rows, cols, width), jnp.float32)
     )(pair, w_gate)
-    edges = jnp.transpose(z.reshape(rows, 2, n_dev, pairs, 2 * cols), (2, 1, 3, 0, 4))
+    edges = z.reshape(n_dev, pairs, 2, rows, 2 * cols)
     edges = lax.all_to_all(edges, ("row", "col"), split_axis=0, concat_axis=0, tiled=True)
     mixed = pl.pallas_call(
-        functools.partial(mix_kernel, n_col=n_col),
+        functools.partial(mix_kernel, n_col=n_col, side_major=False),
         out_shape=jax.ShapeDtypeStruct((n_dev, pairs, rows, 2 * cols), jnp.bfloat16),
     )(edges)
     mixed = lax.all_to_all(mixed, ("row", "col"), split_axis=0, concat_axis=0, tiled=True)

time: 67.6 us -> 66.5 us (0.984)
  local copies, waits for them, and re-layouts: 3.24 us -> 0.8 us
  Pallas kernels: 15 us -> 16.1 us
    reshape x1 -> x0, local copies, waits for them, and re-layouts: 2.44 us -> none  [body_fused(): z.reshape(rows, 2, n_dev, pairs, 2 * cols)]
    pallas_call x1, Pallas kernels: 3.59 us -> 4.7 us  [body_fused(): pl.pallas_call(functools.partial(project_kernel, block=rows), out_shape=j...]
where the time goes in v11:
time: 66.5 us; the launch traced here: 65.4 us
  blocking collectives  32.5 us (49%)
  Pallas kernels  16.1 us (24%)
  waiting for transfers between devices  11.6 us (17%)
  starting transfers between devices  4.45 us (7%)
  local copies, waits for them, and re-layouts  0.8 us (1%)
    all_to_all x1, blocking collectives, body_fused(): lax.all_to_all(edges, ('row', 'col'), split_axis=0, concat_axis=0, tiled=...  32.5 us
    all_to_all x1, waiting for transfers between devices, body_fused(): lax.all_to_all(mixed, ('row', 'col'), split_axis=0, concat_axis=0, tiled=...  11.6 us
    pallas_call x1, Pallas kernels, body_fused(): pl.pallas_call(transition_kernel, out_shape=jax.ShapeDtypeStruct((rows, c...  5.86 us
    pallas_call x1, Pallas kernels, body_fused(): pl.pallas_call(functools.partial(project_kernel, block=rows), out_shape=j...  4.7 us
    all_to_all x1, starting transfers between devices, body_fused(): lax.all_to_all(mixed, ('row', 'col'), split_axis=0, concat_axis=0, tiled=...  4.45 us
    pallas_call x1, Pallas kernels, body_fused(): pl.pallas_call(gate_kernel, out_shape=jax.ShapeDtypeStruct((rows, cols, w...  2.78 us
    pallas_call x1, Pallas kernels, body_fused(): pl.pallas_call(functools.partial(mix_kernel, n_col=n_col, side_major=Fals...  2.73 us
  transfers between devices with their start and end apart: 1, of which 1 were waited for; matrix products, arithmetic and copies ran while one was open for 0% of the time, Pallas kernels for 4%

profile of v11, /device:TPU:0, one launch (start us, length us, event | category | flops | bytes accessed | tf_op | source)
XLA Modules:
  0.0 65.4 jit_solution(1222412735005931908)
XLA Ops:
  0.0 4.7 %shard_map.100 = bf16[4096,128]{1,0:T(8,128)(2,1)} custom-call(s32[256]{0:T(256)} %mask_ref.1, bf16[32,64,128]{2,1,0:T(8,128)(2,1)} %pair_ref.5, bf16[128,128]{1,0:T(8,128)(2,1)} %wag_ref.1, bf16[128,128]{1,0:T(8,128)(2,1)} %wap_ref.1, bf16[128,128]{1,0:T(8,128)(2,1)} %wbg_ref.1, bf16[128,128]{1,0:T(8,128)(2,1)} %wbp_ref.1), custom_call_target="tpu_custom_call" | custom-call | tf_op jit(solution)/shard_map/pallas_call | solution.py:214
  4.7 32.5 %all_to_all.10.edges_ref = bf16[32,2,2,32,128]{4,3,2,1,0:T(8,128)(2,1)} all-to-all(bf16[32,2,2,32,128]{4,3,2,1,0:T(8,128)(2,1)} %bitcast.2), channel_id=1, replica_groups=mesh['row'=8,'col'=4] {'row','col'}, dimensions={0} | all-to-all | bytes 2097152 | tf_op jit(solution)/shard_map/all_to_all | solution.py:224
  37.2 2.7 %shard_map.101 = bf16[32,2,32,128]{3,2,1,0:T(8,128)(2,1)} custom-call(bf16[32,2,2,32,128]{4,3,2,1,0:T(8,128)(2,1)} %all_to_all.10.edges_ref), custom_call_target="tpu_custom_call" | custom-call | tf_op jit(solution)/shard_map/pallas_call | solution.py:225
  39.9 4.5 %all-to-all-start.1 = ((bf16[32,2,32,128]{3,2,1,0:T(8,128)(2,1)}), bf16[32,2,32,128]{3,2,1,0:T(8,128)(2,1)S(1)}, u32[]{:S(2)}, u32[]{:S(2)}) async-start(bf16[32,2,32,128]{3,2,1,0:T(8,128)(2,1)} %shard_map.101), calls=%async_computation.1 | async-start | bytes 1048576 | tf_op jit(solution)/shard_map/all_to_all | solution.py:229
  44.4 2.8 %shard_map.102.gate_ref = f32[32,64,128]{2,1,0:T(8,128)} custom-call(bf16[32,64,128]{2,1,0:T(8,128)(2,1)} %pair_ref.5, bf16[128,128]{1,0:T(8,128)(2,1)} %wg_ref.1), custom_call_target="tpu_custom_call" | custom-call | tf_op jit(solution)/shard_map/pallas_call | solution.py:220
  47.1 11.6 %all-to-all-done.1 = bf16[32,2,32,128]{3,2,1,0:T(8,128)(2,1)S(1)} async-done(((bf16[32,2,32,128]{3,2,1,0:T(8,128)(2,1)}), bf16[32,2,32,128]{3,2,1,0:T(8,128)(2,1)S(1)}, u32[]{:S(2)}, u32[]{:S(2)}) %all-to-all-start.1) | async-done | bytes 524320 | tf_op jit(solution)/shard_map/all_to_all | solution.py:229
  58.7 0.0 copy-start
  58.7 0.8 %copy-done = bf16[32,2,32,128]{3,2,1,0:T(8,128)(2,1)} copy-done((bf16[32,2,32,128]{3,2,1,0:T(8,128)(2,1)}, bf16[32,2,32,128]{3,2,1,0:T(8,128)(2,1)S(1)}, u32[]{:S(2)}) %copy-start) | copy-done | bytes 524312
  59.5 5.9 %shard_map.103 = bf16[32,64,128]{2,1,0:T(8,128)(2,1)} custom-call(bf16[2048,128]{1,0:T(8,128)(2,1)} %bitcast.3, bf16[32,64,128]{2,1,0:T(8,128)(2,1)} %pair_ref.5, f32[32,64,128]{2,1,0:T(8,128)} %shard_map.102.gate_ref, bf16[128,128]{1,0:T(8,128)(2,1)} %wo_ref.1, bf16[128,512]{1,0:T(8,128)(2,1)} %wu_ref.1, bf16[512,128]{1,0:T(8,128)(2,1)} %wd_ref.1), custom_call_target="tpu_custom_call" | custom-call | tf_op jit(solution)/shard_map/pallas_call | solution.py:231
Async XLA Ops:
  39.9 18.8 %all-to-all-start.1 = ((bf16[32,2,32,128]{3,2,1,0:T(8,128)(2,1)}), bf16[32,2,32,128]{3,2,1,0:T(8,128)(2,1)S(1)}, u32[]{:S(2)}, u32[]{:S(2)}) async-start(bf16[32,2,32,128]{3,2,1,0:T(8,128)(2,1)} %shard_map.101), calls=%async_computation.1 | async-start | bytes 1048576 | tf_op jit(solution)/shard_map/all_to_all | solution.py:229
  58.7 0.8 %copy-start = (bf16[32,2,32,128]{3,2,1,0:T(8,128)(2,1)}, bf16[32,2,32,128]{3,2,1,0:T(8,128)(2,1)S(1)}, u32[]{:S(2)}) copy-start(bf16[32,2,32,128]{3,2,1,0:T(8,128)(2,1)S(1)} %all-to-all-done.1) | copy-start | bytes 1572868

commit v12 on v11

--- a/solution.py
+++ b/solution.py
@@ -101,6 +101,28 @@
             mixed = lax.dot_general(
                 left, rhs, (((1,), (1,)), ((), ())), preferred_element_type=jnp.float32
             ).astype(out_ref.dtype)
+            for r in range(n_row):
+                out_ref[r * n_col + c, hp] = mixed[r * rows : (r + 1) * rows]
+
+
+def mix_blocks_kernel(edges_ref, out_ref):
+    n_row, n_col, pairs, _, rows, lanes = edges_ref.shape
+    cols = lanes // 2
+    per = cols // rows
+    parity = (lax.broadcasted_iota(jnp.int32, (1, lanes), 1) // cols) % 2
+    for hp in range(pairs):
+        for c in range(n_col):
+            total = None
+            for k in range(n_col):
+                left = edges_ref[:, k, hp, 0].reshape(n_row * rows, lanes)
+                right = edges_ref[c * per : (c + 1) * per, k, hp, 1].reshape(cols, lanes)
+                rhs = jnp.concatenate(
+                    [jnp.where(parity == 0, right, jnp.zeros_like(right)), jnp.where(parity == 1, right, jnp.zeros_like(right))],
+                    axis=0,
+                )
+                part = lax.dot_general(left, rhs, (((1,), (1,)), ((), ())), preferred_element_type=jnp.float32)
+                total = part if total is None else total + part
+            mixed = total.astype(out_ref.dtype)
             for r in range(n_row):
                 out_ref[r * n_col + c, hp] = mixed[r * rows : (r + 1) * rows]
 
@@ -223,9 +245,9 @@
     edges = z.reshape(n_dev, pairs, 2, rows, 2 * cols)
     edges = lax.all_to_all(edges, ("row", "col"), split_axis=0, concat_axis=0, tiled=True)
     mixed = pl.pallas_call(
-        functools.partial(mix_kernel, n_col=n_col, side_major=False),
+        mix_blocks_kernel,
         out_shape=jax.ShapeDtypeStruct((n_dev, pairs, rows, 2 * cols), jnp.bfloat16),
-    )(edges)
+    )(edges.reshape(n_row, n_col, pairs, 2, rows, 2 * cols))
     mixed = lax.all_to_all(mixed, ("row", "col"), split_axis=0, concat_axis=0, tiled=True)
     mixed = mixed.reshape(n_dev * pairs * rows, 2 * cols)
     return pl.pallas_call(
@@ -274,7 +296,7 @@
     def run(pair, mask, w_agate, *weights):
         hid = w_agate.shape[1]
         rows, cols = pair.shape[0] // n_row, pair.shape[1] // n_col
-        if hid % (2 * n_row * n_col) == 0 and 2 * cols == 128 and rows % 16 == 0 and n_row * rows == n_col * cols:
+        if hid % (2 * n_row * n_col) == 0 and 2 * cols == 128 and rows % 16 == 0 and cols % rows == 0 and n_row * rows == n_col * cols:
             body = functools.partial(body_fused, n_row=n_row, n_col=n_col)
         elif hid % (n_row * n_col) == 0:
             body = functools.partial(body_split, n_row=n_row, n_col=n_col)

time: 66.5 us -> 66.5 us (level)
  no operation moved by 1% of the time
where the time goes in v12:
time: 66.5 us; the launch traced here: 65.4 us
  blocking collectives  32.5 us (49%)
  Pallas kernels  16.1 us (24%)
  waiting for transfers between devices  11.6 us (17%)
  starting transfers between devices  4.46 us (7%)
  local copies, waits for them, and re-layouts  0.8 us (1%)
    all_to_all x1, blocking collectives, body_fused(): lax.all_to_all(edges, ('row', 'col'), split_axis=0, concat_axis=0, tiled=...  32.5 us
    all_to_all x1, waiting for transfers between devices, body_fused(): lax.all_to_all(mixed, ('row', 'col'), split_axis=0, concat_axis=0, tiled=...  11.6 us
    pallas_call x1, Pallas kernels, body_fused(): pl.pallas_call(transition_kernel, out_shape=jax.ShapeDtypeStruct((rows, c...  5.86 us
    pallas_call x1, Pallas kernels, body_fused(): pl.pallas_call(functools.partial(project_kernel, block=rows), out_shape=j...  4.7 us
    all_to_all x1, starting transfers between devices, body_fused(): lax.all_to_all(mixed, ('row', 'col'), split_axis=0, concat_axis=0, tiled=...  4.46 us
    pallas_call x1, Pallas kernels, body_fused(): pl.pallas_call(gate_kernel, out_shape=jax.ShapeDtypeStruct((rows, cols, w...  2.78 us
    pallas_call x1, Pallas kernels, body_fused(): pl.pallas_call(mix_blocks_kernel, out_shape=jax.ShapeDtypeStruct((n_dev,...  2.74 us
  transfers between devices with their start and end apart: 1, of which 1 were waited for; matrix products, arithmetic and copies ran while one was open for 0% of the time, Pallas kernels for 4%

profile of v12, /device:TPU:0, one launch (start us, length us, event | category | flops | bytes accessed | tf_op | source)
XLA Modules:
  0.0 65.4 jit_solution(10447518494332168381)
XLA Ops:
  0.0 4.7 %shard_map.100 = bf16[4096,128]{1,0:T(8,128)(2,1)} custom-call(s32[256]{0:T(256)} %mask_ref.1, bf16[32,64,128]{2,1,0:T(8,128)(2,1)} %pair_ref.5, bf16[128,128]{1,0:T(8,128)(2,1)} %wag_ref.1, bf16[128,128]{1,0:T(8,128)(2,1)} %wap_ref.1, bf16[128,128]{1,0:T(8,128)(2,1)} %wbg_ref.1, bf16[128,128]{1,0:T(8,128)(2,1)} %wbp_ref.1), custom_call_target="tpu_custom_call" | custom-call | tf_op jit(solution)/shard_map/pallas_call | solution.py:236
  4.7 32.5 %all_to_all.10 = bf16[32,2,2,32,128]{4,3,2,1,0:T(8,128)(2,1)} all-to-all(bf16[32,2,2,32,128]{4,3,2,1,0:T(8,128)(2,1)} %bitcast.4), channel_id=1, replica_groups=mesh['row'=8,'col'=4] {'row','col'}, dimensions={0} | all-to-all | bytes 2097152 | tf_op jit(solution)/shard_map/all_to_all | solution.py:246
  37.2 2.7 %shard_map.101 = bf16[32,2,32,128]{3,2,1,0:T(8,128)(2,1)} custom-call(bf16[8,4,2,2,32,128]{5,4,3,2,1,0:T(8,128)(2,1)} %bitcast.3), custom_call_target="tpu_custom_call" | custom-call | tf_op jit(solution)/shard_map/pallas_call | solution.py:247
  39.9 4.5 %all-to-all-start.1 = ((bf16[32,2,32,128]{3,2,1,0:T(8,128)(2,1)}), bf16[32,2,32,128]{3,2,1,0:T(8,128)(2,1)S(1)}, u32[]{:S(2)}, u32[]{:S(2)}) async-start(bf16[32,2,32,128]{3,2,1,0:T(8,128)(2,1)} %shard_map.101), calls=%async_computation.1 | async-start | bytes 1048576 | tf_op jit(solution)/shard_map/all_to_all | solution.py:251
  44.4 2.8 %shard_map.102.gate_ref = f32[32,64,128]{2,1,0:T(8,128)} custom-call(bf16[32,64,128]{2,1,0:T(8,128)(2,1)} %pair_ref.5, bf16[128,128]{1,0:T(8,128)(2,1)} %wg_ref.1), custom_call_target="tpu_custom_call" | custom-call | tf_op jit(solution)/shard_map/pallas_call | solution.py:242
  47.2 11.6 %all-to-all-done.1 = bf16[32,2,32,128]{3,2,1,0:T(8,128)(2,1)S(1)} async-done(((bf16[32,2,32,128]{3,2,1,0:T(8,128)(2,1)}), bf16[32,2,32,128]{3,2,1,0:T(8,128)(2,1)S(1)}, u32[]{:S(2)}, u32[]{:S(2)}) %all-to-all-start.1) | async-done | bytes 524320 | tf_op jit(solution)/shard_map/all_to_all | solution.py:251
  58.7 0.0 copy-start
  58.7 0.8 %copy-done = bf16[32,2,32,128]{3,2,1,0:T(8,128)(2,1)} copy-done((bf16[32,2,32,128]{3,2,1,0:T(8,128)(2,1)}, bf16[32,2,32,128]{3,2,1,0:T(8,128)(2,1)S(1)}, u32[]{:S(2)}) %copy-start) | copy-done | bytes 524312
  59.5 5.9 %shard_map.103 = bf16[32,64,128]{2,1,0:T(8,128)(2,1)} custom-call(bf16[2048,128]{1,0:T(8,128)(2,1)} %bitcast.5, bf16[32,64,128]{2,1,0:T(8,128)(2,1)} %pair_ref.5, f32[32,64,128]{2,1,0:T(8,128)} %shard_map.102.gate_ref, bf16[128,128]{1,0:T(8,128)(2,1)} %wo_ref.1, bf16[128,512]{1,0:T(8,128)(2,1)} %wu_ref.1, bf16[512,128]{1,0:T(8,128)(2,1)} %wd_ref.1), custom_call_target="tpu_custom_call" | custom-call | tf_op jit(solution)/shard_map/pallas_call | solution.py:253
Async XLA Ops:
  39.9 18.8 %all-to-all-start.1 = ((bf16[32,2,32,128]{3,2,1,0:T(8,128)(2,1)}), bf16[32,2,32,128]{3,2,1,0:T(8,128)(2,1)S(1)}, u32[]{:S(2)}, u32[]{:S(2)}) async-start(bf16[32,2,32,128]{3,2,1,0:T(8,128)(2,1)} %shard_map.101), calls=%async_computation.1 | async-start | bytes 1048576 | tf_op jit(solution)/shard_map/all_to_all | solution.py:251
  58.7 0.8 %copy-start = (bf16[32,2,32,128]{3,2,1,0:T(8,128)(2,1)}, bf16[32,2,32,128]{3,2,1,0:T(8,128)(2,1)S(1)}, u32[]{:S(2)}) copy-start(bf16[32,2,32,128]{3,2,1,0:T(8,128)(2,1)S(1)} %all-to-all-done.1) | copy-start | bytes 1572868

commit v13 on v11

--- a/solution.py
+++ b/solution.py
@@ -225,6 +225,9 @@
     mixed = pl.pallas_call(
         functools.partial(mix_kernel, n_col=n_col, side_major=False),
         out_shape=jax.ShapeDtypeStruct((n_dev, pairs, rows, 2 * cols), jnp.bfloat16),
+        grid=(pairs,),
+        in_specs=[pl.BlockSpec((n_dev, 1, 2, rows, 2 * cols), lambda hp: (0, hp, 0, 0, 0))],
+        out_specs=pl.BlockSpec((n_dev, 1, rows, 2 * cols), lambda hp: (0, hp, 0, 0)),
     )(edges)
     mixed = lax.all_to_all(mixed, ("row", "col"), split_axis=0, concat_axis=0, tiled=True)
     mixed = mixed.reshape(n_dev * pairs * rows, 2 * cols)

time: 66.5 us -> 66.4 us (level)
  no operation moved by 1% of the time
where the time goes in v13:
time: 66.4 us; the launch traced here: 65.3 us
  blocking collectives  32.5 us (49%)
  Pallas kernels  16 us (24%)
  waiting for transfers between devices  11.6 us (17%)
  starting transfers between devices  4.45 us (7%)
  local copies, waits for them, and re-layouts  0.8 us (1%)
    all_to_all x1, blocking collectives, body_fused(): lax.all_to_all(edges, ('row', 'col'), split_axis=0, concat_axis=0, tiled=...  32.5 us
    all_to_all x1, waiting for transfers between devices, body_fused(): lax.all_to_all(mixed, ('row', 'col'), split_axis=0, concat_axis=0, tiled=...  11.6 us
    pallas_call x1, Pallas kernels, body_fused(): pl.pallas_call(transition_kernel, out_shape=jax.ShapeDtypeStruct((rows, c...  5.86 us
    pallas_call x1, Pallas kernels, body_fused(): pl.pallas_call(functools.partial(project_kernel, block=rows), out_shape=j...  4.7 us
    all_to_all x1, starting transfers between devices, body_fused(): lax.all_to_all(mixed, ('row', 'col'), split_axis=0, concat_axis=0, tiled=...  4.45 us
    pallas_call x1, Pallas kernels, body_fused(): pl.pallas_call(gate_kernel, out_shape=jax.ShapeDtypeStruct((rows, cols, w...  2.78 us
    pallas_call x1, Pallas kernels, body_fused(): pl.pallas_call(functools.partial(mix_kernel, n_col=n_col, side_major=Fals...  2.66 us
  transfers between devices with their start and end apart: 1, of which 1 were waited for; matrix products, arithmetic and copies ran while one was open for 0% of the time, Pallas kernels for 4%

profile of v13, /device:TPU:0, one launch (start us, length us, event | category | flops | bytes accessed | tf_op | source)
XLA Modules:
  0.0 65.3 jit_solution(7487668001971392177)
XLA Ops:
  0.0 4.7 %shard_map.100 = bf16[4096,128]{1,0:T(8,128)(2,1)} custom-call(s32[256]{0:T(256)} %mask_ref.1, bf16[32,64,128]{2,1,0:T(8,128)(2,1)} %pair_ref.5, bf16[128,128]{1,0:T(8,128)(2,1)} %wag_ref.1, bf16[128,128]{1,0:T(8,128)(2,1)} %wap_ref.1, bf16[128,128]{1,0:T(8,128)(2,1)} %wbg_ref.1, bf16[128,128]{1,0:T(8,128)(2,1)} %wbp_ref.1), custom_call_target="tpu_custom_call" | custom-call | tf_op jit(solution)/shard_map/pallas_call | solution.py:214
  4.7 32.5 %all_to_all.10.edges_ref = bf16[32,2,2,32,128]{4,3,2,1,0:T(8,128)(2,1)} all-to-all(bf16[32,2,2,32,128]{4,3,2,1,0:T(8,128)(2,1)} %bitcast.2), channel_id=1, replica_groups=mesh['row'=8,'col'=4] {'row','col'}, dimensions={0} | all-to-all | bytes 2097152 | tf_op jit(solution)/shard_map/all_to_all | solution.py:224
  37.2 2.7 %shard_map.101 = bf16[32,2,32,128]{3,2,1,0:T(8,128)(2,1)} custom-call(bf16[32,2,2,32,128]{4,3,2,1,0:T(8,128)(2,1)} %all_to_all.10.edges_ref), custom_call_target="tpu_custom_call" | custom-call | tf_op jit(solution)/shard_map/pallas_call | solution.py:225
  39.8 4.5 %all-to-all-start.1 = ((bf16[32,2,32,128]{3,2,1,0:T(8,128)(2,1)}), bf16[32,2,32,128]{3,2,1,0:T(8,128)(2,1)S(1)}, u32[]{:S(2)}, u32[]{:S(2)}) async-start(bf16[32,2,32,128]{3,2,1,0:T(8,128)(2,1)} %shard_map.101), calls=%async_computation.1 | async-start | bytes 1048576 | tf_op jit(solution)/shard_map/all_to_all | solution.py:232
  44.3 2.8 %shard_map.102.gate_ref = f32[32,64,128]{2,1,0:T(8,128)} custom-call(bf16[32,64,128]{2,1,0:T(8,128)(2,1)} %pair_ref.5, bf16[128,128]{1,0:T(8,128)(2,1)} %wg_ref.1), custom_call_target="tpu_custom_call" | custom-call | tf_op jit(solution)/shard_map/pallas_call | solution.py:220
  47.1 11.6 %all-to-all-done.1 = bf16[32,2,32,128]{3,2,1,0:T(8,128)(2,1)S(1)} async-done(((bf16[32,2,32,128]{3,2,1,0:T(8,128)(2,1)}), bf16[32,2,32,128]{3,2,1,0:T(8,128)(2,1)S(1)}, u32[]{:S(2)}, u32[]{:S(2)}) %all-to-all-start.1) | async-done | bytes 524320 | tf_op jit(solution)/shard_map/all_to_all | solution.py:232
  58.7 0.0 copy-start
  58.7 0.8 %copy-done = bf16[32,2,32,128]{3,2,1,0:T(8,128)(2,1)} copy-done((bf16[32,2,32,128]{3,2,1,0:T(8,128)(2,1)}, bf16[32,2,32,128]{3,2,1,0:T(8,128)(2,1)S(1)}, u32[]{:S(2)}) %copy-start) | copy-done | bytes 524312
  59.5 5.9 %shard_map.103 = bf16[32,64,128]{2,1,0:T(8,128)(2,1)} custom-call(bf16[2048,128]{1,0:T(8,128)(2,1)} %bitcast.3, bf16[32,64,128]{2,1,0:T(8,128)(2,1)} %pair_ref.5, f32[32,64,128]{2,1,0:T(8,128)} %shard_map.102.gate_ref, bf16[128,128]{1,0:T(8,128)(2,1)} %wo_ref.1, bf16[128,512]{1,0:T(8,128)(2,1)} %wu_ref.1, bf16[512,128]{1,0:T(8,128)(2,1)} %wd_ref.1), custom_call_target="tpu_custom_call" | custom-call | tf_op jit(solution)/shard_map/pallas_call | solution.py:234
Async XLA Ops:
  39.8 18.8 %all-to-all-start.1 = ((bf16[32,2,32,128]{3,2,1,0:T(8,128)(2,1)}), bf16[32,2,32,128]{3,2,1,0:T(8,128)(2,1)S(1)}, u32[]{:S(2)}, u32[]{:S(2)}) async-start(bf16[32,2,32,128]{3,2,1,0:T(8,128)(2,1)} %shard_map.101), calls=%async_computation.1 | async-start | bytes 1048576 | tf_op jit(solution)/shard_map/all_to_all | solution.py:232
  58.7 0.8 %copy-start = (bf16[32,2,32,128]{3,2,1,0:T(8,128)(2,1)}, bf16[32,2,32,128]{3,2,1,0:T(8,128)(2,1)S(1)}, u32[]{:S(2)}) copy-start(bf16[32,2,32,128]{3,2,1,0:T(8,128)(2,1)S(1)} %all-to-all-done.1) | copy-start | bytes 1572868

commit v14 on v13

--- a/solution.py
+++ b/solution.py
@@ -181,20 +181,25 @@
     gate_ref[...] = gate.reshape(rows, cols, width)
 
 
-def transition_kernel(mixed_ref, pair_ref, gate_ref, wo_ref, wu_ref, wd_ref, out_ref):
+def transition_kernel(mixed_ref, pair_ref, gate_ref, wo_ref, wu_ref, wd_ref, out_ref, gathered_ref, *, all_rows):
     rows, cols, width = pair_ref.shape
-    pairs = mixed_ref.shape[0] // rows
+    pairs = mixed_ref.shape[0] // all_rows
 
     def norm(values):
         center = values - jnp.mean(values, axis=-1, keepdims=True)
         spread = jnp.mean(center * center, axis=-1, keepdims=True)
         return center * lax.rsqrt(spread + 1e-05)
 
-    parts = []
-    for i in range(rows):
-        turned = mixed_ref[pl.ds(i, pairs, stride=rows), :].astype(jnp.float32).T
-        parts.append(jnp.concatenate([turned[:cols], turned[cols:]], axis=1))
-    mixed = jnp.concatenate(parts, axis=0)
+    for step in range(all_rows // rows):
+
+        @pl.when(pl.program_id(0) == step)
+        def _():
+            for i in range(rows):
+                row = step * rows + i
+                turned = mixed_ref[pl.ds(row, pairs, stride=all_rows), :].astype(jnp.float32).T
+                gathered_ref[i * cols : (i + 1) * cols, :] = jnp.concatenate([turned[:cols], turned[cols:]], axis=1)
+
+    mixed = gathered_ref[...]
     pair = pair_ref[...].astype(jnp.float32).reshape(rows * cols, width)
     gate = gate_ref[...].reshape(rows * cols, width)
     mixed_normed = norm(mixed).astype(jnp.bfloat16)
@@ -232,8 +237,19 @@
     mixed = lax.all_to_all(mixed, ("row", "col"), split_axis=0, concat_axis=0, tiled=True)
     mixed = mixed.reshape(n_dev * pairs * rows, 2 * cols)
     return pl.pallas_call(
-        transition_kernel,
+        functools.partial(transition_kernel, all_rows=rows),
         out_shape=jax.ShapeDtypeStruct((rows, cols, width), jnp.bfloat16),
+        grid=(2,),
+        in_specs=[
+            pl.BlockSpec(mixed.shape, lambda b: (0, 0)),
+            pl.BlockSpec((rows // 2, cols, width), lambda b: (b, 0, 0)),
+            pl.BlockSpec((rows // 2, cols, width), lambda b: (b, 0, 0)),
+            pl.BlockSpec(w_out.shape, lambda b: (0, 0)),
+            pl.BlockSpec(w_up.shape, lambda b: (0, 0)),
+            pl.BlockSpec(w_down.shape, lambda b: (0, 0)),
+        ],
+        out_specs=pl.BlockSpec((rows // 2, cols, width), lambda b: (b, 0, 0)),
+        scratch_shapes=[pltpu.VMEM((rows // 2 * cols, hid), jnp.float32)],
     )(mixed, pair, gate, w_out, w_up, w_down)
 
 

time: 66.4 us -> 66.5 us (level)
  no operation moved by 1% of the time
where the time goes in v14:
time: 66.5 us; the launch traced here: 65.4 us
  blocking collectives  32.5 us (49%)
  Pallas kernels  16.1 us (24%)
  waiting for transfers between devices  11.6 us (17%)
  starting transfers between devices  4.45 us (7%)
  local copies, waits for them, and re-layouts  0.8 us (1%)
    all_to_all x1, blocking collectives, body_fused(): lax.all_to_all(edges, ('row', 'col'), split_axis=0, concat_axis=0, tiled=...  32.5 us
    all_to_all x1, waiting for transfers between devices, body_fused(): lax.all_to_all(mixed, ('row', 'col'), split_axis=0, concat_axis=0, tiled=...  11.6 us
    pallas_call x1, Pallas kernels, body_fused(): pl.pallas_call(functools.partial(transition_kernel, all_rows=rows), out_s...  5.96 us
    pallas_call x1, Pallas kernels, body_fused(): pl.pallas_call(functools.partial(project_kernel, block=rows), out_shape=j...  4.7 us
    all_to_all x1, starting transfers between devices, body_fused(): lax.all_to_all(mixed, ('row', 'col'), split_axis=0, concat_axis=0, tiled=...  4.45 us
    pallas_call x1, Pallas kernels, body_fused(): pl.pallas_call(gate_kernel, out_shape=jax.ShapeDtypeStruct((rows, cols, w...  2.78 us
    pallas_call x1, Pallas kernels, body_fused(): pl.pallas_call(functools.partial(mix_kernel, n_col=n_col, side_major=Fals...  2.66 us
  transfers between devices with their start and end apart: 1, of which 1 were waited for; matrix products, arithmetic and copies ran while one was open for 0% of the time, Pallas kernels for 4%

profile of v14, /device:TPU:0, one launch (start us, length us, event | category | flops | bytes accessed | tf_op | source)
XLA Modules:
  0.0 65.4 jit_solution(6745663356785926178)
XLA Ops:
  0.0 4.7 %shard_map.100 = bf16[4096,128]{1,0:T(8,128)(2,1)} custom-call(s32[256]{0:T(256)} %mask_ref.1, bf16[32,64,128]{2,1,0:T(8,128)(2,1)} %pair_ref.5, bf16[128,128]{1,0:T(8,128)(2,1)} %wag_ref.1, bf16[128,128]{1,0:T(8,128)(2,1)} %wap_ref.1, bf16[128,128]{1,0:T(8,128)(2,1)} %wbg_ref.1, bf16[128,128]{1,0:T(8,128)(2,1)} %wbp_ref.1), custom_call_target="tpu_custom_call" | custom-call | tf_op jit(solution)/shard_map/pallas_call | solution.py:219
  4.7 32.5 %all_to_all.10.edges_ref = bf16[32,2,2,32,128]{4,3,2,1,0:T(8,128)(2,1)} all-to-all(bf16[32,2,2,32,128]{4,3,2,1,0:T(8,128)(2,1)} %bitcast.2), channel_id=1, replica_groups=mesh['row'=8,'col'=4] {'row','col'}, dimensions={0} | all-to-all | bytes 2097152 | tf_op jit(solution)/shard_map/all_to_all | solution.py:229
  37.2 2.7 %shard_map.101 = bf16[32,2,32,128]{3,2,1,0:T(8,128)(2,1)} custom-call(bf16[32,2,2,32,128]{4,3,2,1,0:T(8,128)(2,1)} %all_to_all.10.edges_ref), custom_call_target="tpu_custom_call" | custom-call | tf_op jit(solution)/shard_map/pallas_call | solution.py:230
  39.8 4.5 %all-to-all-start.1 = ((bf16[32,2,32,128]{3,2,1,0:T(8,128)(2,1)}), bf16[32,2,32,128]{3,2,1,0:T(8,128)(2,1)S(1)}, u32[]{:S(2)}, u32[]{:S(2)}) async-start(bf16[32,2,32,128]{3,2,1,0:T(8,128)(2,1)} %shard_map.101), calls=%async_computation.1 | async-start | bytes 1048576 | tf_op jit(solution)/shard_map/all_to_all | solution.py:237
  44.3 2.8 %shard_map.102.gate_ref = f32[32,64,128]{2,1,0:T(8,128)} custom-call(bf16[32,64,128]{2,1,0:T(8,128)(2,1)} %pair_ref.5, bf16[128,128]{1,0:T(8,128)(2,1)} %wg_ref.1), custom_call_target="tpu_custom_call" | custom-call | tf_op jit(solution)/shard_map/pallas_call | solution.py:225
  47.1 11.6 %all-to-all-done.1 = bf16[32,2,32,128]{3,2,1,0:T(8,128)(2,1)S(1)} async-done(((bf16[32,2,32,128]{3,2,1,0:T(8,128)(2,1)}), bf16[32,2,32,128]{3,2,1,0:T(8,128)(2,1)S(1)}, u32[]{:S(2)}, u32[]{:S(2)}) %all-to-all-start.1) | async-done | bytes 524320 | tf_op jit(solution)/shard_map/all_to_all | solution.py:237
  58.7 0.0 copy-start
  58.7 0.8 %copy-done = bf16[32,2,32,128]{3,2,1,0:T(8,128)(2,1)} copy-done((bf16[32,2,32,128]{3,2,1,0:T(8,128)(2,1)}, bf16[32,2,32,128]{3,2,1,0:T(8,128)(2,1)S(1)}, u32[]{:S(2)}) %copy-start) | copy-done | bytes 524312
  59.5 6.0 %shard_map.103 = bf16[32,64,128]{2,1,0:T(8,128)(2,1)} custom-call(bf16[2048,128]{1,0:T(8,128)(2,1)} %bitcast.3, bf16[32,64,128]{2,1,0:T(8,128)(2,1)} %pair_ref.5, f32[32,64,128]{2,1,0:T(8,128)} %shard_map.102.gate_ref, bf16[128,128]{1,0:T(8,128)(2,1)} %wo_ref.1, bf16[128,512]{1,0:T(8,128)(2,1)} %wu_ref.1, bf16[512,128]{1,0:T(8,128)(2,1)} %wd_ref.1), custom_call_target="tpu_custom_call" | custom-call | tf_op jit(solution)/shard_map/pallas_call | solution.py:239
Async XLA Ops:
  39.8 18.8 %all-to-all-start.1 = ((bf16[32,2,32,128]{3,2,1,0:T(8,128)(2,1)}), bf16[32,2,32,128]{3,2,1,0:T(8,128)(2,1)S(1)}, u32[]{:S(2)}, u32[]{:S(2)}) async-start(bf16[32,2,32,128]{3,2,1,0:T(8,128)(2,1)} %shard_map.101), calls=%async_computation.1 | async-start | bytes 1048576 | tf_op jit(solution)/shard_map/all_to_all | solution.py:237
  58.7 0.8 %copy-start = (bf16[32,2,32,128]{3,2,1,0:T(8,128)(2,1)}, bf16[32,2,32,128]{3,2,1,0:T(8,128)(2,1)S(1)}, u32[]{:S(2)}) copy-start(bf16[32,2,32,128]{3,2,1,0:T(8,128)(2,1)S(1)} %all-to-all-done.1) | copy-start | bytes 1572868

commit v15 on v13

--- a/solution.py
+++ b/solution.py
@@ -200,8 +200,12 @@
     mixed_normed = norm(mixed).astype(jnp.bfloat16)
     middle = pair + gate * jnp.dot(mixed_normed, wo_ref[...], preferred_element_type=jnp.float32)
     trans_in = norm(middle).astype(jnp.bfloat16)
-    hidden = jnp.maximum(jnp.dot(trans_in, wu_ref[...], preferred_element_type=jnp.float32), 0.0)
-    result = middle + jnp.dot(hidden.astype(jnp.bfloat16), wd_ref[...], preferred_element_type=jnp.float32)
+    result = middle
+    span = 128 if wu_ref.shape[1] % 128 == 0 else wu_ref.shape[1]
+    for t in range(wu_ref.shape[1] // span):
+        cut = slice(t * span, (t + 1) * span)
+        hidden = jnp.maximum(jnp.dot(trans_in, wu_ref[:, cut], preferred_element_type=jnp.float32), 0.0)
+        result = result + jnp.dot(hidden.astype(jnp.bfloat16), wd_ref[cut, :], preferred_element_type=jnp.float32)
     out_ref[...] = result.astype(out_ref.dtype).reshape(rows, cols, width)
 
 

time: 66.4 us -> 66.4 us (level)
  no operation moved by 1% of the time
where the time goes in v15:
time: 66.4 us; the launch traced here: 65.3 us
  blocking collectives  32.5 us (49%)
  Pallas kernels  16 us (24%)
  waiting for transfers between devices  11.6 us (17%)
  starting transfers between devices  4.45 us (7%)
  local copies, waits for them, and re-layouts  0.8 us (1%)
    all_to_all x1, blocking collectives, body_fused(): lax.all_to_all(edges, ('row', 'col'), split_axis=0, concat_axis=0, tiled=...  32.5 us
    all_to_all x1, waiting for transfers between devices, body_fused(): lax.all_to_all(mixed, ('row', 'col'), split_axis=0, concat_axis=0, tiled=...  11.6 us
    pallas_call x1, Pallas kernels, body_fused(): pl.pallas_call(transition_kernel, out_shape=jax.ShapeDtypeStruct((rows, c...  5.88 us
    pallas_call x1, Pallas kernels, body_fused(): pl.pallas_call(functools.partial(project_kernel, block=rows), out_shape=j...  4.7 us
    all_to_all x1, starting transfers between devices, body_fused(): lax.all_to_all(mixed, ('row', 'col'), split_axis=0, concat_axis=0, tiled=...  4.45 us
    pallas_call x1, Pallas kernels, body_fused(): pl.pallas_call(gate_kernel, out_shape=jax.ShapeDtypeStruct((rows, cols, w...  2.78 us
    pallas_call x1, Pallas kernels, body_fused(): pl.pallas_call(functools.partial(mix_kernel, n_col=n_col, side_major=Fals...  2.66 us
  transfers between devices with their start and end apart: 1, of which 1 were waited for; matrix products, arithmetic and copies ran while one was open for 0% of the time, Pallas kernels for 4%

profile of v15, /device:TPU:0, one launch (start us, length us, event | category | flops | bytes accessed | tf_op | source)
XLA Modules:
  0.0 65.3 jit_solution(16617730628361702759)
XLA Ops:
  0.0 4.7 %shard_map.100 = bf16[4096,128]{1,0:T(8,128)(2,1)} custom-call(s32[256]{0:T(256)} %mask_ref.1, bf16[32,64,128]{2,1,0:T(8,128)(2,1)} %pair_ref.5, bf16[128,128]{1,0:T(8,128)(2,1)} %wag_ref.1, bf16[128,128]{1,0:T(8,128)(2,1)} %wap_ref.1, bf16[128,128]{1,0:T(8,128)(2,1)} %wbg_ref.1, bf16[128,128]{1,0:T(8,128)(2,1)} %wbp_ref.1), custom_call_target="tpu_custom_call" | custom-call | tf_op jit(solution)/shard_map/pallas_call | solution.py:218
  4.7 32.5 %all_to_all.10.edges_ref = bf16[32,2,2,32,128]{4,3,2,1,0:T(8,128)(2,1)} all-to-all(bf16[32,2,2,32,128]{4,3,2,1,0:T(8,128)(2,1)} %bitcast.2), channel_id=1, replica_groups=mesh['row'=8,'col'=4] {'row','col'}, dimensions={0} | all-to-all | bytes 2097152 | tf_op jit(solution)/shard_map/all_to_all | solution.py:228
  37.2 2.7 %shard_map.101 = bf16[32,2,32,128]{3,2,1,0:T(8,128)(2,1)} custom-call(bf16[32,2,2,32,128]{4,3,2,1,0:T(8,128)(2,1)} %all_to_all.10.edges_ref), custom_call_target="tpu_custom_call" | custom-call | tf_op jit(solution)/shard_map/pallas_call | solution.py:229
  39.8 4.5 %all-to-all-start.1 = ((bf16[32,2,32,128]{3,2,1,0:T(8,128)(2,1)}), bf16[32,2,32,128]{3,2,1,0:T(8,128)(2,1)S(1)}, u32[]{:S(2)}, u32[]{:S(2)}) async-start(bf16[32,2,32,128]{3,2,1,0:T(8,128)(2,1)} %shard_map.101), calls=%async_computation.1 | async-start | bytes 1048576 | tf_op jit(solution)/shard_map/all_to_all | solution.py:236
  44.3 2.8 %shard_map.102.gate_ref = f32[32,64,128]{2,1,0:T(8,128)} custom-call(bf16[32,64,128]{2,1,0:T(8,128)(2,1)} %pair_ref.5, bf16[128,128]{1,0:T(8,128)(2,1)} %wg_ref.1), custom_call_target="tpu_custom_call" | custom-call | tf_op jit(solution)/shard_map/pallas_call | solution.py:224
  47.1 11.6 %all-to-all-done.1 = bf16[32,2,32,128]{3,2,1,0:T(8,128)(2,1)S(1)} async-done(((bf16[32,2,32,128]{3,2,1,0:T(8,128)(2,1)}), bf16[32,2,32,128]{3,2,1,0:T(8,128)(2,1)S(1)}, u32[]{:S(2)}, u32[]{:S(2)}) %all-to-all-start.1) | async-done | bytes 524320 | tf_op jit(solution)/shard_map/all_to_all | solution.py:236
  58.7 0.0 copy-start
  58.7 0.8 %copy-done = bf16[32,2,32,128]{3,2,1,0:T(8,128)(2,1)} copy-done((bf16[32,2,32,128]{3,2,1,0:T(8,128)(2,1)}, bf16[32,2,32,128]{3,2,1,0:T(8,128)(2,1)S(1)}, u32[]{:S(2)}) %copy-start) | copy-done | bytes 524312
  59.5 5.9 %shard_map.103 = bf16[32,64,128]{2,1,0:T(8,128)(2,1)} custom-call(bf16[2048,128]{1,0:T(8,128)(2,1)} %bitcast.3, bf16[32,64,128]{2,1,0:T(8,128)(2,1)} %pair_ref.5, f32[32,64,128]{2,1,0:T(8,128)} %shard_map.102.gate_ref, bf16[128,128]{1,0:T(8,128)(2,1)} %wo_ref.1, bf16[128,512]{1,0:T(8,128)(2,1)} %wu_ref.1, bf16[512,128]{1,0:T(8,128)(2,1)} %wd_ref.1), custom_call_target="tpu_custom_call" | custom-call | tf_op jit(solution)/shard_map/pallas_call | solution.py:238
Async XLA Ops:
  39.8 18.8 %all-to-all-start.1 = ((bf16[32,2,32,128]{3,2,1,0:T(8,128)(2,1)}), bf16[32,2,32,128]{3,2,1,0:T(8,128)(2,1)S(1)}, u32[]{:S(2)}, u32[]{:S(2)}) async-start(bf16[32,2,32,128]{3,2,1,0:T(8,128)(2,1)} %shard_map.101), calls=%async_computation.1 | async-start | bytes 1048576 | tf_op jit(solution)/shard_map/all_to_all | solution.py:236
  58.7 0.8 %copy-start = (bf16[32,2,32,128]{3,2,1,0:T(8,128)(2,1)}, bf16[32,2,32,128]{3,2,1,0:T(8,128)(2,1)S(1)}, u32[]{:S(2)}) copy-start(bf16[32,2,32,128]{3,2,1,0:T(8,128)(2,1)S(1)} %all-to-all-done.1) | copy-start | bytes 1572868

commit v16 on v13

--- a/solution.py
+++ b/solution.py
@@ -138,7 +138,7 @@
         return jnp.concatenate([turned[:quarter], turned[quarter:]], axis=1)
 
     w2 = jnp.concatenate([paired(w) for w in (wag_ref, wap_ref, wbg_ref, wbp_ref)], axis=0)
-    row_start = lax.axis_index("row") * rows
+    row_start = lax.axis_index("row") * rows * pl.num_programs(0) + pl.program_id(0) * rows
     col_start = lax.axis_index("col") * cols
     lane = lax.broadcasted_iota(jnp.int32, (1, 2 * cols), 1) % cols
     col_mask = jnp.zeros((1, 2 * cols), jnp.float32)
@@ -168,7 +168,7 @@
         return carry
 
     lax.fori_loop(0, rows // block, rows_of, 0)
-    z_ref[...] = staged_ref[...].astype(z_ref.dtype)
+    z_ref[...] = staged_ref[...].reshape(z_ref.shape).astype(z_ref.dtype)
 
 
 def gate_kernel(pair_ref, wg_ref, gate_ref):
@@ -211,11 +211,22 @@
     hid = w_agate.shape[1]
     pairs = hid // n_dev // 2
 
+    half = rows // 2
+    weight = pl.BlockSpec(w_agate.shape, lambda b: (0, 0))
     z = pl.pallas_call(
-        functools.partial(project_kernel, block=rows),
-        out_shape=jax.ShapeDtypeStruct((hid * rows, 2 * cols), jnp.bfloat16),
-        in_specs=[pl.BlockSpec(memory_space=pltpu.SMEM)] + [pl.BlockSpec(memory_space=pltpu.VMEM)] * 5,
-        scratch_shapes=[pltpu.VMEM((hid * rows, 2 * cols), jnp.float32)],
+        functools.partial(project_kernel, block=half),
+        out_shape=jax.ShapeDtypeStruct((hid // 2, 2, rows, 2 * cols), jnp.bfloat16),
+        grid=(2,),
+        in_specs=[
+            pl.BlockSpec(memory_space=pltpu.SMEM),
+            pl.BlockSpec((half, cols, width), lambda b: (b, 0, 0)),
+            weight,
+            weight,
+            weight,
+            weight,
+        ],
+        out_specs=pl.BlockSpec((hid // 2, 2, half, 2 * cols), lambda b: (0, 0, b, 0)),
+        scratch_shapes=[pltpu.VMEM((hid * half, 2 * cols), jnp.float32)],
     )(mask, pair, w_agate, w_aproj, w_bgate, w_bproj)
     gate = pl.pallas_call(
         gate_kernel, out_shape=jax.ShapeDtypeStruct((rows, cols, width), jnp.float32)
@@ -277,7 +288,7 @@
     def run(pair, mask, w_agate, *weights):
         hid = w_agate.shape[1]
         rows, cols = pair.shape[0] // n_row, pair.shape[1] // n_col
-        if hid % (2 * n_row * n_col) == 0 and 2 * cols == 128 and rows % 16 == 0 and n_row * rows == n_col * cols:
+        if hid % (2 * n_row * n_col) == 0 and 2 * cols == 128 and rows % 32 == 0 and n_row * rows == n_col * cols:
             body = functools.partial(body_fused, n_row=n_row, n_col=n_col)
         elif hid % (n_row * n_col) == 0:
             body = functools.partial(body_split, n_row=n_row, n_col=n_col)

time: 66.4 us -> 66.5 us (level)
  no operation moved by 1% of the time
where the time goes in v16:
time: 66.5 us; the launch traced here: 65.4 us
  blocking collectives  32.5 us (49%)
  Pallas kernels  16.1 us (24%)
  waiting for transfers between devices  11.6 us (17%)
  starting transfers between devices  4.45 us (7%)
  local copies, waits for them, and re-layouts  0.8 us (1%)
    all_to_all x1, blocking collectives, body_fused(): lax.all_to_all(edges, ('row', 'col'), split_axis=0, concat_axis=0, tiled=...  32.5 us
    all_to_all x1, waiting for transfers between devices, body_fused(): lax.all_to_all(mixed, ('row', 'col'), split_axis=0, concat_axis=0, tiled=...  11.6 us
    pallas_call x1, Pallas kernels, body_fused(): pl.pallas_call(transition_kernel, out_shape=jax.ShapeDtypeStruct((rows, c...  5.86 us
    pallas_call x1, Pallas kernels, body_fused(): pl.pallas_call(functools.partial(project_kernel, block=half), out_shape=j...  4.76 us
    all_to_all x1, starting transfers between devices, body_fused(): lax.all_to_all(mixed, ('row', 'col'), split_axis=0, concat_axis=0, tiled=...  4.45 us
    pallas_call x1, Pallas kernels, body_fused(): pl.pallas_call(gate_kernel, out_shape=jax.ShapeDtypeStruct((rows, cols, w...  2.78 us
    pallas_call x1, Pallas kernels, body_fused(): pl.pallas_call(functools.partial(mix_kernel, n_col=n_col, side_major=Fals...  2.66 us
  transfers between devices with their start and end apart: 1, of which 1 were waited for; matrix products, arithmetic and copies ran while one was open for 0% of the time, Pallas kernels for 4%

profile of v16, /device:TPU:0, one launch (start us, length us, event | category | flops | bytes accessed | tf_op | source)
XLA Modules:
  0.0 65.4 jit_solution(8732563156421019972)
XLA Ops:
  0.0 4.8 %shard_map.100 = bf16[64,2,32,128]{3,2,1,0:T(8,128)(2,1)} custom-call(s32[256]{0:T(256)} %mask_ref.1, bf16[32,64,128]{2,1,0:T(8,128)(2,1)} %pair_ref.5, bf16[128,128]{1,0:T(8,128)(2,1)} %wag_ref.1, bf16[128,128]{1,0:T(8,128)(2,1)} %wap_ref.1, bf16[128,128]{1,0:T(8,128)(2,1)} %wbg_ref.1, bf16[128,128]{1,0:T(8,128)(2,1)} %wbp_ref.1), custom_call_target="tpu_custom_call" | custom-call | tf_op jit(solution)/shard_map/pallas_call | solution.py:216
  4.8 32.5 %all_to_all.10.edges_ref = bf16[32,2,2,32,128]{4,3,2,1,0:T(8,128)(2,1)} all-to-all(bf16[32,2,2,32,128]{4,3,2,1,0:T(8,128)(2,1)} %bitcast.2), channel_id=1, replica_groups=mesh['row'=8,'col'=4] {'row','col'}, dimensions={0} | all-to-all | bytes 2097152 | tf_op jit(solution)/shard_map/all_to_all | solution.py:235
  37.2 2.7 %shard_map.101 = bf16[32,2,32,128]{3,2,1,0:T(8,128)(2,1)} custom-call(bf16[32,2,2,32,128]{4,3,2,1,0:T(8,128)(2,1)} %all_to_all.10.edges_ref), custom_call_target="tpu_custom_call" | custom-call | tf_op jit(solution)/shard_map/pallas_call | solution.py:236
  39.9 4.5 %all-to-all-start.1 = ((bf16[32,2,32,128]{3,2,1,0:T(8,128)(2,1)}), bf16[32,2,32,128]{3,2,1,0:T(8,128)(2,1)S(1)}, u32[]{:S(2)}, u32[]{:S(2)}) async-start(bf16[32,2,32,128]{3,2,1,0:T(8,128)(2,1)} %shard_map.101), calls=%async_computation.1 | async-start | bytes 1048576 | tf_op jit(solution)/shard_map/all_to_all | solution.py:243
  44.3 2.8 %shard_map.102.gate_ref = f32[32,64,128]{2,1,0:T(8,128)} custom-call(bf16[32,64,128]{2,1,0:T(8,128)(2,1)} %pair_ref.5, bf16[128,128]{1,0:T(8,128)(2,1)} %wg_ref.1), custom_call_target="tpu_custom_call" | custom-call | tf_op jit(solution)/shard_map/pallas_call | solution.py:231
  47.1 11.6 %all-to-all-done.1 = bf16[32,2,32,128]{3,2,1,0:T(8,128)(2,1)S(1)} async-done(((bf16[32,2,32,128]{3,2,1,0:T(8,128)(2,1)}), bf16[32,2,32,128]{3,2,1,0:T(8,128)(2,1)S(1)}, u32[]{:S(2)}, u32[]{:S(2)}) %all-to-all-start.1) | async-done | bytes 524320 | tf_op jit(solution)/shard_map/all_to_all | solution.py:243
  58.7 0.0 copy-start
  58.7 0.8 %copy-done = bf16[32,2,32,128]{3,2,1,0:T(8,128)(2,1)} copy-done((bf16[32,2,32,128]{3,2,1,0:T(8,128)(2,1)}, bf16[32,2,32,128]{3,2,1,0:T(8,128)(2,1)S(1)}, u32[]{:S(2)}) %copy-start) | copy-done | bytes 524312
  59.5 5.9 %shard_map.103 = bf16[32,64,128]{2,1,0:T(8,128)(2,1)} custom-call(bf16[2048,128]{1,0:T(8,128)(2,1)} %bitcast.3, bf16[32,64,128]{2,1,0:T(8,128)(2,1)} %pair_ref.5, f32[32,64,128]{2,1,0:T(8,128)} %shard_map.102.gate_ref, bf16[128,128]{1,0:T(8,128)(2,1)} %wo_ref.1, bf16[128,512]{1,0:T(8,128)(2,1)} %wu_ref.1, bf16[512,128]{1,0:T(8,128)(2,1)} %wd_ref.1), custom_call_target="tpu_custom_call" | custom-call | tf_op jit(solution)/shard_map/pallas_call | solution.py:245
Async XLA Ops:
  39.9 18.8 %all-to-all-start.1 = ((bf16[32,2,32,128]{3,2,1,0:T(8,128)(2,1)}), bf16[32,2,32,128]{3,2,1,0:T(8,128)(2,1)S(1)}, u32[]{:S(2)}, u32[]{:S(2)}) async-start(bf16[32,2,32,128]{3,2,1,0:T(8,128)(2,1)} %shard_map.101), calls=%async_computation.1 | async-start | bytes 1048576 | tf_op jit(solution)/shard_map/all_to_all | solution.py:243
  58.7 0.8 %copy-start = (bf16[32,2,32,128]{3,2,1,0:T(8,128)(2,1)}, bf16[32,2,32,128]{3,2,1,0:T(8,128)(2,1)S(1)}, u32[]{:S(2)}) copy-start(bf16[32,2,32,128]{3,2,1,0:T(8,128)(2,1)S(1)} %all-to-all-done.1) | copy-start | bytes 1572868

commit v17 on v13

--- a/solution.py
+++ b/solution.py
@@ -181,7 +181,7 @@
     gate_ref[...] = gate.reshape(rows, cols, width)
 
 
-def transition_kernel(mixed_ref, pair_ref, gate_ref, wo_ref, wu_ref, wd_ref, out_ref):
+def transition_kernel(mixed_ref, pair_ref, wg_ref, wo_ref, wu_ref, wd_ref, out_ref):
     rows, cols, width = pair_ref.shape
     pairs = mixed_ref.shape[0] // rows
 
@@ -196,7 +196,7 @@
         parts.append(jnp.concatenate([turned[:cols], turned[cols:]], axis=1))
     mixed = jnp.concatenate(parts, axis=0)
     pair = pair_ref[...].astype(jnp.float32).reshape(rows * cols, width)
-    gate = gate_ref[...].reshape(rows * cols, width)
+    gate = jax.nn.sigmoid(jnp.dot(norm(pair).astype(jnp.bfloat16), wg_ref[...], preferred_element_type=jnp.float32))
     mixed_normed = norm(mixed).astype(jnp.bfloat16)
     middle = pair + gate * jnp.dot(mixed_normed, wo_ref[...], preferred_element_type=jnp.float32)
     trans_in = norm(middle).astype(jnp.bfloat16)
@@ -217,9 +217,6 @@
         in_specs=[pl.BlockSpec(memory_space=pltpu.SMEM)] + [pl.BlockSpec(memory_space=pltpu.VMEM)] * 5,
         scratch_shapes=[pltpu.VMEM((hid * rows, 2 * cols), jnp.float32)],
     )(mask, pair, w_agate, w_aproj, w_bgate, w_bproj)
-    gate = pl.pallas_call(
-        gate_kernel, out_shape=jax.ShapeDtypeStruct((rows, cols, width), jnp.float32)
-    )(pair, w_gate)
     edges = z.reshape(n_dev, pairs, 2, rows, 2 * cols)
     edges = lax.all_to_all(edges, ("row", "col"), split_axis=0, concat_axis=0, tiled=True)
     mixed = pl.pallas_call(
@@ -234,7 +231,7 @@
     return pl.pallas_call(
         transition_kernel,
         out_shape=jax.ShapeDtypeStruct((rows, cols, width), jnp.bfloat16),
-    )(mixed, pair, gate, w_out, w_up, w_down)
+    )(mixed, pair, w_gate, w_out, w_up, w_down)
 
 
 def body_rows(pair, mask, w_agate, w_aproj, w_bgate, w_bproj, w_gate, w_out, w_up, w_down):

time: 66.4 us -> 65.4 us (0.985)
  blocking collectives: 32.5 us -> 51.4 us
  waiting for transfers between devices: 11.6 us -> 0 us
  starting transfers between devices: 4.45 us -> 0 us
  Pallas kernels: 16 us -> 13 us
  local copies, waits for them, and re-layouts: 0.8 us -> 0 us
    all_to_all x0 -> x1, blocking collectives: none -> 18.9 us  [body_fused(): lax.all_to_all(mixed, ('row', 'col'), split_axis=0, concat_axis=0, tiled=...]
    all_to_all x1 -> x0, waiting for transfers between devices: 11.6 us -> none  [body_fused(): lax.all_to_all(mixed, ('row', 'col'), split_axis=0, concat_axis=0, tiled=...]
    all_to_all x1 -> x0, starting transfers between devices: 4.45 us -> none  [body_fused(): lax.all_to_all(mixed, ('row', 'col'), split_axis=0, concat_axis=0, tiled=...]
    pallas_call x1 -> x0, Pallas kernels: 2.78 us -> none  [body_fused(): pl.pallas_call(gate_kernel, out_shape=jax.ShapeDtypeStruct((rows, cols, w...]
    unnamed x2 -> x0, local copies, waits for them, and re-layouts: 0.8 us -> none
  transfers between devices with their start and end apart: 1 -> 0, of which waited for: 1 -> 0; matrix products, arithmetic and copies ran while one was open for 0% -> 0% of each run, Pallas kernels for 4% -> 0%
where the time goes in v17:
time: 65.4 us; the launch traced here: 64.4 us
  blocking collectives  51.4 us (79%)
  Pallas kernels  13 us (20%)
    all_to_all x1, blocking collectives, body_fused(): lax.all_to_all(edges, ('row', 'col'), split_axis=0, concat_axis=0, tiled=...  32.5 us
    all_to_all x1, blocking collectives, body_fused(): lax.all_to_all(mixed, ('row', 'col'), split_axis=0, concat_axis=0, tiled=...  18.9 us
    pallas_call x1, Pallas kernels, body_fused(): pl.pallas_call(transition_kernel, out_shape=jax.ShapeDtypeStruct((rows, c...  5.61 us
    pallas_call x1, Pallas kernels, body_fused(): pl.pallas_call(functools.partial(project_kernel, block=rows), out_shape=j...  4.72 us
    pallas_call x1, Pallas kernels, body_fused(): pl.pallas_call(functools.partial(mix_kernel, n_col=n_col, side_major=Fals...  2.65 us

profile of v17, /device:TPU:0, one launch (start us, length us, event | category | flops | bytes accessed | tf_op | source)
XLA Modules:
  0.0 64.4 jit_solution(12988602664753780352)
XLA Ops:
  0.0 4.7 %shard_map.100 = bf16[4096,128]{1,0:T(8,128)(2,1)} custom-call(s32[256]{0:T(256)} %mask_ref.1, bf16[32,64,128]{2,1,0:T(8,128)(2,1)} %pair_ref.3, bf16[128,128]{1,0:T(8,128)(2,1)} %wag_ref.1, bf16[128,128]{1,0:T(8,128)(2,1)} %wap_ref.1, bf16[128,128]{1,0:T(8,128)(2,1)} %wbg_ref.1, bf16[128,128]{1,0:T(8,128)(2,1)} %wbp_ref.1), custom_call_target="tpu_custom_call" | custom-call | tf_op jit(solution)/shard_map/pallas_call | solution.py:214
  4.7 32.5 %all_to_all.10.edges_ref = bf16[32,2,2,32,128]{4,3,2,1,0:T(8,128)(2,1)} all-to-all(bf16[32,2,2,32,128]{4,3,2,1,0:T(8,128)(2,1)} %bitcast.2), channel_id=1, replica_groups=mesh['row'=8,'col'=4] {'row','col'}, dimensions={0} | all-to-all | bytes 2097152 | tf_op jit(solution)/shard_map/all_to_all | solution.py:221
  37.2 2.7 %shard_map.101 = bf16[32,2,32,128]{3,2,1,0:T(8,128)(2,1)} custom-call(bf16[32,2,2,32,128]{4,3,2,1,0:T(8,128)(2,1)} %all_to_all.10.edges_ref), custom_call_target="tpu_custom_call" | custom-call | tf_op jit(solution)/shard_map/pallas_call | solution.py:222
  39.8 18.9 %all_to_all.11 = bf16[32,2,32,128]{3,2,1,0:T(8,128)(2,1)} all-to-all(bf16[32,2,32,128]{3,2,1,0:T(8,128)(2,1)} %shard_map.101), channel_id=1, replica_groups=mesh['row'=8,'col'=4] {'row','col'}, dimensions={0} | all-to-all | bytes 1048576 | tf_op jit(solution)/shard_map/all_to_all | solution.py:229
  58.8 5.6 %shard_map.102 = bf16[32,64,128]{2,1,0:T(8,128)(2,1)} custom-call(bf16[2048,128]{1,0:T(8,128)(2,1)} %bitcast.3, bf16[32,64,128]{2,1,0:T(8,128)(2,1)} %pair_ref.3, bf16[128,128]{1,0:T(8,128)(2,1)} %wg_ref.1, bf16[128,128]{1,0:T(8,128)(2,1)} %wo_ref.1, bf16[128,512]{1,0:T(8,128)(2,1)} %wu_ref.1, bf16[512,128]{1,0:T(8,128)(2,1)} %wd_ref.1), custom_call_target="tpu_custom_call" | custom-call | tf_op jit(solution)/shard_map/pallas_call | solution.py:231
